TPU v7x, 256 devices: a whole 4x4x8 slice. The times are simulated.
256 devices in a mesh: rows: 32 (over y, z), grp: 8 (over x, core).
Axes of the slice: x: 4, y: 4, z: 8, core: 2. Of those that a mesh axis runs over, the one named last changes fastest.
Arguments:
- item_table: bfloat16 [507904, 128], P(('rows', 'grp'))
- histories: int32 [16384, 64], P(('rows', 'grp')), may hold values from 0 to 507903, as said below
- counts: int32 [16384], P(('rows', 'grp')), may hold values from 32 to 64
Outputs:
- user_vectors: float32 [16384, 128], P(('rows', 'grp'))
- item_rhs: float32 [507904, 128], P(('rows', 'grp'))
Inputs may be any that keep to these rules, and one draw needn't show every extreme that they name: `histories`: entry j of user u is used only if j < counts[u]. The used entries of the users of one device name items of one owner (rows o * 1984 to (o + 1) * 1984 - 1) at most 32 times, and in every draw some owner is named exactly 32 times by the used entries of every device.
All inputs are finite; a program needn't handle non-finite values.
Results may differ from a plain program's by a relative error of at most 0.0064.
Values may be sent and summed in bfloat16 or wider, within the bound.
No kernel may reach another device: no remote copies, remote signals or barrier semaphores. Data moves between devices by JAX's collectives and lax.ppermute only.
A program may use at most 64 MiB of HBM per device.

v0:
```python
import jax
import jax.numpy as jnp
from jax import lax
from jax.sharding import PartitionSpec as P

ITERS = 3


unobserved_weight = 25.0
ridge = 0.1


def on_device(item_table, histories, counts):
    row_count = lax.axis_size("rows")
    group_count = lax.axis_size("grp")
    devices = row_count * group_count
    table_rows, embed_width = item_table.shape
    user_count, history_length = histories.shape
    lookups = user_count * history_length
    capacity = max(4, 2 * lookups // devices)
    slots_total = devices * capacity
    local_gram = lax.dot_general(
        item_table, item_table, (((0,), (0,)), ((), ())), preferred_element_type=jnp.float32
    )
    gramian = lax.psum(local_gram, ("rows", "grp"))
    positions = lax.broadcasted_iota(jnp.int32, (user_count, history_length), 1)
    live = positions < counts[:, None]
    weights = live.astype(jnp.float32)
    flat_ids = histories.reshape(-1)
    owners = flat_ids // table_rows
    local_rows = flat_ids - owners * table_rows
    owner_key = jnp.where(live.reshape(-1), owners, devices)
    ordering = jnp.argsort(owner_key, stable=True)
    sorted_key = owner_key[ordering]
    starts = jnp.searchsorted(sorted_key, jnp.arange(devices + 1, dtype=jnp.int32), side="left")
    ranks = jnp.arange(lookups, dtype=jnp.int32) - starts[sorted_key]
    sorted_slots = jnp.where(sorted_key < devices, sorted_key * capacity + ranks, slots_total)
    slot_index = jnp.zeros((lookups,), jnp.int32).at[ordering].set(sorted_slots)
    requests = (
        jnp.full((slots_total,), table_rows, jnp.int32).at[slot_index].set(local_rows, mode="drop")
    )
    requests = requests.reshape(row_count, group_count, capacity)
    incoming = lax.all_to_all(
        lax.all_to_all(requests, "grp", split_axis=1, concat_axis=1, tiled=True),
        "rows",
        split_axis=0,
        concat_axis=0,
        tiled=True,
    )
    answered = item_table[jnp.minimum(incoming, table_rows - 1)]
    replies = lax.all_to_all(
        lax.all_to_all(answered, "grp", split_axis=1, concat_axis=1, tiled=True),
        "rows",
        split_axis=0,
        concat_axis=0,
        tiled=True,
    )
    reply_rows = replies.reshape(slots_total, embed_width)
    fetched = reply_rows[jnp.minimum(slot_index, slots_total - 1)].reshape(
        user_count, history_length, embed_width
    )
    narrow_weights = weights.astype(jnp.bfloat16)
    target = jnp.einsum("ul,ulk->uk", narrow_weights, fetched, preferred_element_type=jnp.float32)
    unseen_scale = unobserved_weight / (table_rows * devices)
    solution = jnp.zeros_like(target)
    residual = target
    direction = target
    norm_now = jnp.sum(residual * residual, axis=1)
    for iteration in range(ITERS):
        narrow = direction.astype(jnp.bfloat16)
        scores = jnp.einsum("ulk,uk->ul", fetched, narrow, preferred_element_type=jnp.float32)
        scores = (scores * weights).astype(jnp.bfloat16)
        returned = jnp.einsum("ulk,ul->uk", fetched, scores, preferred_element_type=jnp.float32)
        curved = jnp.dot(direction, gramian, precision=lax.Precision.HIGHEST)
        applied = unseen_scale * curved + returned + ridge * direction
        step_size = norm_now / jnp.sum(direction * applied, axis=1)
        solution = solution + step_size[:, None] * direction
        residual = residual - step_size[:, None] * applied
        norm_next = jnp.sum(residual * residual, axis=1)
        direction = residual + (norm_next / norm_now)[:, None] * direction
        norm_now = norm_next
    repeated = jnp.repeat(solution, history_length, axis=0)
    partials = (
        jnp.zeros((slots_total, embed_width), jnp.float32).at[slot_index].set(repeated, mode="drop")
    )
    partials = partials.reshape(row_count, group_count, capacity, embed_width)
    arrived = lax.all_to_all(
        lax.all_to_all(partials, "grp", split_axis=1, concat_axis=1, tiled=True),
        "rows",
        split_axis=0,
        concat_axis=0,
        tiled=True,
    )
    item_rhs = (
        jnp.zeros((table_rows, embed_width), jnp.float32)
        .at[incoming.reshape(-1)]
        .add(arrived.reshape(-1, embed_width), mode="drop")
    )
    return (solution, item_rhs)


def solution(mesh):
    return jax.shard_map(
        on_device,
        mesh=mesh,
        in_specs=(P(("rows", "grp"), None), P(("rows", "grp"), None), P(("rows", "grp"))),
        out_specs=(P(("rows", "grp"), None), P(("rows", "grp"), None)),
        check_vma=False,
    )
```

profile of v0, /device:TPU:1, one launch (start us, length us, event | category | flops | bytes accessed | tf_op | source)
XLA Modules:
  0.0 698.0 jit_solution(2141229603027904647)
XLA Ops:
  7.2 0.9 reshape.99
  8.1 0.7 fusion.28
  8.8 0.1 lt.63
  8.9 5.8 sort.17
  14.7 23.0 %gather_fusion.1 = s32[4096]{0:T(1024)S(1)} fusion(s32[4096]{0:T(1024)S(1)} %get-tuple-element.108, s32[4096]{0:T(1024)S(1)} %get-tuple-element.109), kind=kCustom, calls=%fused_computation.1 | custom fusion | bytes 49152 | tf_op jit(solution)/shard_map/gather | solution.py:34
  37.8 30.3 %while.24 = (s32[]{:T(128)}, u32[257]{0:T(512)S(1)}, u32[257]{0:T(512)S(1)}, s32[4096]{0:T(1024)S(1)}, s32[]{:T(128)}, /*index=5*/s32[]{:T(128)}, s32[]{}) while((s32[]{:T(128)}, u32[257]{0:T(512)S(1)}, u32[257]{0:T(512)S(1)}, s32[4096]{0:T(1024)S(1)}, s32[]{:T(128)}, /*index=5*/s32[]{:T(128)}, s32[]{}) %tuple.47), condition=%wide.region_2.3_spmd.clone, body=%wide.region_1.2_spmd.clone.sunk | while | flops 5654 | bytes 21159 | solution.py:35
  37.8 2.2 gather_fusion
  40.1 2.2 gather_fusion
  42.5 2.2 gather_fusion
  44.8 2.2 gather_fusion
  47.1 2.2 gather_fusion
  49.4 2.2 gather_fusion
  51.8 2.2 gather_fusion
  54.1 2.2 gather_fusion
  56.4 2.2 gather_fusion
  58.7 2.2 gather_fusion
  61.1 2.2 gather_fusion
  63.4 2.2 gather_fusion
  65.7 2.2 gather_fusion
  68.1 25.9 %gather_fusion.2 = s32[4096]{0:T(1024)S(1)} fusion(s32[257]{0:T(512)S(1)} %convert_element_type.36, s32[4096]{0:T(1024)S(1)} %broadcast_clamp_fusion.1), kind=kCustom, calls=%fused_computation.2 | custom fusion | bytes 49152 | tf_op jit(solution)/shard_map/gather | solution.py:36
  94.0 15.5 %scatter_custom_fusion = s32[4096]{0:T(1024)S(1)} fusion(s32[4096]{0:T(1024)S(1)} %get-tuple-element.110, s32[4096]{0:T(1024)S(1)} %add_select_fusion.1, s32[]{:T(128)} %constant.59.clone.1), kind=kCustom, calls=%fused_computation.85 | custom fusion | bytes 16388 | tf_op jit(solution)/shard_map/scatter | solution.py:38
  109.5 15.5 %scatter_custom_fusion.1 = s32[8192]{0:T(1024)S(1)} fusion(s32[4096]{0:T(1024)S(1)} %get-tuple-element.106, s32[4096]{0:T(1024)S(1)} %get-tuple-element.107, s32[]{:T(128)} %constant.58.clone.1), kind=kCustom, calls=%fused_computation.79 | custom fusion | bytes 32772 | tf_op jit(solution)/shard_map/scatter | solution.py:40
  125.2 0.1 reshape.212
  125.3 10.3 %all_to_all.30 = s32[8,1,1024]{2,1,0:T(1,128)S(1)} all-to-all(s32[8,1,1024]{2,1,0:T(1,128)S(1)} %reshape.212), channel_id=1, replica_groups=mesh['rows'=32,'grp'=8] {'grp'}, dimensions={0} | all-to-all | bytes 65536 | tf_op jit(solution)/shard_map/all_to_all | solution.py:44
  135.7 0.5 broadcast.142
  136.2 0.7 reduce
  136.9 0.1 reshape.213
  137.1 0.1 reshape.214
  137.2 19.8 %all_to_all.31 = s32[32,1,256]{2,1,0:T(1,128)S(1)} all-to-all(s32[32,1,256]{2,1,0:T(1,128)S(1)} %reshape.214), channel_id=1, replica_groups=mesh['rows'=32,'grp'=8] {'rows'}, dimensions={0} | all-to-all | bytes 65536 | tf_op jit(solution)/shard_map/all_to_all | solution.py:43
  157.0 0.7 reduce.1
  157.9 24.0 %gather_fusion.3 = bf16[8192,128]{1,0:T(8,128)(2,1)S(1)} fusion(bf16[1984,128]{1,0:T(8,128)(2,1)S(1)} %copy-done, s32[8192]{0:T(1024)S(1)} %broadcast_clamp_fusion), kind=kCustom, calls=%fused_computation.3 | custom fusion | bytes 4227072 | tf_op jit(solution)/shard_map/gather | solution.py:50
  182.0 0.4 copy.16
  182.4 31.1 %all_to_all.32 = bf16[32,8,32,128]{3,2,0,1:T(8,128)(2,1)S(1)} all-to-all(bf16[32,8,32,128]{3,2,0,1:T(8,128)(2,1)S(1)} %copy.16), channel_id=1, replica_groups=mesh['rows'=32,'grp'=8] {'grp'}, dimensions={1} | all-to-all | bytes 4194304 | tf_op jit(solution)/shard_map/all_to_all | solution.py:52
  213.5 2.0 copy.17
  215.5 4.0 all-to-all-start.3
  219.5 0.2 all-reduce.2.cloned.1.call-start
  219.7 1.0 fusion.38
  220.7 47.8 %all-to-all-done.3 = bf16[32,8,32,128]{3,2,1,0:T(8,128)(2,1)S(1)} async-done(((bf16[32,8,32,128]{3,2,1,0:T(8,128)(2,1)}), bf16[32,8,32,128]{3,2,1,0:T(8,128)(2,1)S(1)}, u32[]{:S(2)}, u32[]{:S(2)}) %all-to-all-start.3) | async-done | bytes 2097184 | tf_op jit(solution)/shard_map/all_to_all | solution.py:51
  268.5 14.9 %gather_fusion.4 = bf16[4096,128]{1,0:T(8,128)(2,1)} fusion(bf16[8192,128]{1,0:T(8,128)(2,1)S(1)} %bitcast.60, s32[4096]{0:T(1024)S(1)} %get-tuple-element.105), kind=kCustom, calls=%fused_computation.4 | custom fusion | bytes 2113536 | tf_op jit(solution)/shard_map/gather | solution.py:59
  283.4 1.7 fusion.26
  285.1 1.9 fusion.24
  287.1 1.6 fusion.22
  288.7 180.9 %all-reduce.2.cloned.1.call-done = f32[128,128]{1,0:T(8,128)} async-done(((f32[128,128]{1,0:T(8,128)}), f32[128,128]{1,0:T(8,128)}) %all-reduce.2.cloned.1.call-update) | async-done | bytes 65552 | tf_op jit(solution)/shard_map/psum | solution.py:25
  469.6 1.2 multiply_reduce_fusion.3
  470.8 0.2 multiply_reduce_fusion.2
  471.0 0.1 convert_bitcast_fusion.1
  471.1 1.9 fusion.20
  473.1 0.4 fusion.18
  473.5 1.1 multiply_reduce_fusion.1
  474.6 0.2 multiply_reduce_fusion
  474.8 0.1 convert_bitcast_fusion
  474.9 0.6 fusion.16
  475.6 0.4 fusion.14
  476.0 0.3 fusion.11
  476.3 0.1 multiply_add_fusion
  476.5 0.1 broadcast_in_dim.68
  476.6 12.8 %scatter_custom_fusion.2 = f32[8192,128]{1,0:T(8,128)} fusion(s32[4096]{0:T(1024)S(1)} %get-tuple-element.106, f32[4096,128]{1,0:T(8,128)S(1)} %bitcast.63, f32[]{:T(128)} %constant.71.clone.1), kind=kCustom, calls=%fused_computation.15 | custom fusion | bytes 4194308 | tf_op jit(solution)/shard_map/scatter | solution.py:84
  489.4 2.8 copy.18
  492.2 52.7 %all_to_all.33 = f32[32,8,32,128]{3,2,0,1:T(8,128)S(1)} all-to-all(f32[32,8,32,128]{3,2,0,1:T(8,128)S(1)} %copy.18), channel_id=1, replica_groups=mesh['rows'=32,'grp'=8] {'grp'}, dimensions={1} | all-to-all | bytes 8388608 | tf_op jit(solution)/shard_map/all_to_all | solution.py:88
  544.8 2.6 copy.19
  547.5 5.9 all-to-all-start.5
  553.3 0.1 reshape.103
  553.5 92.4 %all-to-all-done.5 = f32[32,8,32,128]{3,2,1,0:T(8,128)} async-done(((f32[32,8,32,128]{3,2,1,0:T(8,128)}), f32[32,8,32,128]{3,2,1,0:T(8,128)}, u32[]{:S(2)}, u32[]{:S(2)}) %all-to-all-start.5) | async-done | bytes 4194336 | tf_op jit(solution)/shard_map/all_to_all | solution.py:87
  645.9 45.3 %scatter_custom_fusion.3 = f32[1984,128]{1,0:T(8,128)} fusion(s32[8192]{0:T(1024)S(1)} %bitcast.84, f32[8192,128]{1,0:T(8,128)} %bitcast.29, f32[]{:T(128)} %constant.71.clone.1), kind=kCustom, calls=%fused_computation.28 | custom fusion | flops 1048576 | bytes 1016320 | tf_op jit(solution)/shard_map/scatter-add | solution.py:97
  (103 shorter events, 1.4 us)
Async XLA Ops:
  7.2 150.8 %copy-start = (bf16[1984,128]{1,0:T(8,128)(2,1)S(1)}, bf16[1984,128]{1,0:T(8,128)(2,1)}, u32[]{:S(2)}) copy-start(bf16[1984,128]{1,0:T(8,128)(2,1)} %param.5) | copy-start | bytes 1523716
  215.5 53.1 %all-to-all-start.3 = ((bf16[32,8,32,128]{3,2,1,0:T(8,128)(2,1)}), bf16[32,8,32,128]{3,2,1,0:T(8,128)(2,1)S(1)}, u32[]{:S(2)}, u32[]{:S(2)}) async-start(bf16[32,8,32,128]{3,2,1,0:T(8,128)(2,1)} %copy.17), calls=%async_computation.3 | async-start | bytes 4194304 | tf_op jit(solution)/shard_map/all_to_all | solution.py:51
  219.5 250.1 %all-reduce.2.cloned.1.call-start = ((), (), s32[]{:S(2)}) async-start(), calls=%async_computation.6 | async-start | bytes 131072 | tf_op jit(solution)/shard_map/psum | solution.py:25
  268.5 18.5 %copy-start.4 = (s32[64]{0:T(128)S(1)}, s32[64]{0:T(128)}, u32[]{:S(2)}) copy-start(s32[64]{0:T(128)} %param.7) | copy-start | bytes 772
  283.4 189.6 %copy-start.1 = (bf16[4096,128]{1,0:T(8,128)(2,1)S(1)}, bf16[4096,128]{1,0:T(8,128)(2,1)}, u32[]{:S(2)}) copy-start(bf16[4096,128]{1,0:T(8,128)(2,1)} %gather_fusion.4) | copy-start | bytes 3145732
  469.6 6.4 copy-start.2
  476.4 15.7 %copy-start.3 = (f32[64,128]{1,0:T(8,128)}, f32[64,128]{1,0:T(8,128)S(1)}, u32[]{:S(2)}) copy-start(f32[64,128]{1,0:T(8,128)S(1)} %multiply_add_fusion) | copy-start | bytes 98308
  547.5 98.4 %all-to-all-start.5 = ((f32[32,8,32,128]{3,2,1,0:T(8,128)}), f32[32,8,32,128]{3,2,1,0:T(8,128)}, u32[]{:S(2)}, u32[]{:S(2)}) async-start(f32[32,8,32,128]{3,2,1,0:T(8,128)} %copy.19), calls=%async_computation.5 | async-start | bytes 8388608 | tf_op jit(solution)/shard_map/all_to_all | solution.py:87
Sparse Core Ops, SparseCore 0:
  226.4 243.1 all-reduce.1
where the time goes:
time: 702 us; the launch traced here: 698 us
  waiting for transfers between devices  321 us (46%)
  local copies, waits for them, and re-layouts  171 us (24%)
  blocking collectives  114 us (16%)
  other arithmetic  54.8 us (8%)
  between operations  14.4 us (2%)
  matrix products  12 us (2%)
  starting transfers between devices  10.1 us (1%)
    psum x1, waiting for transfers between devices, on_device(): gramian = lax.psum(local_gram, ('rows', 'grp'))  181 us
    all_to_all x1, waiting for transfers between devices, on_device(): lax.all_to_all(lax.all_to_all(partials, 'grp', split_axis=1, concat_axis=...  92.4 us
    all_to_all x1, blocking collectives, on_device(): lax.all_to_all(partials, 'grp', split_axis=1, concat_axis=1, tiled=True)  52.7 us
    all_to_all x1, waiting for transfers between devices, on_device(): lax.all_to_all(lax.all_to_all(answered, 'grp', split_axis=1, concat_axis=...  47.8 us
    scatter-add x1, other arithmetic, on_device(): item_rhs = jnp.zeros((table_rows, embed_width), jnp.float32).at[incoming....  45.3 us
    all_to_all x1, blocking collectives, on_device(): lax.all_to_all(answered, 'grp', split_axis=1, concat_axis=1, tiled=True)  31.1 us
    gather x13, local copies, waits for them, and re-layouts, on_device(): jnp.searchsorted(sorted_key, jnp.arange(devices + 1, dtype=jnp.int32), si...  29 us
    gather x1, local copies, waits for them, and re-layouts, on_device(): ranks = jnp.arange(lookups, dtype=jnp.int32) - starts[sorted_key]  25.9 us
  transfers between devices with their start and end apart: 3, of which 3 were waited for; matrix products, arithmetic and copies ran while one was open for 3% of the time, Pallas kernels for 0%

commit v1 on v0

v1 whole, which is shorter than its diff:
```python
import jax
import jax.numpy as jnp
from jax import lax
from jax.sharding import PartitionSpec as P

ITERS = 3


unobserved_weight = 25.0
ridge = 0.1


def exchange(values):
    return lax.all_to_all(values, ("rows", "grp"), 0, 0, tiled=True)


def sum_over_devices(value):
    for axis in ("grp", "rows"):
        size = lax.axis_size(axis)
        stride = 1
        while stride < size:
            partners = [(i, i ^ stride) for i in range(size)]
            value = value + lax.ppermute(value, axis, partners)
            stride *= 2
    return value


def on_device(item_table, histories, counts):
    row_count = lax.axis_size("rows")
    group_count = lax.axis_size("grp")
    devices = row_count * group_count
    table_rows, embed_width = item_table.shape
    user_count, history_length = histories.shape
    lookups = user_count * history_length
    capacity = max(4, 2 * lookups // devices)
    slots_total = devices * capacity
    bf16 = jnp.bfloat16
    f32 = jnp.float32

    local_gram = lax.dot_general(
        item_table, item_table, (((0,), (0,)), ((), ())), preferred_element_type=f32
    )
    gramian = sum_over_devices(local_gram)

    positions = lax.broadcasted_iota(jnp.int32, (user_count, history_length), 1)
    live = positions < counts[:, None]
    owners = histories // table_rows
    local_rows = histories - owners * table_rows
    owner_ids = lax.broadcasted_iota(jnp.int32, (user_count, history_length, devices), 2)
    by_owner = ((owners[:, :, None] == owner_ids) & live[:, :, None]).astype(bf16)
    slot_ids = lax.broadcasted_iota(jnp.int32, (history_length, history_length), 0)
    earlier = (lax.broadcasted_iota(jnp.int32, (history_length, history_length), 1) < slot_ids).astype(bf16)
    within_user = jnp.einsum("jk,uko->ujo", earlier, by_owner, preferred_element_type=f32)
    per_user = jnp.sum(by_owner.astype(f32), axis=1)
    user_ids = lax.broadcasted_iota(jnp.int32, (user_count, user_count), 0)
    earlier_users = (lax.broadcasted_iota(jnp.int32, (user_count, user_count), 1) < user_ids).astype(bf16)
    before_user = jnp.einsum("uv,vo->uo", earlier_users, per_user.astype(bf16), preferred_element_type=f32)
    ranks = jnp.sum(by_owner.astype(f32) * (within_user + before_user[:, None, :]), axis=2)
    rank_ids = lax.broadcasted_iota(jnp.int32, (user_count, history_length, capacity), 2)
    by_rank = ((ranks.astype(jnp.int32)[:, :, None] == rank_ids) & live[:, :, None]).astype(bf16)

    row_high = local_rows // 32
    row_low = local_rows - row_high * 32
    user_of = lax.broadcasted_iota(jnp.int32, (user_count, history_length), 0)
    payload = jnp.stack([row_high, row_low, user_of, jnp.ones_like(user_of)], axis=2).astype(bf16)
    spread = (payload[:, :, :, None] * by_rank[:, :, None, :]).reshape(lookups, 4 * capacity)
    slots = jnp.einsum(
        "io,ic->oc", by_owner.reshape(lookups, devices), spread, preferred_element_type=f32
    ).reshape(devices, 4, capacity)
    slots = slots.astype(jnp.int32)
    requests = slots[:, 0] * 32 + slots[:, 1]
    slot_user = slots[:, 2].reshape(slots_total)
    slot_used = slots[:, 3].reshape(slots_total)

    slot_index = (owners * capacity + ranks.astype(jnp.int32)).reshape(lookups)

    incoming = exchange(requests).reshape(slots_total)
    answered = jnp.take(item_table, incoming, axis=0, mode="clip")
    reply_rows = exchange(answered.reshape(devices, capacity, embed_width)).reshape(
        slots_total, embed_width
    )
    fetched = jnp.take(reply_rows, slot_index, axis=0, mode="clip").reshape(
        user_count, history_length, embed_width
    )
    weights = live.astype(f32)
    narrow_weights = weights.astype(bf16)
    target = jnp.einsum("ul,ulk->uk", narrow_weights, fetched, preferred_element_type=f32)
    unseen_scale = unobserved_weight / (table_rows * devices)
    solution = jnp.zeros_like(target)
    residual = target
    direction = target
    norm_now = jnp.sum(residual * residual, axis=1)
    for iteration in range(ITERS):
        narrow = direction.astype(bf16)
        scores = jnp.einsum("ulk,uk->ul", fetched, narrow, preferred_element_type=f32)
        scores = (scores * weights).astype(bf16)
        returned = jnp.einsum("ulk,ul->uk", fetched, scores, preferred_element_type=f32)
        curved = jnp.dot(direction, gramian, precision=lax.Precision.HIGHEST)
        applied = unseen_scale * curved + returned + ridge * direction
        step_size = norm_now / jnp.sum(direction * applied, axis=1)
        solution = solution + step_size[:, None] * direction
        residual = residual - step_size[:, None] * applied
        norm_next = jnp.sum(residual * residual, axis=1)
        direction = residual + (norm_next / norm_now)[:, None] * direction
        norm_now = norm_next

    member_ids = lax.broadcasted_iota(jnp.int32, (slots_total, user_count), 1)
    member = ((slot_user[:, None] == member_ids) & (slot_used[:, None] > 0)).astype(bf16)
    partials = jnp.einsum("su,uk->sk", member, solution.astype(bf16), preferred_element_type=f32)
    partials = partials.astype(bf16).reshape(devices, capacity, embed_width)
    arrived = exchange(partials).reshape(slots_total, embed_width)
    item_rhs = (
        jnp.zeros((table_rows, embed_width), f32)
        .at[incoming]
        .add(arrived.astype(f32), mode="drop")
    )
    return (solution, item_rhs)


def solution(mesh):
    return jax.shard_map(
        on_device,
        mesh=mesh,
        in_specs=(P(("rows", "grp"), None), P(("rows", "grp"), None), P(("rows", "grp"))),
        out_specs=(P(("rows", "grp"), None), P(("rows", "grp"), None)),
        check_vma=False,
    )
```

time: 702 us -> 297 us (0.42)
  waiting for transfers between devices: 321 us -> 107 us
  local copies, waits for them, and re-layouts: 171 us -> 48 us
  blocking collectives: 114 us -> 28.3 us
  starting transfers between devices: 10.1 us -> 36.8 us
  between operations: 14.4 us -> 0.96 us
    psum x1 -> x0, waiting for transfers between devices: 181 us -> none  [on_device(): gramian = lax.psum(local_gram, ('rows', 'grp'))]
    all_to_all x2, waiting for transfers between devices: 140 us -> 53.2 us  [exchange(): return lax.all_to_all(values, ('rows', 'grp'), 0, 0, tiled=True)]
    all_to_all x4 -> x1, blocking collectives: 114 us -> 28.3 us  [exchange(): return lax.all_to_all(values, ('rows', 'grp'), 0, 0, tiled=True)]
    gather x18 -> x2, local copies, waits for them, and re-layouts: 117 us -> 44.1 us  [the longest x1 29.2 us: on_device(): answered = jnp.take(item_table, incoming, axis=0, mode='clip')]
    ppermute x0 -> x8, waiting for transfers between devices: none -> 53.5 us  [sum_over_devices(): value = value + lax.ppermute(value, axis, partners)]
    scatter x3 -> x0, local copies, waits for them, and re-layouts: 43.8 us -> none  [the longest x1 15.5 us: on_device(): jnp.full((slots_total,), table_rows, jnp.int32).at[slot_index]]
    ppermute x0 -> x8, starting transfers between devices: none -> 14.8 us  [sum_over_devices(): value = value + lax.ppermute(value, axis, partners)]
    all_to_all x2, starting transfers between devices: 9.86 us -> 22 us  [exchange(): return lax.all_to_all(values, ('rows', 'grp'), 0, 0, tiled=True)]
  transfers between devices with their start and end apart: 3 -> 10, of which waited for: 3 -> 9; matrix products, arithmetic and copies ran while one was open for 3% -> 0% of each run, Pallas kernels for 0% -> 0%
where the time goes in v1:
time: 297 us; the launch traced here: 296 us
  waiting for transfers between devices  107 us (36%)
  other arithmetic  58.5 us (20%)
  local copies, waits for them, and re-layouts  48 us (16%)
  starting transfers between devices  36.8 us (12%)
  blocking collectives  28.3 us (10%)
  matrix products  16.6 us (6%)
    ppermute x8, waiting for transfers between devices, sum_over_devices(): value = value + lax.ppermute(value, axis, partners)  53.5 us
    all_to_all x2, waiting for transfers between devices, exchange(): return lax.all_to_all(values, ('rows', 'grp'), 0, 0, tiled=True)  53.2 us
    scatter-add x1, other arithmetic, on_device(): item_rhs = jnp.zeros((table_rows, embed_width), f32).at[incoming].add(arr...  50.5 us
    gather x1, local copies, waits for them, and re-layouts, on_device(): answered = jnp.take(item_table, incoming, axis=0, mode='clip')  29.2 us
    all_to_all x1, blocking collectives, exchange(): return lax.all_to_all(values, ('rows', 'grp'), 0, 0, tiled=True)  28.3 us
    all_to_all x2, starting transfers between devices, exchange(): return lax.all_to_all(values, ('rows', 'grp'), 0, 0, tiled=True)  22 us
    gather x1, local copies, waits for them, and re-layouts, on_device(): jnp.take(reply_rows, slot_index, axis=0, mode='clip')  14.9 us
    ppermute x8, starting transfers between devices, sum_over_devices(): value = value + lax.ppermute(value, axis, partners)  14.8 us
  transfers between devices with their start and end apart: 10, of which 9 were waited for; matrix products, arithmetic and copies ran while one was open for 0% of the time, Pallas kernels for 0%

profile of v1, /device:TPU:1, one launch (start us, length us, event | category | flops | bytes accessed | tf_op | source)
XLA Modules:
  0.0 295.9 jit_solution(3764134093623888858)
XLA Ops:
  0.7 0.8 fusion.40
  1.5 0.8 add_select_fusion.1
  2.2 1.4 convert_reduce_fusion
  3.7 0.1 fusion.34
  3.8 4.4 %fusion.2 = f32[64,64]{1,0:T(8,128)S(1)} fusion(f32[64,256]{1,0:T(8,128)S(1)} %fusion.34, pred[64,64]{1,0:T(8,128)(4,1)S(1)} %get-tuple-element.16, s32[64,64]{1,0:T(8,128)S(1)} %add_select_fusion.1), kind=kOutput, calls=%fused_computation.7 | convolution fusion | flops 143654912 | bytes 102400 | tf_op jit(solution)/shard_map/jk,uko->ujo/dot_general | solution.py:53
  8.3 2.5 fusion.3
  10.8 0.2 fusion.16
  11.0 0.1 pad.3.clone
  11.0 0.1 maximum_maximum_fusion
  11.1 0.2 broadcast_multiply_fusion
  11.3 2.5 mul.140
  13.8 2.2 convolution_convert_fusion.1
  16.0 0.1 copy.12
  16.1 28.3 %all_to_all.16 = s32[256,1,32]{2,1,0:T(1,128)S(1)} all-to-all(s32[256,1,32]{2,1,0:T(1,128)S(1)} %copy.12), channel_id=1, replica_groups=mesh['rows'=32,'grp'=8] {'rows','grp'}, dimensions={0} | all-to-all | bytes 65536 | tf_op jit(solution)/shard_map/all_to_all | solution.py:14
  44.4 0.5 broadcast.146
  44.9 1.0 reduce.6
  45.9 0.1 reshape.218
  46.0 29.2 %gather_fusion = bf16[8192,128]{1,0:T(8,128)(2,1)} fusion(bf16[1984,128]{1,0:T(8,128)(2,1)S(1)} %copy-done, s32[8192]{0:T(1024)S(1)} %broadcast_clamp_fusion), kind=kCustom, calls=%fused_computation | custom fusion | bytes 4227072 | tf_op jit(solution)/shard_map/jit(_take)/gather | solution.py:78
  75.2 5.5 %all-to-all-start.1 = ((bf16[256,32,128]{2,1,0:T(8,128)(2,1)}), bf16[256,32,128]{2,1,0:T(8,128)(2,1)S(1)}, u32[]{:S(2)}, u32[]{:S(2)}) async-start(bf16[256,32,128]{2,1,0:T(8,128)(2,1)} %bitcast.81), calls=%async_computation.1 | async-start | bytes 4194304 | tf_op jit(solution)/shard_map/all_to_all | solution.py:14
  80.8 0.3 fusion.49
  81.1 2.4 collective-permute-start
  83.5 0.9 collective-permute-done
  84.4 0.1 collective-permute-start.1
  84.5 4.6 %collective-permute-done.1 = f32[128,128]{1,0:T(8,128)S(1)} collective-permute-done((f32[128,128]{1,0:T(8,128)S(1)}, f32[128,128]{1,0:T(8,128)S(1)}, u32[]{:S(2)}, u32[]{:S(2)}) %collective-permute-start.1) | collective-permute-done | bytes 65568 | tf_op jit(solution)/shard_map/ppermute | solution.py:23
  89.1 1.3 collective-permute-start.2
  90.4 4.7 %collective-permute-done.2 = f32[128,128]{1,0:T(8,128)S(1)} collective-permute-done((f32[128,128]{1,0:T(8,128)S(1)}, f32[128,128]{1,0:T(8,128)S(1)}, u32[]{:S(2)}, u32[]{:S(2)}) %collective-permute-start.2) | collective-permute-done | bytes 65568 | tf_op jit(solution)/shard_map/ppermute | solution.py:23
  95.1 0.1 collective-permute-start.3
  95.2 32.7 %collective-permute-done.3 = f32[128,128]{1,0:T(8,128)S(1)} collective-permute-done((f32[128,128]{1,0:T(8,128)S(1)}, f32[128,128]{1,0:T(8,128)S(1)}, u32[]{:S(2)}, u32[]{:S(2)}) %collective-permute-start.3) | collective-permute-done | bytes 65568 | tf_op jit(solution)/shard_map/ppermute | solution.py:23
  127.9 1.4 collective-permute-start.4
  129.3 4.8 %collective-permute-done.4 = f32[128,128]{1,0:T(8,128)S(1)} collective-permute-done((f32[128,128]{1,0:T(8,128)S(1)}, f32[128,128]{1,0:T(8,128)S(1)}, u32[]{:S(2)}, u32[]{:S(2)}) %collective-permute-start.4) | collective-permute-done | bytes 65568 | tf_op jit(solution)/shard_map/ppermute | solution.py:23
  134.1 4.7 %collective-permute-start.5 = (f32[128,128]{1,0:T(8,128)S(1)}, f32[128,128]{1,0:T(8,128)S(1)}, u32[]{:S(2)}, u32[]{:S(2)}) collective-permute-start(f32[128,128]{1,0:T(8,128)S(1)} %add.98), channel_id=1, source_target_pairs={{0,32},{8,40},{16,48},{24,56},{32,0},{40,8},{48,16},{56,24},{64,96... | collective-permute-start | bytes 196616 | tf_op jit(solution)/shard_map/ppermute | solution.py:23
  138.8 2.5 collective-permute-done.5
  141.3 1.6 collective-permute-start.6
  142.9 1.6 collective-permute-done.6
  144.5 3.3 %collective-permute-start.7 = (f32[128,128]{1,0:T(8,128)S(1)}, f32[128,128]{1,0:T(8,128)S(1)}, u32[]{:S(2)}, u32[]{:S(2)}) collective-permute-start(f32[128,128]{1,0:T(8,128)S(1)} %add.100), channel_id=1, source_target_pairs={{0,128},{8,136},{16,144},{24,152},{32,160},{40,168},{48,176},{56,1... | collective-permute-start | bytes 196616 | tf_op jit(solution)/shard_map/ppermute | solution.py:23
  147.8 0.1 copy.14
  148.0 0.1 gt.13
  148.1 0.1 copy.13
  148.2 0.1 eq.42
  148.3 1.8 collective-permute-done.7
  150.1 14.9 %gather_fusion.1 = bf16[4096,128]{1,0:T(8,128)(2,1)} fusion(bf16[8192,128]{1,0:T(8,128)(2,1)S(1)} %bitcast.80, s32[4096]{0:T(1024)S(1)} %broadcast_clamp_fusion.1), kind=kCustom, calls=%fused_computation.1 | custom fusion | bytes 2113536 | tf_op jit(solution)/shard_map/jit(_take)/gather | solution.py:82
  165.0 1.7 fusion.32
  166.7 1.9 fusion.30
  168.5 0.1 fusion.41
  168.6 0.4 fusion.28
  169.0 0.3 multiply_reduce_fusion.3
  169.3 0.2 multiply_reduce_fusion.2
  169.5 0.1 convert_bitcast_fusion.1
  169.6 0.6 fusion.26
  170.3 0.1 fusion.42
  170.3 0.4 fusion.24
  170.7 0.3 multiply_reduce_fusion.1
  171.1 0.2 multiply_reduce_fusion
  171.3 0.1 convert_bitcast_fusion
  171.4 0.6 fusion.22
  172.0 0.1 fusion.43
  172.1 0.4 fusion.20
  172.5 0.3 fusion.13
  172.8 0.1 multiply_add_fusion
  172.9 2.6 convolution_convert_fusion
  175.5 16.5 %all-to-all-start.2 = ((bf16[256,32,128]{2,1,0:T(8,128)(2,1)}), bf16[256,32,128]{2,1,0:T(8,128)(2,1)S(1)}, u32[]{:S(2)}, u32[]{:S(2)}) async-start(bf16[256,32,128]{2,1,0:T(8,128)(2,1)} %bitcast.83), calls=%async_computation.2 | async-start | bytes 4194304 | tf_op jit(solution)/shard_map/all_to_all | solution.py:14
  192.0 0.1 broadcast_in_dim.8
  192.2 53.2 %all-to-all-done.2 = bf16[256,32,128]{2,1,0:T(8,128)(2,1)S(1)} async-done(((bf16[256,32,128]{2,1,0:T(8,128)(2,1)}), bf16[256,32,128]{2,1,0:T(8,128)(2,1)S(1)}, u32[]{:S(2)}, u32[]{:S(2)}) %all-to-all-start.2) | async-done | bytes 2097184 | tf_op jit(solution)/shard_map/all_to_all | solution.py:14
  245.4 50.5 %scatter_custom_fusion = f32[1984,128]{1,0:T(8,128)} fusion(s32[8192]{0:T(1024)S(1)} %bitcast.104, bf16[8192,128]{1,0:T(8,128)(2,1)S(1)} %bitcast.82, f32[]{:T(128)} %constant.41.clone.1), kind=kCustom, calls=%fused_computation.4 | custom fusion | flops 2097152 | bytes 3112964 | tf_op jit(solution)/shard_map/scatter-add | solution.py:115
  (34 shorter events, 0.4 us)
Async XLA Ops:
  0.6 45.4 %copy-start = (bf16[1984,128]{1,0:T(8,128)(2,1)S(1)}, bf16[1984,128]{1,0:T(8,128)(2,1)}, u32[]{:S(2)}) copy-start(bf16[1984,128]{1,0:T(8,128)(2,1)} %param.3) | copy-start | bytes 1523716
  3.8 4.4 %copy-start.3 = (s32[64,64]{1,0:T(8,128)S(1)}, s32[64,64]{1,0:T(8,128)}, u32[]{:S(2)}) copy-start(s32[64,64]{1,0:T(8,128)} %param.4) | copy-start | bytes 49156
  75.2 74.8 %all-to-all-start.1 = ((bf16[256,32,128]{2,1,0:T(8,128)(2,1)}), bf16[256,32,128]{2,1,0:T(8,128)(2,1)S(1)}, u32[]{:S(2)}, u32[]{:S(2)}) async-start(bf16[256,32,128]{2,1,0:T(8,128)(2,1)} %bitcast.81), calls=%async_computation.1 | async-start | bytes 4194304 | tf_op jit(solution)/shard_map/all_to_all | solution.py:14
  81.1 3.3 %collective-permute-start = (f32[128,128]{1,0:T(8,128)S(1)}, f32[128,128]{1,0:T(8,128)S(1)}, u32[]{:S(2)}, u32[]{:S(2)}) collective-permute-start(f32[128,128]{1,0:T(8,128)S(1)} %fusion.49), channel_id=1, source_target_pairs={{0,1},{1,0},{2,3},{3,2},{4,5},{5,4},{6,7},{7,6},{8,9},{9,8},{10,11... | collective-permute-start | bytes 196616 | tf_op jit(solution)/shard_map/ppermute | solution.py:23
  84.4 4.7 %collective-permute-start.1 = (f32[128,128]{1,0:T(8,128)S(1)}, f32[128,128]{1,0:T(8,128)S(1)}, u32[]{:S(2)}, u32[]{:S(2)}) collective-permute-start(f32[128,128]{1,0:T(8,128)S(1)} %add.94), channel_id=1, source_target_pairs={{0,2},{1,3},{2,0},{3,1},{4,6},{5,7},{6,4},{7,5},{8,10},{9,11},{10,... | collective-permute-start | bytes 196616 | tf_op jit(solution)/shard_map/ppermute | solution.py:23
  89.1 6.0 %collective-permute-start.2 = (f32[128,128]{1,0:T(8,128)S(1)}, f32[128,128]{1,0:T(8,128)S(1)}, u32[]{:S(2)}, u32[]{:S(2)}) collective-permute-start(f32[128,128]{1,0:T(8,128)S(1)} %add.95), channel_id=1, source_target_pairs={{0,4},{1,5},{2,6},{3,7},{4,0},{5,1},{6,2},{7,3},{8,12},{9,13},{10,... | collective-permute-start | bytes 196616 | tf_op jit(solution)/shard_map/ppermute | solution.py:23
  95.1 32.8 %collective-permute-start.3 = (f32[128,128]{1,0:T(8,128)S(1)}, f32[128,128]{1,0:T(8,128)S(1)}, u32[]{:S(2)}, u32[]{:S(2)}) collective-permute-start(f32[128,128]{1,0:T(8,128)S(1)} %add.96), channel_id=1, source_target_pairs={{0,8},{8,0},{16,24},{24,16},{32,40},{40,32},{48,56},{56,48},{64,72... | collective-permute-start | bytes 196616 | tf_op jit(solution)/shard_map/ppermute | solution.py:23
  127.9 6.2 %collective-permute-start.4 = (f32[128,128]{1,0:T(8,128)S(1)}, f32[128,128]{1,0:T(8,128)S(1)}, u32[]{:S(2)}, u32[]{:S(2)}) collective-permute-start(f32[128,128]{1,0:T(8,128)S(1)} %add.97), channel_id=1, source_target_pairs={{0,16},{8,24},{16,0},{24,8},{32,48},{40,56},{48,32},{56,40},{64,80... | collective-permute-start | bytes 196616 | tf_op jit(solution)/shard_map/ppermute | solution.py:23
  134.1 7.2 %collective-permute-start.5 = (f32[128,128]{1,0:T(8,128)S(1)}, f32[128,128]{1,0:T(8,128)S(1)}, u32[]{:S(2)}, u32[]{:S(2)}) collective-permute-start(f32[128,128]{1,0:T(8,128)S(1)} %add.98), channel_id=1, source_target_pairs={{0,32},{8,40},{16,48},{24,56},{32,0},{40,8},{48,16},{56,24},{64,96... | collective-permute-start | bytes 196616 | tf_op jit(solution)/shard_map/ppermute | solution.py:23
  141.3 3.2 %collective-permute-start.6 = (f32[128,128]{1,0:T(8,128)S(1)}, f32[128,128]{1,0:T(8,128)S(1)}, u32[]{:S(2)}, u32[]{:S(2)}) collective-permute-start(f32[128,128]{1,0:T(8,128)S(1)} %add.99), channel_id=1, source_target_pairs={{0,64},{8,72},{16,80},{24,88},{32,96},{40,104},{48,112},{56,120},{... | collective-permute-start | bytes 196616 | tf_op jit(solution)/shard_map/ppermute | solution.py:23
  144.5 5.5 %collective-permute-start.7 = (f32[128,128]{1,0:T(8,128)S(1)}, f32[128,128]{1,0:T(8,128)S(1)}, u32[]{:S(2)}, u32[]{:S(2)}) collective-permute-start(f32[128,128]{1,0:T(8,128)S(1)} %add.100), channel_id=1, source_target_pairs={{0,128},{8,136},{16,144},{24,152},{32,160},{40,168},{48,176},{56,1... | collective-permute-start | bytes 196616 | tf_op jit(solution)/shard_map/ppermute | solution.py:23
  165.0 3.6 %copy-start.4 = (s32[64]{0:T(128)S(1)}, s32[64]{0:T(128)}, u32[]{:S(2)}) copy-start(s32[64]{0:T(128)} %param.5) | copy-start | bytes 772
  165.0 3.7 %copy-start.1 = (bf16[4096,128]{1,0:T(8,128)(2,1)S(1)}, bf16[4096,128]{1,0:T(8,128)(2,1)}, u32[]{:S(2)}) copy-start(bf16[4096,128]{1,0:T(8,128)(2,1)} %gather_fusion.1) | copy-start | bytes 3145732
  172.9 2.6 copy-start.2
  175.5 69.9 %all-to-all-start.2 = ((bf16[256,32,128]{2,1,0:T(8,128)(2,1)}), bf16[256,32,128]{2,1,0:T(8,128)(2,1)S(1)}, u32[]{:S(2)}, u32[]{:S(2)}) async-start(bf16[256,32,128]{2,1,0:T(8,128)(2,1)} %bitcast.83), calls=%async_computation.2 | async-start | bytes 4194304 | tf_op jit(solution)/shard_map/all_to_all | solution.py:14

commit v2 on v1

--- a/solution.py
+++ b/solution.py
@@ -75,7 +75,9 @@
     slot_index = (owners * capacity + ranks.astype(jnp.int32)).reshape(lookups)
 
     incoming = exchange(requests).reshape(slots_total)
-    answered = jnp.take(item_table, incoming, axis=0, mode="clip")
+    table_ids = lax.broadcasted_iota(jnp.int32, (slots_total, table_rows), 1)
+    picks = (incoming[:, None] == table_ids).astype(bf16)
+    answered = jnp.dot(picks, item_table, preferred_element_type=f32).astype(bf16)
     reply_rows = exchange(answered.reshape(devices, capacity, embed_width)).reshape(
         slots_total, embed_width
     )
@@ -109,11 +111,7 @@
     partials = jnp.einsum("su,uk->sk", member, solution.astype(bf16), preferred_element_type=f32)
     partials = partials.astype(bf16).reshape(devices, capacity, embed_width)
     arrived = exchange(partials).reshape(slots_total, embed_width)
-    item_rhs = (
-        jnp.zeros((table_rows, embed_width), f32)
-        .at[incoming]
-        .add(arrived.astype(f32), mode="drop")
-    )
+    item_rhs = jnp.einsum("st,sk->tk", picks, arrived, preferred_element_type=f32)
     return (solution, item_rhs)
 
 

time: 297 us -> 246 us (0.83)
  blocking collectives: 28.3 us -> 98.2 us
  waiting for transfers between devices: 107 us -> 53.3 us
  other arithmetic: 58.5 us -> 7.94 us
  local copies, waits for them, and re-layouts: 48 us -> 18.7 us
  matrix products: 16.6 us -> 45.7 us
  starting transfers between devices: 36.8 us -> 20.3 us
    all_to_all x1 -> x2, blocking collectives: 28.3 us -> 98.2 us  [exchange(): return lax.all_to_all(values, ('rows', 'grp'), 0, 0, tiled=True)]
    all_to_all x2 -> x1, waiting for transfers between devices: 53.2 us -> 0.01 us  [exchange(): return lax.all_to_all(values, ('rows', 'grp'), 0, 0, tiled=True)]
    scatter-add x1 -> x0, other arithmetic: 50.5 us -> none  [on_device(): item_rhs = jnp.zeros((table_rows, embed_width), f32).at[incoming].add(arr...]
    dot_general x0 -> x2, matrix products: none -> 30.5 us  [the longest x1 19.4 us: on_device(): jnp.dot(picks, item_table, preferred_element_type=f32).astype(bf16)]
    gather x1 -> x0, local copies, waits for them, and re-layouts: 29.2 us -> none  [on_device(): answered = jnp.take(item_table, incoming, axis=0, mode='clip')]
    all_to_all x2 -> x1, starting transfers between devices: 22 us -> 5.72 us  [exchange(): return lax.all_to_all(values, ('rows', 'grp'), 0, 0, tiled=True)]
  transfers between devices with their start and end apart: 10 -> 9, of which waited for: 9 -> 8; matrix products, arithmetic and copies ran while one was open for 0% -> 0% of each run, Pallas kernels for 0% -> 0%
where the time goes in v2:
time: 246 us; the launch traced here: 245 us
  blocking collectives  98.2 us (40%)
  waiting for transfers between devices  53.3 us (22%)
  matrix products  45.7 us (19%)
  starting transfers between devices  20.3 us (8%)
  local copies, waits for them, and re-layouts  18.7 us (8%)
  other arithmetic  7.94 us (3%)
    all_to_all x2, blocking collectives, exchange(): return lax.all_to_all(values, ('rows', 'grp'), 0, 0, tiled=True)  98.2 us
    ppermute x8, waiting for transfers between devices, sum_over_devices(): value = value + lax.ppermute(value, axis, partners)  53.3 us
    dot_general x1, matrix products, on_device(): jnp.dot(picks, item_table, preferred_element_type=f32).astype(bf16)  19.4 us
    gather x1, local copies, waits for them, and re-layouts, on_device(): jnp.take(reply_rows, slot_index, axis=0, mode='clip')  14.9 us
    ppermute x8, starting transfers between devices, sum_over_devices(): value = value + lax.ppermute(value, axis, partners)  14.6 us
    dot_general x1, matrix products, on_device(): jnp.einsum('st,sk->tk', picks, arrived, preferred_element_type=f32)  11 us
    all_to_all x1, starting transfers between devices, exchange(): return lax.all_to_all(values, ('rows', 'grp'), 0, 0, tiled=True)  5.72 us
  transfers between devices with their start and end apart: 9, of which 8 were waited for; matrix products, arithmetic and copies ran while one was open for 0% of the time, Pallas kernels for 0%

profile of v2, /device:TPU:1, one launch (start us, length us, event | category | flops | bytes accessed | tf_op | source)
XLA Modules:
  0.0 245.2 jit_solution(17884865894300515012)
XLA Ops:
  0.7 0.8 fusion.42
  1.5 0.8 add_select_fusion.1
  2.2 1.4 convert_reduce_fusion
  3.7 0.1 fusion.36
  3.8 4.4 %fusion.5 = f32[64,64]{1,0:T(8,128)S(1)} fusion(f32[64,256]{1,0:T(8,128)S(1)} %fusion.36, pred[64,64]{1,0:T(8,128)(4,1)S(1)} %get-tuple-element.16, s32[64,64]{1,0:T(8,128)S(1)} %add_select_fusion.1), kind=kOutput, calls=%fused_computation.9 | convolution fusion | flops 143654912 | bytes 102400 | tf_op jit(solution)/shard_map/jk,uko->ujo/dot_general | solution.py:53
  8.2 0.1 multiply_add_fusion.3
  8.3 2.5 %fusion.6 = pred[64,64,256]{2,1,0:T(32,128)(4,1)} fusion(s32[64,64]{1,0:T(8,128)S(1)} %add_select_fusion.1, pred[64,64]{1,0:T(8,128)(4,1)S(1)} %get-tuple-element.16), kind=kLoop, calls=%fused_computation.11 | loop fusion | flops 2097152 | bytes 1069056 | tf_op jit(solution)/shard_map/and | solution.py:50
  10.8 0.2 fusion.19
  11.0 0.1 pad.3.clone
  11.0 0.1 maximum_maximum_fusion
  11.1 0.2 broadcast_multiply_fusion
  11.3 2.5 %mul.140 = bf16[4096,128]{0,1:T(8,128)(2,1)} reshape(bf16[64,64,4,32]{1,0,3,2:T(8,128)(2,1)S(1)} %broadcast_multiply_fusion) | data formatting | bytes 2097152 | tf_op jit(solution)/shard_map/mul | solution.py:66
  13.8 2.2 convolution_convert_fusion.1
  16.0 0.1 copy.14
  16.1 28.3 %all_to_all.16 = s32[256,1,32]{2,1,0:T(1,128)S(1)} all-to-all(s32[256,1,32]{2,1,0:T(1,128)S(1)} %copy.14), channel_id=1, replica_groups=mesh['rows'=32,'grp'=8] {'rows','grp'}, dimensions={0} | all-to-all | bytes 65536 | tf_op jit(solution)/shard_map/all_to_all | solution.py:14
  44.4 0.5 broadcast.126
  44.9 1.0 reduce.4
  45.9 0.1 eq.52
  46.0 19.4 %fusion.4 = bf16[8192,128]{1,0:T(8,128)(2,1)} fusion(bf16[1984,128]{1,0:T(8,128)(2,1)S(1)} %copy-done, s32[8192]{0:T(1024)S(1)} %eq.52), kind=kOutput, calls=%fused_computation.6 | convolution fusion | flops 4178051072 | bytes 2637824 | tf_op jit(solution)/shard_map/dot_general | solution.py:80
  65.4 5.7 %all-to-all-start.1 = ((bf16[256,32,128]{2,1,0:T(8,128)(2,1)}), bf16[256,32,128]{2,1,0:T(8,128)(2,1)S(1)}, u32[]{:S(2)}, u32[]{:S(2)}) async-start(bf16[256,32,128]{2,1,0:T(8,128)(2,1)} %bitcast.81), calls=%async_computation.1 | async-start | bytes 4194304 | tf_op jit(solution)/shard_map/all_to_all | solution.py:14
  71.2 0.3 fusion.51
  71.5 2.4 collective-permute-start
  73.9 0.9 collective-permute-done
  74.8 0.1 collective-permute-start.1
  74.9 4.6 %collective-permute-done.1 = f32[128,128]{1,0:T(8,128)S(1)} collective-permute-done((f32[128,128]{1,0:T(8,128)S(1)}, f32[128,128]{1,0:T(8,128)S(1)}, u32[]{:S(2)}, u32[]{:S(2)}) %collective-permute-start.1) | collective-permute-done | bytes 65568 | tf_op jit(solution)/shard_map/ppermute | solution.py:23
  79.5 1.3 collective-permute-start.2
  80.7 4.7 %collective-permute-done.2 = f32[128,128]{1,0:T(8,128)S(1)} collective-permute-done((f32[128,128]{1,0:T(8,128)S(1)}, f32[128,128]{1,0:T(8,128)S(1)}, u32[]{:S(2)}, u32[]{:S(2)}) %collective-permute-start.2) | collective-permute-done | bytes 65568 | tf_op jit(solution)/shard_map/ppermute | solution.py:23
  85.5 0.1 collective-permute-start.3
  85.6 32.7 %collective-permute-done.3 = f32[128,128]{1,0:T(8,128)S(1)} collective-permute-done((f32[128,128]{1,0:T(8,128)S(1)}, f32[128,128]{1,0:T(8,128)S(1)}, u32[]{:S(2)}, u32[]{:S(2)}) %collective-permute-start.3) | collective-permute-done | bytes 65568 | tf_op jit(solution)/shard_map/ppermute | solution.py:23
  118.3 1.4 collective-permute-start.4
  119.7 4.8 %collective-permute-done.4 = f32[128,128]{1,0:T(8,128)S(1)} collective-permute-done((f32[128,128]{1,0:T(8,128)S(1)}, f32[128,128]{1,0:T(8,128)S(1)}, u32[]{:S(2)}, u32[]{:S(2)}) %collective-permute-start.4) | collective-permute-done | bytes 65568 | tf_op jit(solution)/shard_map/ppermute | solution.py:23
  124.4 4.7 %collective-permute-start.5 = (f32[128,128]{1,0:T(8,128)S(1)}, f32[128,128]{1,0:T(8,128)S(1)}, u32[]{:S(2)}, u32[]{:S(2)}) collective-permute-start(f32[128,128]{1,0:T(8,128)S(1)} %add.83), channel_id=1, source_target_pairs={{0,32},{8,40},{16,48},{24,56},{32,0},{40,8},{48,16},{56,24},{64,96... | collective-permute-start | bytes 196616 | tf_op jit(solution)/shard_map/ppermute | solution.py:23
  129.1 2.5 %collective-permute-done.5 = f32[128,128]{1,0:T(8,128)S(1)} collective-permute-done((f32[128,128]{1,0:T(8,128)S(1)}, f32[128,128]{1,0:T(8,128)S(1)}, u32[]{:S(2)}, u32[]{:S(2)}) %collective-permute-start.5) | collective-permute-done | bytes 65568 | tf_op jit(solution)/shard_map/ppermute | solution.py:23
  131.6 1.6 collective-permute-start.6
  133.2 0.1 reshape.188
  133.3 1.6 collective-permute-done.6
  134.9 3.1 %collective-permute-start.7 = (f32[128,128]{1,0:T(8,128)S(1)}, f32[128,128]{1,0:T(8,128)S(1)}, u32[]{:S(2)}, u32[]{:S(2)}) collective-permute-start(f32[128,128]{1,0:T(8,128)S(1)} %add.85), channel_id=1, source_target_pairs={{0,128},{8,136},{16,144},{24,152},{32,160},{40,168},{48,176},{56,1... | collective-permute-start | bytes 196616 | tf_op jit(solution)/shard_map/ppermute | solution.py:23
  138.0 0.1 copy.16
  138.1 0.1 gt.16
  138.3 0.1 copy.15
  138.4 0.1 eq.55
  138.5 1.6 collective-permute-done.7
  140.1 14.9 %gather_fusion = bf16[4096,128]{1,0:T(8,128)(2,1)} fusion(bf16[8192,128]{1,0:T(8,128)(2,1)S(1)} %bitcast.79, s32[4096]{0:T(1024)S(1)} %broadcast_clamp_fusion), kind=kCustom, calls=%fused_computation | custom fusion | bytes 2113536 | tf_op jit(solution)/shard_map/jit(_take)/gather | solution.py:84
  155.0 1.7 fusion.34
  156.7 1.9 fusion.32
  158.6 0.1 fusion.43
  158.7 0.4 fusion.30
  159.0 0.3 multiply_reduce_fusion.3
  159.3 0.2 multiply_reduce_fusion.2
  159.6 0.1 convert_bitcast_fusion.1
  159.6 0.6 fusion.28
  160.3 0.1 fusion.44
  160.4 0.4 fusion.26
  160.8 0.3 multiply_reduce_fusion.1
  161.1 0.2 multiply_reduce_fusion
  161.3 0.1 convert_bitcast_fusion
  161.4 0.6 fusion.24
  162.0 0.1 fusion.45
  162.1 0.4 fusion.22
  162.5 0.3 fusion.16
  162.8 0.1 multiply_add_fusion
  162.9 1.3 convolution_convert_fusion
  164.2 69.9 %all_to_all.17 = bf16[256,32,128]{2,1,0:T(8,128)(2,1)S(1)} all-to-all(bf16[256,32,128]{2,1,0:T(8,128)(2,1)S(1)} %bitcast.80), channel_id=1, replica_groups=mesh['rows'=32,'grp'=8] {'rows','grp'}, dimensions={0} | all-to-all | bytes 4194304 | tf_op jit(solution)/shard_map/all_to_all | solution.py:14
  234.1 11.0 %fusion = f32[1984,128]{1,0:T(8,128)} fusion(bf16[8192,128]{1,0:T(8,128)(2,1)S(1)} %bitcast.82, s32[8192]{0:T(1024)S(1)} %eq.52), kind=kOutput, calls=%fused_computation.2 | convolution fusion | flops 4177002496 | bytes 3145728 | tf_op jit(solution)/shard_map/st,sk->tk/dot_general | solution.py:114
  (30 shorter events, 0.2 us)
Async XLA Ops:
  0.6 45.4 %copy-start = (bf16[1984,128]{1,0:T(8,128)(2,1)S(1)}, bf16[1984,128]{1,0:T(8,128)(2,1)}, u32[]{:S(2)}) copy-start(bf16[1984,128]{1,0:T(8,128)(2,1)} %param.3) | copy-start | bytes 1523716
  3.8 4.4 %copy-start.3 = (s32[64,64]{1,0:T(8,128)S(1)}, s32[64,64]{1,0:T(8,128)}, u32[]{:S(2)}) copy-start(s32[64,64]{1,0:T(8,128)} %param.4) | copy-start | bytes 49156
  65.4 74.7 %all-to-all-start.1 = ((bf16[256,32,128]{2,1,0:T(8,128)(2,1)}), bf16[256,32,128]{2,1,0:T(8,128)(2,1)S(1)}, u32[]{:S(2)}, u32[]{:S(2)}) async-start(bf16[256,32,128]{2,1,0:T(8,128)(2,1)} %bitcast.81), calls=%async_computation.1 | async-start | bytes 4194304 | tf_op jit(solution)/shard_map/all_to_all | solution.py:14
  71.5 3.3 %collective-permute-start = (f32[128,128]{1,0:T(8,128)S(1)}, f32[128,128]{1,0:T(8,128)S(1)}, u32[]{:S(2)}, u32[]{:S(2)}) collective-permute-start(f32[128,128]{1,0:T(8,128)S(1)} %fusion.51), channel_id=1, source_target_pairs={{0,1},{1,0},{2,3},{3,2},{4,5},{5,4},{6,7},{7,6},{8,9},{9,8},{10,11... | collective-permute-start | bytes 196616 | tf_op jit(solution)/shard_map/ppermute | solution.py:23
  74.8 4.7 %collective-permute-start.1 = (f32[128,128]{1,0:T(8,128)S(1)}, f32[128,128]{1,0:T(8,128)S(1)}, u32[]{:S(2)}, u32[]{:S(2)}) collective-permute-start(f32[128,128]{1,0:T(8,128)S(1)} %add.79), channel_id=1, source_target_pairs={{0,2},{1,3},{2,0},{3,1},{4,6},{5,7},{6,4},{7,5},{8,10},{9,11},{10,... | collective-permute-start | bytes 196616 | tf_op jit(solution)/shard_map/ppermute | solution.py:23
  79.5 6.0 %collective-permute-start.2 = (f32[128,128]{1,0:T(8,128)S(1)}, f32[128,128]{1,0:T(8,128)S(1)}, u32[]{:S(2)}, u32[]{:S(2)}) collective-permute-start(f32[128,128]{1,0:T(8,128)S(1)} %add.80), channel_id=1, source_target_pairs={{0,4},{1,5},{2,6},{3,7},{4,0},{5,1},{6,2},{7,3},{8,12},{9,13},{10,... | collective-permute-start | bytes 196616 | tf_op jit(solution)/shard_map/ppermute | solution.py:23
  85.5 32.8 %collective-permute-start.3 = (f32[128,128]{1,0:T(8,128)S(1)}, f32[128,128]{1,0:T(8,128)S(1)}, u32[]{:S(2)}, u32[]{:S(2)}) collective-permute-start(f32[128,128]{1,0:T(8,128)S(1)} %add.81), channel_id=1, source_target_pairs={{0,8},{8,0},{16,24},{24,16},{32,40},{40,32},{48,56},{56,48},{64,72... | collective-permute-start | bytes 196616 | tf_op jit(solution)/shard_map/ppermute | solution.py:23
  118.3 6.2 %collective-permute-start.4 = (f32[128,128]{1,0:T(8,128)S(1)}, f32[128,128]{1,0:T(8,128)S(1)}, u32[]{:S(2)}, u32[]{:S(2)}) collective-permute-start(f32[128,128]{1,0:T(8,128)S(1)} %add.82), channel_id=1, source_target_pairs={{0,16},{8,24},{16,0},{24,8},{32,48},{40,56},{48,32},{56,40},{64,80... | collective-permute-start | bytes 196616 | tf_op jit(solution)/shard_map/ppermute | solution.py:23
  124.4 7.2 %collective-permute-start.5 = (f32[128,128]{1,0:T(8,128)S(1)}, f32[128,128]{1,0:T(8,128)S(1)}, u32[]{:S(2)}, u32[]{:S(2)}) collective-permute-start(f32[128,128]{1,0:T(8,128)S(1)} %add.83), channel_id=1, source_target_pairs={{0,32},{8,40},{16,48},{24,56},{32,0},{40,8},{48,16},{56,24},{64,96... | collective-permute-start | bytes 196616 | tf_op jit(solution)/shard_map/ppermute | solution.py:23
  131.6 3.2 %collective-permute-start.6 = (f32[128,128]{1,0:T(8,128)S(1)}, f32[128,128]{1,0:T(8,128)S(1)}, u32[]{:S(2)}, u32[]{:S(2)}) collective-permute-start(f32[128,128]{1,0:T(8,128)S(1)} %add.84), channel_id=1, source_target_pairs={{0,64},{8,72},{16,80},{24,88},{32,96},{40,104},{48,112},{56,120},{... | collective-permute-start | bytes 196616 | tf_op jit(solution)/shard_map/ppermute | solution.py:23
  134.9 5.2 %collective-permute-start.7 = (f32[128,128]{1,0:T(8,128)S(1)}, f32[128,128]{1,0:T(8,128)S(1)}, u32[]{:S(2)}, u32[]{:S(2)}) collective-permute-start(f32[128,128]{1,0:T(8,128)S(1)} %add.85), channel_id=1, source_target_pairs={{0,128},{8,136},{16,144},{24,152},{32,160},{40,168},{48,176},{56,1... | collective-permute-start | bytes 196616 | tf_op jit(solution)/shard_map/ppermute | solution.py:23
  155.0 3.6 %copy-start.4 = (s32[64]{0:T(128)S(1)}, s32[64]{0:T(128)}, u32[]{:S(2)}) copy-start(s32[64]{0:T(128)} %param.5) | copy-start | bytes 772
  155.0 3.7 %copy-start.1 = (bf16[4096,128]{1,0:T(8,128)(2,1)S(1)}, bf16[4096,128]{1,0:T(8,128)(2,1)}, u32[]{:S(2)}) copy-start(bf16[4096,128]{1,0:T(8,128)(2,1)} %gather_fusion) | copy-start | bytes 3145732
  162.9 71.2 %copy-start.2 = (f32[64,128]{1,0:T(8,128)}, f32[64,128]{1,0:T(8,128)S(1)}, u32[]{:S(2)}) copy-start(f32[64,128]{1,0:T(8,128)S(1)} %multiply_add_fusion) | copy-start | bytes 98308

commit v3 on v2

--- a/solution.py
+++ b/solution.py
@@ -1,6 +1,7 @@
 import jax
 import jax.numpy as jnp
 from jax import lax
+from jax.experimental import pallas as pl
 from jax.sharding import PartitionSpec as P
 
 ITERS = 3
@@ -23,6 +24,56 @@
             value = value + lax.ppermute(value, axis, partners)
             stride *= 2
     return value
+
+
+def pick_rows_kernel(index_ref, table_ref, out_ref):
+    block = index_ref.shape[0]
+    row_ids = lax.broadcasted_iota(jnp.int32, (block, table_ref.shape[0]), 1)
+    picks = (index_ref[...] == row_ids).astype(jnp.bfloat16)
+    out_ref[...] = jnp.dot(picks, table_ref[...], preferred_element_type=jnp.float32).astype(
+        out_ref.dtype
+    )
+
+
+def pick_rows(table, index, block=512):
+    count = index.shape[0]
+    rows, width = table.shape
+    padded = -(-rows // 256) * 256
+    table = jnp.pad(table, ((0, padded - rows), (0, 0)))
+    return pl.pallas_call(
+        pick_rows_kernel,
+        grid=(count // block,),
+        in_specs=[
+            pl.BlockSpec((block, 1), lambda i: (i, 0)),
+            pl.BlockSpec((padded, width), lambda i: (0, 0)),
+        ],
+        out_specs=pl.BlockSpec((block, width), lambda i: (i, 0)),
+        out_shape=jax.ShapeDtypeStruct((count, width), table.dtype),
+    )(index.reshape(count, 1), table)
+
+
+def add_rows_kernel(index_ref, values_ref, out_ref):
+    @pl.when(pl.program_id(0) == 0)
+    def _():
+        out_ref[...] = jnp.zeros_like(out_ref)
+
+    row_ids = lax.broadcasted_iota(jnp.int32, (out_ref.shape[0], index_ref.shape[1]), 0)
+    picks = (row_ids == index_ref[...]).astype(jnp.bfloat16)
+    out_ref[...] += jnp.dot(picks, values_ref[...], preferred_element_type=jnp.float32)
+
+
+def add_rows(values, index, rows, block=512):
+    count, width = values.shape
+    return pl.pallas_call(
+        add_rows_kernel,
+        grid=(count // block,),
+        in_specs=[
+            pl.BlockSpec((1, block), lambda i: (0, i)),
+            pl.BlockSpec((block, width), lambda i: (i, 0)),
+        ],
+        out_specs=pl.BlockSpec((rows, width), lambda i: (0, 0)),
+        out_shape=jax.ShapeDtypeStruct((rows, width), jnp.float32),
+    )(index.reshape(1, count), values)
 
 
 def on_device(item_table, histories, counts):
@@ -75,9 +126,7 @@
     slot_index = (owners * capacity + ranks.astype(jnp.int32)).reshape(lookups)
 
     incoming = exchange(requests).reshape(slots_total)
-    table_ids = lax.broadcasted_iota(jnp.int32, (slots_total, table_rows), 1)
-    picks = (incoming[:, None] == table_ids).astype(bf16)
-    answered = jnp.dot(picks, item_table, preferred_element_type=f32).astype(bf16)
+    answered = pick_rows(item_table, incoming)
     reply_rows = exchange(answered.reshape(devices, capacity, embed_width)).reshape(
         slots_total, embed_width
     )
@@ -111,7 +160,7 @@
     partials = jnp.einsum("su,uk->sk", member, solution.astype(bf16), preferred_element_type=f32)
     partials = partials.astype(bf16).reshape(devices, capacity, embed_width)
     arrived = exchange(partials).reshape(slots_total, embed_width)
-    item_rhs = jnp.einsum("st,sk->tk", picks, arrived, preferred_element_type=f32)
+    item_rhs = add_rows(arrived, incoming, table_rows)
     return (solution, item_rhs)
 
 

time: 246 us -> 250 us (1.016)
  blocking collectives: 98.2 us -> 0 us
  waiting for transfers between devices: 53.3 us -> 118 us
  starting transfers between devices: 20.3 us -> 52.7 us
  matrix products: 45.7 us -> 14.1 us
  Pallas kernels: 0 us -> 30.4 us
  local copies, waits for them, and re-layouts: 18.7 us -> 25 us
    all_to_all x2 -> x0, blocking collectives: 98.2 us -> none  [exchange(): return lax.all_to_all(values, ('rows', 'grp'), 0, 0, tiled=True)]
    all_to_all x1 -> x3, waiting for transfers between devices: 0.01 us -> 64.6 us  [exchange(): return lax.all_to_all(values, ('rows', 'grp'), 0, 0, tiled=True)]
    all_to_all x1 -> x3, starting transfers between devices: 5.72 us -> 37.9 us  [exchange(): return lax.all_to_all(values, ('rows', 'grp'), 0, 0, tiled=True)]
    dot_general x2 -> x0, matrix products: 30.5 us -> none  [the longest x1 19.4 us: on_device(): jnp.dot(picks, item_table, preferred_element_type=f32).astype(bf16)]
    pallas_call x0 -> x2, Pallas kernels: none -> 30.4 us  [the longest x1 15.7 us: pick_rows(): pl.pallas_call(pick_rows_kernel, grid=(count // block,), in_specs=[pl.Blo...]
    another operation x0 -> x2, local copies, waits for them, and re-layouts: none -> 6.39 us  [the longest x1 5.65 us: pick_rows(): index.reshape(count, 1)]
    gather x1, local copies, waits for them, and re-layouts: 14.9 us -> 12.1 us  [on_device(): jnp.take(reply_rows, slot_index, axis=0, mode='clip')]
  transfers between devices with their start and end apart: 9 -> 11, of which waited for: 8 -> 10; matrix products, arithmetic and copies ran while one was open for 0% -> 1% of each run, Pallas kernels for 0% -> 0%
where the time goes in v3:
time: 250 us; the launch traced here: 249 us
  waiting for transfers between devices  118 us (47%)
  starting transfers between devices  52.7 us (21%)
  Pallas kernels  30.4 us (12%)
  local copies, waits for them, and re-layouts  25 us (10%)
  matrix products  14.1 us (6%)
  other arithmetic  7.87 us (3%)
    all_to_all x3, waiting for transfers between devices, exchange(): return lax.all_to_all(values, ('rows', 'grp'), 0, 0, tiled=True)  64.6 us
    ppermute x8, waiting for transfers between devices, sum_over_devices(): value = value + lax.ppermute(value, axis, partners)  53.3 us
    all_to_all x3, starting transfers between devices, exchange(): return lax.all_to_all(values, ('rows', 'grp'), 0, 0, tiled=True)  37.9 us
    pallas_call x1, Pallas kernels, pick_rows(): pl.pallas_call(pick_rows_kernel, grid=(count // block,), in_specs=[pl.Blo...  15.7 us
    ppermute x8, starting transfers between devices, sum_over_devices(): value = value + lax.ppermute(value, axis, partners)  14.8 us
    pallas_call x1, Pallas kernels, add_rows(): pl.pallas_call(add_rows_kernel, grid=(count // block,), in_specs=[pl.Bloc...  14.6 us
    gather x1, local copies, waits for them, and re-layouts, on_device(): jnp.take(reply_rows, slot_index, axis=0, mode='clip')  12.1 us
    another operation x1, local copies, waits for them, and re-layouts, pick_rows(): index.reshape(count, 1)  5.65 us
  transfers between devices with their start and end apart: 11, of which 10 were waited for; matrix products, arithmetic and copies ran while one was open for 1% of the time, Pallas kernels for 0%

profile of v3, /device:TPU:1, one launch (start us, length us, event | category | flops | bytes accessed | tf_op | source)
XLA Modules:
  0.0 249.0 jit_solution(3912858898567767412)
XLA Ops:
  0.7 0.7 fusion.37
  1.4 0.8 add_select_fusion.1
  2.2 1.4 convert_reduce_fusion
  3.6 0.1 fusion.31
  3.7 4.4 %fusion = f32[64,64]{1,0:T(8,128)S(1)} fusion(f32[64,256]{1,0:T(8,128)S(1)} %fusion.31, pred[64,64]{1,0:T(8,128)(4,1)S(1)} %get-tuple-element.16, s32[64,64]{1,0:T(8,128)S(1)} %add_select_fusion.1), kind=kOutput, calls=%fused_computation.3 | convolution fusion | flops 143654912 | bytes 102400 | tf_op jit(solution)/shard_map/jk,uko->ujo/dot_general | solution.py:104
  8.2 2.5 fusion.1
  10.7 0.2 fusion.14
  11.0 0.1 maximum_maximum_fusion
  11.0 0.2 broadcast_multiply_fusion
  11.2 2.5 %mul.140 = bf16[4096,128]{0,1:T(8,128)(2,1)} reshape(bf16[64,64,4,32]{1,0,3,2:T(8,128)(2,1)S(1)} %broadcast_multiply_fusion) | data formatting | bytes 2097152 | tf_op jit(solution)/shard_map/mul | solution.py:117
  13.7 2.2 convolution_convert_fusion.1
  16.0 0.8 copy.16
  16.7 15.7 %all-to-all-start = ((s32[256,1,32]{2,1,0:T(1,128)}), s32[256,1,32]{2,1,0:T(1,128)S(1)}, u32[]{:S(2)}, u32[]{:S(2)}) async-start(s32[256,1,32]{2,1,0:T(1,128)} %copy.16), calls=%async_computation | async-start | bytes 262144 | tf_op jit(solution)/shard_map/all_to_all | solution.py:15
  32.4 0.8 pad.4.table_ref
  33.2 11.9 %all-to-all-done = s32[256,1,32]{2,1,0:T(1,128)S(1)} async-done(((s32[256,1,32]{2,1,0:T(1,128)}), s32[256,1,32]{2,1,0:T(1,128)S(1)}, u32[]{:S(2)}, u32[]{:S(2)}) %all-to-all-start) | async-done | bytes 32800 | tf_op jit(solution)/shard_map/all_to_all | solution.py:15
  45.2 0.5 broadcast.130
  45.7 1.0 reduce.6
  46.7 5.7 %reshape_reshape.8.index_ref = s32[8192,1]{1,0:T(8,128)} reshape(s32[256,32]{1,0:T(8,128)S(1)} %reduce.6) | data formatting | bytes 65536 | tf_op jit(solution)/shard_map/reshape;reshape | solution.py:52
  52.3 15.7 %shard_map.50 = bf16[8192,128]{1,0:T(8,128)(2,1)} custom-call(s32[8192,1]{1,0:T(8,128)} %reshape_reshape.8.index_ref, bf16[2048,128]{1,0:T(8,128)(2,1)} %pad.4.table_ref), custom_call_target="tpu_custom_call" | custom-call | tf_op jit(solution)/shard_map/pallas_call | solution.py:43
  68.0 5.5 %all-to-all-start.1 = ((bf16[256,32,128]{2,1,0:T(8,128)(2,1)}), bf16[256,32,128]{2,1,0:T(8,128)(2,1)S(1)}, u32[]{:S(2)}, u32[]{:S(2)}) async-start(bf16[256,32,128]{2,1,0:T(8,128)(2,1)} %bitcast.79), calls=%async_computation.1 | async-start | bytes 4194304 | tf_op jit(solution)/shard_map/all_to_all | solution.py:15
  73.6 0.3 fusion.46
  73.9 2.4 collective-permute-start
  76.3 0.9 collective-permute-done
  77.2 0.1 collective-permute-start.1
  77.3 4.6 %collective-permute-done.1 = f32[128,128]{1,0:T(8,128)S(1)} collective-permute-done((f32[128,128]{1,0:T(8,128)S(1)}, f32[128,128]{1,0:T(8,128)S(1)}, u32[]{:S(2)}, u32[]{:S(2)}) %collective-permute-start.1) | collective-permute-done | bytes 65568 | tf_op jit(solution)/shard_map/ppermute | solution.py:24
  81.9 1.3 collective-permute-start.2
  83.2 4.7 %collective-permute-done.2 = f32[128,128]{1,0:T(8,128)S(1)} collective-permute-done((f32[128,128]{1,0:T(8,128)S(1)}, f32[128,128]{1,0:T(8,128)S(1)}, u32[]{:S(2)}, u32[]{:S(2)}) %collective-permute-start.2) | collective-permute-done | bytes 65568 | tf_op jit(solution)/shard_map/ppermute | solution.py:24
  87.9 0.1 collective-permute-start.3
  88.0 32.7 %collective-permute-done.3 = f32[128,128]{1,0:T(8,128)S(1)} collective-permute-done((f32[128,128]{1,0:T(8,128)S(1)}, f32[128,128]{1,0:T(8,128)S(1)}, u32[]{:S(2)}, u32[]{:S(2)}) %collective-permute-start.3) | collective-permute-done | bytes 65568 | tf_op jit(solution)/shard_map/ppermute | solution.py:24
  120.7 1.4 collective-permute-start.4
  122.1 4.8 %collective-permute-done.4 = f32[128,128]{1,0:T(8,128)S(1)} collective-permute-done((f32[128,128]{1,0:T(8,128)S(1)}, f32[128,128]{1,0:T(8,128)S(1)}, u32[]{:S(2)}, u32[]{:S(2)}) %collective-permute-start.4) | collective-permute-done | bytes 65568 | tf_op jit(solution)/shard_map/ppermute | solution.py:24
  126.9 4.7 %collective-permute-start.5 = (f32[128,128]{1,0:T(8,128)S(1)}, f32[128,128]{1,0:T(8,128)S(1)}, u32[]{:S(2)}, u32[]{:S(2)}) collective-permute-start(f32[128,128]{1,0:T(8,128)S(1)} %add.85), channel_id=1, source_target_pairs={{0,32},{8,40},{16,48},{24,56},{32,0},{40,8},{48,16},{56,24},{64,96... | collective-permute-start | bytes 196616 | tf_op jit(solution)/shard_map/ppermute | solution.py:24
  131.6 2.5 %collective-permute-done.5 = f32[128,128]{1,0:T(8,128)S(1)} collective-permute-done((f32[128,128]{1,0:T(8,128)S(1)}, f32[128,128]{1,0:T(8,128)S(1)}, u32[]{:S(2)}, u32[]{:S(2)}) %collective-permute-start.5) | collective-permute-done | bytes 65568 | tf_op jit(solution)/shard_map/ppermute | solution.py:24
  134.1 1.8 collective-permute-start.6
  135.9 1.6 collective-permute-done.6
  137.5 3.1 %collective-permute-start.7 = (f32[128,128]{1,0:T(8,128)S(1)}, f32[128,128]{1,0:T(8,128)S(1)}, u32[]{:S(2)}, u32[]{:S(2)}) collective-permute-start(f32[128,128]{1,0:T(8,128)S(1)} %add.87), channel_id=1, source_target_pairs={{0,128},{8,136},{16,144},{24,152},{32,160},{40,168},{48,176},{56,1... | collective-permute-start | bytes 196616 | tf_op jit(solution)/shard_map/ppermute | solution.py:24
  140.6 0.1 copy.19
  140.8 0.1 gt.16
  140.9 0.1 copy.18
  141.0 0.1 eq.42
  141.1 1.6 collective-permute-done.7
  142.7 12.1 %gather_fusion = bf16[4096,128]{1,0:T(8,128)(2,1)S(1)} fusion(bf16[8192,128]{1,0:T(8,128)(2,1)S(1)} %bitcast.78, s32[4096]{0:T(1024)S(1)} %broadcast_clamp_fusion), kind=kCustom, calls=%fused_computation | custom fusion | bytes 2113536 | tf_op jit(solution)/shard_map/jit(_take)/gather | solution.py:133
  154.9 0.4 fusion.29
  155.3 0.6 fusion.27
  156.0 0.4 fusion.25
  156.4 0.3 multiply_reduce_fusion.3
  156.7 0.2 multiply_reduce_fusion.2
  156.9 0.1 convert_bitcast_fusion.1
  157.0 0.6 fusion.23
  157.6 0.1 fusion.39
  157.7 0.4 fusion.21
  158.1 0.3 multiply_reduce_fusion.1
  158.4 0.2 multiply_reduce_fusion
  158.6 0.1 convert_bitcast_fusion
  158.7 0.6 fusion.19
  159.4 0.4 fusion.17
  159.8 0.3 fusion.11
  160.1 0.1 multiply_add_fusion
  160.2 2.6 %convolution_convert_fusion = bf16[8192,128]{1,0:T(8,128)(2,1)} fusion(s32[8192]{0:T(1024)S(1)} %eq.42, pred[8192]{0:T(1024)(128)(4,1)S(1)} %gt.16, f32[64,128]{1,0:T(8,128)S(1)} %multiply_add_fusion), kind=kOutput, calls=%fused_computation.1 | convolution fusion | flops 136323072 | bytes 2170880 | tf_op jit(solution)/shard_map/su,uk->sk/dot_general | solution.py:160
  162.9 16.7 %all-to-all-start.2 = ((bf16[256,32,128]{2,1,0:T(8,128)(2,1)}), bf16[256,32,128]{2,1,0:T(8,128)(2,1)S(1)}, u32[]{:S(2)}, u32[]{:S(2)}) async-start(bf16[256,32,128]{2,1,0:T(8,128)(2,1)} %bitcast.81), calls=%async_computation.2 | async-start | bytes 4194304 | tf_op jit(solution)/shard_map/all_to_all | solution.py:15
  179.6 0.7 reshape_reshape.7.index_ref
  180.3 52.7 %all-to-all-done.2 = bf16[256,32,128]{2,1,0:T(8,128)(2,1)S(1)} async-done(((bf16[256,32,128]{2,1,0:T(8,128)(2,1)}), bf16[256,32,128]{2,1,0:T(8,128)(2,1)S(1)}, u32[]{:S(2)}, u32[]{:S(2)}) %all-to-all-start.2) | async-done | bytes 2097184 | tf_op jit(solution)/shard_map/all_to_all | solution.py:15
  233.0 1.3 copy-done
  234.4 14.6 %shard_map.51 = f32[1984,128]{1,0:T(8,128)} custom-call(s32[1,8192]{1,0:T(1,128)} %reshape_reshape.7.index_ref, bf16[8192,128]{1,0:T(8,128)(2,1)} %bitcast.80), custom_call_target="tpu_custom_call" | custom-call | tf_op jit(solution)/shard_map/pallas_call | solution.py:67
  (34 shorter events, 0.5 us)
Async XLA Ops:
  0.6 7.5 %copy-start.3 = (s32[64,64]{1,0:T(8,128)S(1)}, s32[64,64]{1,0:T(8,128)}, u32[]{:S(2)}) copy-start(s32[64,64]{1,0:T(8,128)} %param.4) | copy-start | bytes 49156
  11.2 21.2 %copy-start.1 = (bf16[1984,128]{1,0:T(8,128)(2,1)S(1)}, bf16[1984,128]{1,0:T(8,128)(2,1)}, u32[]{:S(2)}) copy-start(bf16[1984,128]{1,0:T(8,128)(2,1)} %param.3) | copy-start | bytes 1523716
  16.7 28.5 %all-to-all-start = ((s32[256,1,32]{2,1,0:T(1,128)}), s32[256,1,32]{2,1,0:T(1,128)S(1)}, u32[]{:S(2)}, u32[]{:S(2)}) async-start(s32[256,1,32]{2,1,0:T(1,128)} %copy.16), calls=%async_computation | async-start | bytes 262144 | tf_op jit(solution)/shard_map/all_to_all | solution.py:15
  68.0 74.7 %all-to-all-start.1 = ((bf16[256,32,128]{2,1,0:T(8,128)(2,1)}), bf16[256,32,128]{2,1,0:T(8,128)(2,1)S(1)}, u32[]{:S(2)}, u32[]{:S(2)}) async-start(bf16[256,32,128]{2,1,0:T(8,128)(2,1)} %bitcast.79), calls=%async_computation.1 | async-start | bytes 4194304 | tf_op jit(solution)/shard_map/all_to_all | solution.py:15
  73.9 3.3 %collective-permute-start = (f32[128,128]{1,0:T(8,128)S(1)}, f32[128,128]{1,0:T(8,128)S(1)}, u32[]{:S(2)}, u32[]{:S(2)}) collective-permute-start(f32[128,128]{1,0:T(8,128)S(1)} %fusion.46), channel_id=1, source_target_pairs={{0,1},{1,0},{2,3},{3,2},{4,5},{5,4},{6,7},{7,6},{8,9},{9,8},{10,11... | collective-permute-start | bytes 196616 | tf_op jit(solution)/shard_map/ppermute | solution.py:24
  77.2 4.7 %collective-permute-start.1 = (f32[128,128]{1,0:T(8,128)S(1)}, f32[128,128]{1,0:T(8,128)S(1)}, u32[]{:S(2)}, u32[]{:S(2)}) collective-permute-start(f32[128,128]{1,0:T(8,128)S(1)} %add.81), channel_id=1, source_target_pairs={{0,2},{1,3},{2,0},{3,1},{4,6},{5,7},{6,4},{7,5},{8,10},{9,11},{10,... | collective-permute-start | bytes 196616 | tf_op jit(solution)/shard_map/ppermute | solution.py:24
  81.9 6.0 %collective-permute-start.2 = (f32[128,128]{1,0:T(8,128)S(1)}, f32[128,128]{1,0:T(8,128)S(1)}, u32[]{:S(2)}, u32[]{:S(2)}) collective-permute-start(f32[128,128]{1,0:T(8,128)S(1)} %add.82), channel_id=1, source_target_pairs={{0,4},{1,5},{2,6},{3,7},{4,0},{5,1},{6,2},{7,3},{8,12},{9,13},{10,... | collective-permute-start | bytes 196616 | tf_op jit(solution)/shard_map/ppermute | solution.py:24
  87.9 32.8 %collective-permute-start.3 = (f32[128,128]{1,0:T(8,128)S(1)}, f32[128,128]{1,0:T(8,128)S(1)}, u32[]{:S(2)}, u32[]{:S(2)}) collective-permute-start(f32[128,128]{1,0:T(8,128)S(1)} %add.83), channel_id=1, source_target_pairs={{0,8},{8,0},{16,24},{24,16},{32,40},{40,32},{48,56},{56,48},{64,72... | collective-permute-start | bytes 196616 | tf_op jit(solution)/shard_map/ppermute | solution.py:24
  120.7 6.2 %collective-permute-start.4 = (f32[128,128]{1,0:T(8,128)S(1)}, f32[128,128]{1,0:T(8,128)S(1)}, u32[]{:S(2)}, u32[]{:S(2)}) collective-permute-start(f32[128,128]{1,0:T(8,128)S(1)} %add.84), channel_id=1, source_target_pairs={{0,16},{8,24},{16,0},{24,8},{32,48},{40,56},{48,32},{56,40},{64,80... | collective-permute-start | bytes 196616 | tf_op jit(solution)/shard_map/ppermute | solution.py:24
  126.9 7.2 %collective-permute-start.5 = (f32[128,128]{1,0:T(8,128)S(1)}, f32[128,128]{1,0:T(8,128)S(1)}, u32[]{:S(2)}, u32[]{:S(2)}) collective-permute-start(f32[128,128]{1,0:T(8,128)S(1)} %add.85), channel_id=1, source_target_pairs={{0,32},{8,40},{16,48},{24,56},{32,0},{40,8},{48,16},{56,24},{64,96... | collective-permute-start | bytes 196616 | tf_op jit(solution)/shard_map/ppermute | solution.py:24
  134.1 3.4 %collective-permute-start.6 = (f32[128,128]{1,0:T(8,128)S(1)}, f32[128,128]{1,0:T(8,128)S(1)}, u32[]{:S(2)}, u32[]{:S(2)}) collective-permute-start(f32[128,128]{1,0:T(8,128)S(1)} %add.86), channel_id=1, source_target_pairs={{0,64},{8,72},{16,80},{24,88},{32,96},{40,104},{48,112},{56,120},{... | collective-permute-start | bytes 196616 | tf_op jit(solution)/shard_map/ppermute | solution.py:24
  137.5 5.2 %collective-permute-start.7 = (f32[128,128]{1,0:T(8,128)S(1)}, f32[128,128]{1,0:T(8,128)S(1)}, u32[]{:S(2)}, u32[]{:S(2)}) collective-permute-start(f32[128,128]{1,0:T(8,128)S(1)} %add.87), channel_id=1, source_target_pairs={{0,128},{8,136},{16,144},{24,152},{32,160},{40,168},{48,176},{56,1... | collective-permute-start | bytes 196616 | tf_op jit(solution)/shard_map/ppermute | solution.py:24
  142.7 13.2 %copy-start.4 = (s32[64]{0:T(128)S(1)}, s32[64]{0:T(128)}, u32[]{:S(2)}) copy-start(s32[64]{0:T(128)} %param.5) | copy-start | bytes 772
  160.2 88.8 %copy-start.2 = (f32[64,128]{1,0:T(8,128)}, f32[64,128]{1,0:T(8,128)S(1)}, u32[]{:S(2)}) copy-start(f32[64,128]{1,0:T(8,128)S(1)} %multiply_add_fusion) | copy-start | bytes 98308
  162.9 70.1 %all-to-all-start.2 = ((bf16[256,32,128]{2,1,0:T(8,128)(2,1)}), bf16[256,32,128]{2,1,0:T(8,128)(2,1)S(1)}, u32[]{:S(2)}, u32[]{:S(2)}) async-start(bf16[256,32,128]{2,1,0:T(8,128)(2,1)} %bitcast.81), calls=%async_computation.2 | async-start | bytes 4194304 | tf_op jit(solution)/shard_map/all_to_all | solution.py:15
  233.0 1.3 copy-start

commit v4 on v2

--- a/solution.py
+++ b/solution.py
@@ -48,22 +48,29 @@
     local_rows = histories - owners * table_rows
     owner_ids = lax.broadcasted_iota(jnp.int32, (user_count, history_length, devices), 2)
     by_owner = ((owners[:, :, None] == owner_ids) & live[:, :, None]).astype(bf16)
-    slot_ids = lax.broadcasted_iota(jnp.int32, (history_length, history_length), 0)
-    earlier = (lax.broadcasted_iota(jnp.int32, (history_length, history_length), 1) < slot_ids).astype(bf16)
-    within_user = jnp.einsum("jk,uko->ujo", earlier, by_owner, preferred_element_type=f32)
     per_user = jnp.sum(by_owner.astype(f32), axis=1)
     user_ids = lax.broadcasted_iota(jnp.int32, (user_count, user_count), 0)
     earlier_users = (lax.broadcasted_iota(jnp.int32, (user_count, user_count), 1) < user_ids).astype(bf16)
     before_user = jnp.einsum("uv,vo->uo", earlier_users, per_user.astype(bf16), preferred_element_type=f32)
-    ranks = jnp.sum(by_owner.astype(f32) * (within_user + before_user[:, None, :]), axis=2)
-    rank_ids = lax.broadcasted_iota(jnp.int32, (user_count, history_length, capacity), 2)
-    by_rank = ((ranks.astype(jnp.int32)[:, :, None] == rank_ids) & live[:, :, None]).astype(bf16)
+    companions = jnp.concatenate([by_owner, before_user.astype(bf16)[:, None, :]], axis=1)
+    same = jnp.einsum("ujo,uko->ujk", by_owner, companions, preferred_element_type=f32)
+    slot_ids = lax.broadcasted_iota(jnp.int32, (history_length, history_length + 1), 0)
+    other_ids = lax.broadcasted_iota(jnp.int32, (history_length, history_length + 1), 1)
+    counted = ((other_ids < slot_ids) | (other_ids == history_length)).astype(f32)
+    ranks = jnp.sum(same * counted[None], axis=2).astype(jnp.int32).reshape(lookups)
 
-    row_high = local_rows // 32
-    row_low = local_rows - row_high * 32
-    user_of = lax.broadcasted_iota(jnp.int32, (user_count, history_length), 0)
-    payload = jnp.stack([row_high, row_low, user_of, jnp.ones_like(user_of)], axis=2).astype(bf16)
-    spread = (payload[:, :, :, None] * by_rank[:, :, None, :]).reshape(lookups, 4 * capacity)
+    flat_rows = local_rows.reshape(lookups, 1)
+    row_high = flat_rows // 32
+    row_low = flat_rows - row_high * 32
+    user_of = lax.broadcasted_iota(jnp.int32, (user_count, history_length), 0).reshape(lookups, 1)
+    flat_live = live.reshape(lookups, 1)
+    columns = lax.broadcasted_iota(jnp.int32, (lookups, 4 * capacity), 1)
+    part = columns // capacity
+    chosen = (columns - part * capacity == ranks[:, None]) & flat_live
+    value = jnp.where(
+        part == 0, row_high, jnp.where(part == 1, row_low, jnp.where(part == 2, user_of, 1))
+    )
+    spread = jnp.where(chosen, value, 0).astype(bf16)
     slots = jnp.einsum(
         "io,ic->oc", by_owner.reshape(lookups, devices), spread, preferred_element_type=f32
     ).reshape(devices, 4, capacity)
@@ -72,7 +79,7 @@
     slot_user = slots[:, 2].reshape(slots_total)
     slot_used = slots[:, 3].reshape(slots_total)
 
-    slot_index = (owners * capacity + ranks.astype(jnp.int32)).reshape(lookups)
+    slot_index = owners.reshape(lookups) * capacity + ranks
 
     incoming = exchange(requests).reshape(slots_total)
     table_ids = lax.broadcasted_iota(jnp.int32, (slots_total, table_rows), 1)

time: 246 us -> 240 us (0.976)
    mul x1 -> x0, local copies, waits for them, and re-layouts: 2.49 us -> none  [on_device(): payload[:, :, :, None] * by_rank[:, :, None, :]]
where the time goes in v4:
time: 240 us
  blocking collectives  98.2 us (41%)
  waiting for transfers between devices  53.3 us (22%)
  matrix products  44 us (18%)
  starting transfers between devices  20.3 us (8%)
  local copies, waits for them, and re-layouts  16.6 us (7%)
  other arithmetic  6.47 us (3%)
    all_to_all x2, blocking collectives, exchange(): return lax.all_to_all(values, ('rows', 'grp'), 0, 0, tiled=True)  98.2 us
    ppermute x8, waiting for transfers between devices, sum_over_devices(): value = value + lax.ppermute(value, axis, partners)  53.3 us
    dot_general x1, matrix products, on_device(): jnp.dot(picks, item_table, preferred_element_type=f32).astype(bf16)  19.4 us
    gather x1, local copies, waits for them, and re-layouts, on_device(): jnp.take(reply_rows, slot_index, axis=0, mode='clip')  14.9 us
    ppermute x8, starting transfers between devices, sum_over_devices(): value = value + lax.ppermute(value, axis, partners)  14.6 us
    dot_general x1, matrix products, on_device(): jnp.einsum('st,sk->tk', picks, arrived, preferred_element_type=f32)  11 us
    all_to_all x1, starting transfers between devices, exchange(): return lax.all_to_all(values, ('rows', 'grp'), 0, 0, tiled=True)  5.72 us
  transfers between devices with their start and end apart: 9, of which 8 were waited for; matrix products, arithmetic and copies ran while one was open for 0% of the time, Pallas kernels for 0%

profile of v4, /device:TPU:1, one launch (start us, length us, event | category | flops | bytes accessed | tf_op | source)
XLA Modules:
  0.0 239.9 jit_solution(8003408992131985950)
XLA Ops:
  0.7 0.8 fusion.75
  1.5 0.1 lt.32
  1.6 0.8 add_select_fusion
  2.4 0.1 eq.92
  2.4 1.4 fusion.56
  3.8 1.4 fusion.10
  5.3 0.1 fusion.28
  5.4 0.1 copy.18
  5.5 3.2 %multiply_reduce_fusion = f32[64,64]{1,0:T(8,128)S(1)} fusion(f32[64,65]{1,0:T(8,128)S(1)} %fusion.73, bf16[64,1,256]{2,1,0:T(2,128)(2,1)S(1)} %copy.18, bf16[64,64,256]{2,1,0:T(8,128)(2,1)S(1)} %fusion.10, s32[64,64]{1,0:T(8,128)S(1)} %add_select_fusion, pred[64,64]{1,0:T(8,128)(4,1)S(1)} %get-tuple-element.17), kind=kOutput, calls=%fused_computation.27 | convolution fusion | flops 143200256 | bytes 2183424 | tf_op jit(solution)/shard_map/ujo,uko->ujk/dot_general | solution.py:56
  8.8 0.1 broadcast_in_dim.46
  8.9 0.1 convert_element_type.87
  9.0 0.1 reshape.341
  9.1 1.7 fusion.25
  10.8 0.1 copy.19
  10.9 28.3 %all_to_all.16 = s32[256,1,32]{2,1,0:T(1,128)S(1)} all-to-all(s32[256,1,32]{2,1,0:T(1,128)S(1)} %copy.19), channel_id=1, replica_groups=mesh['rows'=32,'grp'=8] {'rows','grp'}, dimensions={0} | all-to-all | bytes 65536 | tf_op jit(solution)/shard_map/all_to_all | solution.py:14
  39.1 0.5 broadcast.337
  39.6 1.0 reduce.4
  40.6 0.1 eq.105
  40.7 19.4 %fusion.4 = bf16[8192,128]{1,0:T(8,128)(2,1)} fusion(bf16[1984,128]{1,0:T(8,128)(2,1)S(1)} %copy-done, s32[8192]{0:T(1024)S(1)} %eq.105), kind=kOutput, calls=%fused_computation.6 | convolution fusion | flops 4178051072 | bytes 2637824 | tf_op jit(solution)/shard_map/dot_general | solution.py:87
  60.2 5.7 %all-to-all-start.1 = ((bf16[256,32,128]{2,1,0:T(8,128)(2,1)}), bf16[256,32,128]{2,1,0:T(8,128)(2,1)S(1)}, u32[]{:S(2)}, u32[]{:S(2)}) async-start(bf16[256,32,128]{2,1,0:T(8,128)(2,1)} %bitcast.64), calls=%async_computation.1 | async-start | bytes 4194304 | tf_op jit(solution)/shard_map/all_to_all | solution.py:14
  65.9 0.3 fusion.89
  66.2 2.4 collective-permute-start
  68.6 0.9 collective-permute-done
  69.5 0.1 collective-permute-start.1
  69.6 4.6 %collective-permute-done.1 = f32[128,128]{1,0:T(8,128)S(1)} collective-permute-done((f32[128,128]{1,0:T(8,128)S(1)}, f32[128,128]{1,0:T(8,128)S(1)}, u32[]{:S(2)}, u32[]{:S(2)}) %collective-permute-start.1) | collective-permute-done | bytes 65568 | tf_op jit(solution)/shard_map/ppermute | solution.py:23
  74.2 1.3 collective-permute-start.2
  75.5 4.7 %collective-permute-done.2 = f32[128,128]{1,0:T(8,128)S(1)} collective-permute-done((f32[128,128]{1,0:T(8,128)S(1)}, f32[128,128]{1,0:T(8,128)S(1)}, u32[]{:S(2)}, u32[]{:S(2)}) %collective-permute-start.2) | collective-permute-done | bytes 65568 | tf_op jit(solution)/shard_map/ppermute | solution.py:23
  80.2 0.1 collective-permute-start.3
  80.3 32.7 %collective-permute-done.3 = f32[128,128]{1,0:T(8,128)S(1)} collective-permute-done((f32[128,128]{1,0:T(8,128)S(1)}, f32[128,128]{1,0:T(8,128)S(1)}, u32[]{:S(2)}, u32[]{:S(2)}) %collective-permute-start.3) | collective-permute-done | bytes 65568 | tf_op jit(solution)/shard_map/ppermute | solution.py:23
  113.0 1.4 collective-permute-start.4
  114.4 4.8 %collective-permute-done.4 = f32[128,128]{1,0:T(8,128)S(1)} collective-permute-done((f32[128,128]{1,0:T(8,128)S(1)}, f32[128,128]{1,0:T(8,128)S(1)}, u32[]{:S(2)}, u32[]{:S(2)}) %collective-permute-start.4) | collective-permute-done | bytes 65568 | tf_op jit(solution)/shard_map/ppermute | solution.py:23
  119.2 4.7 %collective-permute-start.5 = (f32[128,128]{1,0:T(8,128)S(1)}, f32[128,128]{1,0:T(8,128)S(1)}, u32[]{:S(2)}, u32[]{:S(2)}) collective-permute-start(f32[128,128]{1,0:T(8,128)S(1)} %add.99), channel_id=1, source_target_pairs={{0,32},{8,40},{16,48},{24,56},{32,0},{40,8},{48,16},{56,24},{64,96... | collective-permute-start | bytes 196616 | tf_op jit(solution)/shard_map/ppermute | solution.py:23
  123.9 2.5 %collective-permute-done.5 = f32[128,128]{1,0:T(8,128)S(1)} collective-permute-done((f32[128,128]{1,0:T(8,128)S(1)}, f32[128,128]{1,0:T(8,128)S(1)}, u32[]{:S(2)}, u32[]{:S(2)}) %collective-permute-start.5) | collective-permute-done | bytes 65568 | tf_op jit(solution)/shard_map/ppermute | solution.py:23
  126.4 1.6 collective-permute-start.6
  128.0 0.1 reshape.349
  128.1 1.6 collective-permute-done.6
  129.6 3.1 %collective-permute-start.7 = (f32[128,128]{1,0:T(8,128)S(1)}, f32[128,128]{1,0:T(8,128)S(1)}, u32[]{:S(2)}, u32[]{:S(2)}) collective-permute-start(f32[128,128]{1,0:T(8,128)S(1)} %add.101), channel_id=1, source_target_pairs={{0,128},{8,136},{16,144},{24,152},{32,160},{40,168},{48,176},{56,1... | collective-permute-start | bytes 196616 | tf_op jit(solution)/shard_map/ppermute | solution.py:23
  132.8 0.1 copy.21
  132.9 0.1 gt.16
  133.0 0.1 copy.20
  133.1 0.1 eq.108
  133.2 1.6 collective-permute-done.7
  134.8 14.9 %gather_fusion = bf16[4096,128]{1,0:T(8,128)(2,1)} fusion(bf16[8192,128]{1,0:T(8,128)(2,1)S(1)} %bitcast.62, s32[4096]{0:T(1024)S(1)} %broadcast_clamp_fusion), kind=kCustom, calls=%fused_computation | custom fusion | bytes 2113536 | tf_op jit(solution)/shard_map/jit(_take)/gather | solution.py:91
  149.7 1.7 fusion.69
  151.4 1.9 fusion.67
  153.3 0.1 fusion.76
  153.4 0.4 fusion.65
  153.8 0.3 multiply_reduce_fusion.4
  154.1 0.2 multiply_reduce_fusion.3
  154.3 0.1 convert_bitcast_fusion.1
  154.4 0.6 fusion.63
  155.0 0.1 fusion.77
  155.1 0.4 fusion.61
  155.5 0.3 multiply_reduce_fusion.2
  155.8 0.2 multiply_reduce_fusion.1
  156.0 0.1 convert_bitcast_fusion
  156.1 0.6 fusion.59
  156.8 0.1 fusion.78
  156.8 0.4 fusion.57
  157.2 0.3 fusion.36
  157.5 0.1 multiply_add_fusion
  157.7 1.3 convolution_convert_fusion
  158.9 69.9 %all_to_all.17 = bf16[256,32,128]{2,1,0:T(8,128)(2,1)S(1)} all-to-all(bf16[256,32,128]{2,1,0:T(8,128)(2,1)S(1)} %bitcast.63), channel_id=1, replica_groups=mesh['rows'=32,'grp'=8] {'rows','grp'}, dimensions={0} | all-to-all | bytes 4194304 | tf_op jit(solution)/shard_map/all_to_all | solution.py:14
  228.9 11.0 %fusion = f32[1984,128]{1,0:T(8,128)} fusion(bf16[8192,128]{1,0:T(8,128)(2,1)S(1)} %bitcast.65, s32[8192]{0:T(1024)S(1)} %eq.105), kind=kOutput, calls=%fused_computation.2 | convolution fusion | flops 4177002496 | bytes 3145728 | tf_op jit(solution)/shard_map/st,sk->tk/dot_general | solution.py:121
  (37 shorter events, 0.3 us)
Async XLA Ops:
  0.6 40.1 %copy-start = (bf16[1984,128]{1,0:T(8,128)(2,1)S(1)}, bf16[1984,128]{1,0:T(8,128)(2,1)}, u32[]{:S(2)}) copy-start(bf16[1984,128]{1,0:T(8,128)(2,1)} %param.3) | copy-start | bytes 1523716
  5.5 3.3 %copy-start.3 = (s32[64,64]{1,0:T(8,128)S(1)}, s32[64,64]{1,0:T(8,128)}, u32[]{:S(2)}) copy-start(s32[64,64]{1,0:T(8,128)} %param.4) | copy-start | bytes 49156
  60.2 74.7 %all-to-all-start.1 = ((bf16[256,32,128]{2,1,0:T(8,128)(2,1)}), bf16[256,32,128]{2,1,0:T(8,128)(2,1)S(1)}, u32[]{:S(2)}, u32[]{:S(2)}) async-start(bf16[256,32,128]{2,1,0:T(8,128)(2,1)} %bitcast.64), calls=%async_computation.1 | async-start | bytes 4194304 | tf_op jit(solution)/shard_map/all_to_all | solution.py:14
  66.2 3.3 %collective-permute-start = (f32[128,128]{1,0:T(8,128)S(1)}, f32[128,128]{1,0:T(8,128)S(1)}, u32[]{:S(2)}, u32[]{:S(2)}) collective-permute-start(f32[128,128]{1,0:T(8,128)S(1)} %fusion.89), channel_id=1, source_target_pairs={{0,1},{1,0},{2,3},{3,2},{4,5},{5,4},{6,7},{7,6},{8,9},{9,8},{10,11... | collective-permute-start | bytes 196616 | tf_op jit(solution)/shard_map/ppermute | solution.py:23
  69.5 4.7 %collective-permute-start.1 = (f32[128,128]{1,0:T(8,128)S(1)}, f32[128,128]{1,0:T(8,128)S(1)}, u32[]{:S(2)}, u32[]{:S(2)}) collective-permute-start(f32[128,128]{1,0:T(8,128)S(1)} %add.95), channel_id=1, source_target_pairs={{0,2},{1,3},{2,0},{3,1},{4,6},{5,7},{6,4},{7,5},{8,10},{9,11},{10,... | collective-permute-start | bytes 196616 | tf_op jit(solution)/shard_map/ppermute | solution.py:23
  74.2 6.0 %collective-permute-start.2 = (f32[128,128]{1,0:T(8,128)S(1)}, f32[128,128]{1,0:T(8,128)S(1)}, u32[]{:S(2)}, u32[]{:S(2)}) collective-permute-start(f32[128,128]{1,0:T(8,128)S(1)} %add.96), channel_id=1, source_target_pairs={{0,4},{1,5},{2,6},{3,7},{4,0},{5,1},{6,2},{7,3},{8,12},{9,13},{10,... | collective-permute-start | bytes 196616 | tf_op jit(solution)/shard_map/ppermute | solution.py:23
  80.2 32.8 %collective-permute-start.3 = (f32[128,128]{1,0:T(8,128)S(1)}, f32[128,128]{1,0:T(8,128)S(1)}, u32[]{:S(2)}, u32[]{:S(2)}) collective-permute-start(f32[128,128]{1,0:T(8,128)S(1)} %add.97), channel_id=1, source_target_pairs={{0,8},{8,0},{16,24},{24,16},{32,40},{40,32},{48,56},{56,48},{64,72... | collective-permute-start | bytes 196616 | tf_op jit(solution)/shard_map/ppermute | solution.py:23
  113.0 6.2 %collective-permute-start.4 = (f32[128,128]{1,0:T(8,128)S(1)}, f32[128,128]{1,0:T(8,128)S(1)}, u32[]{:S(2)}, u32[]{:S(2)}) collective-permute-start(f32[128,128]{1,0:T(8,128)S(1)} %add.98), channel_id=1, source_target_pairs={{0,16},{8,24},{16,0},{24,8},{32,48},{40,56},{48,32},{56,40},{64,80... | collective-permute-start | bytes 196616 | tf_op jit(solution)/shard_map/ppermute | solution.py:23
  119.2 7.2 %collective-permute-start.5 = (f32[128,128]{1,0:T(8,128)S(1)}, f32[128,128]{1,0:T(8,128)S(1)}, u32[]{:S(2)}, u32[]{:S(2)}) collective-permute-start(f32[128,128]{1,0:T(8,128)S(1)} %add.99), channel_id=1, source_target_pairs={{0,32},{8,40},{16,48},{24,56},{32,0},{40,8},{48,16},{56,24},{64,96... | collective-permute-start | bytes 196616 | tf_op jit(solution)/shard_map/ppermute | solution.py:23
  126.4 3.2 %collective-permute-start.6 = (f32[128,128]{1,0:T(8,128)S(1)}, f32[128,128]{1,0:T(8,128)S(1)}, u32[]{:S(2)}, u32[]{:S(2)}) collective-permute-start(f32[128,128]{1,0:T(8,128)S(1)} %add.100), channel_id=1, source_target_pairs={{0,64},{8,72},{16,80},{24,88},{32,96},{40,104},{48,112},{56,120},{... | collective-permute-start | bytes 196616 | tf_op jit(solution)/shard_map/ppermute | solution.py:23
  129.6 5.2 %collective-permute-start.7 = (f32[128,128]{1,0:T(8,128)S(1)}, f32[128,128]{1,0:T(8,128)S(1)}, u32[]{:S(2)}, u32[]{:S(2)}) collective-permute-start(f32[128,128]{1,0:T(8,128)S(1)} %add.101), channel_id=1, source_target_pairs={{0,128},{8,136},{16,144},{24,152},{32,160},{40,168},{48,176},{56,1... | collective-permute-start | bytes 196616 | tf_op jit(solution)/shard_map/ppermute | solution.py:23
  149.7 3.6 %copy-start.4 = (s32[64]{0:T(128)S(1)}, s32[64]{0:T(128)}, u32[]{:S(2)}) copy-start(s32[64]{0:T(128)} %param.5) | copy-start | bytes 772
  149.7 3.7 %copy-start.1 = (bf16[4096,128]{1,0:T(8,128)(2,1)S(1)}, bf16[4096,128]{1,0:T(8,128)(2,1)}, u32[]{:S(2)}) copy-start(bf16[4096,128]{1,0:T(8,128)(2,1)} %gather_fusion) | copy-start | bytes 3145732
  157.6 71.2 %copy-start.2 = (f32[64,128]{1,0:T(8,128)}, f32[64,128]{1,0:T(8,128)S(1)}, u32[]{:S(2)}) copy-start(f32[64,128]{1,0:T(8,128)S(1)} %multiply_add_fusion) | copy-start | bytes 98308

commit v5 on v4

--- a/solution.py
+++ b/solution.py
@@ -88,9 +88,8 @@
     reply_rows = exchange(answered.reshape(devices, capacity, embed_width)).reshape(
         slots_total, embed_width
     )
-    fetched = jnp.take(reply_rows, slot_index, axis=0, mode="clip").reshape(
-        user_count, history_length, embed_width
-    )
+    fetched = reply_rows.astype(f32).at[slot_index].get(mode="promise_in_bounds")
+    fetched = fetched.astype(bf16).reshape(user_count, history_length, embed_width)
     weights = live.astype(f32)
     narrow_weights = weights.astype(bf16)
     target = jnp.einsum("ul,ulk->uk", narrow_weights, fetched, preferred_element_type=f32)

time: 240 us -> 240 us (level)
  no operation moved by 1% of the time
where the time goes in v5:
time: 240 us
  blocking collectives  98.2 us (41%)
  waiting for transfers between devices  53.3 us (22%)
  matrix products  44 us (18%)
  starting transfers between devices  20.3 us (8%)
  local copies, waits for them, and re-layouts  16.6 us (7%)
  other arithmetic  6.49 us (3%)
    all_to_all x2, blocking collectives, exchange(): return lax.all_to_all(values, ('rows', 'grp'), 0, 0, tiled=True)  98.2 us
    ppermute x8, waiting for transfers between devices, sum_over_devices(): value = value + lax.ppermute(value, axis, partners)  53.3 us
    dot_general x1, matrix products, on_device(): jnp.dot(picks, item_table, preferred_element_type=f32).astype(bf16)  19.4 us
    gather x1, local copies, waits for them, and re-layouts, on_device(): reply_rows.astype(f32).at[slot_index].get(mode='promise_in_bounds')  14.9 us
    ppermute x8, starting transfers between devices, sum_over_devices(): value = value + lax.ppermute(value, axis, partners)  14.6 us
    dot_general x1, matrix products, on_device(): jnp.einsum('st,sk->tk', picks, arrived, preferred_element_type=f32)  11 us
    all_to_all x1, starting transfers between devices, exchange(): return lax.all_to_all(values, ('rows', 'grp'), 0, 0, tiled=True)  5.72 us
  transfers between devices with their start and end apart: 9, of which 8 were waited for; matrix products, arithmetic and copies ran while one was open for 0% of the time, Pallas kernels for 0%

profile of v5, /device:TPU:1, one launch (start us, length us, event | category | flops | bytes accessed | tf_op | source)
XLA Modules:
  0.0 239.9 jit_solution(14904958177693494763)
XLA Ops:
  0.7 0.8 fusion.75
  1.5 0.1 lt.43
  1.6 0.8 add_select_fusion
  2.4 0.1 eq.92
  2.4 1.4 fusion.56
  3.8 1.4 fusion.10
  5.3 0.1 fusion.28
  5.4 0.1 copy.18
  5.5 3.2 %multiply_reduce_fusion = f32[64,64]{1,0:T(8,128)S(1)} fusion(f32[64,65]{1,0:T(8,128)S(1)} %fusion.73, bf16[64,1,256]{2,1,0:T(2,128)(2,1)S(1)} %copy.18, bf16[64,64,256]{2,1,0:T(8,128)(2,1)S(1)} %fusion.10, s32[64,64]{1,0:T(8,128)S(1)} %add_select_fusion, pred[64,64]{1,0:T(8,128)(4,1)S(1)} %get-tuple-element.17), kind=kOutput, calls=%fused_computation.28 | convolution fusion | flops 143200256 | bytes 2183424 | tf_op jit(solution)/shard_map/ujo,uko->ujk/dot_general | solution.py:56
  8.8 0.1 broadcast_in_dim.45
  8.9 0.1 convert_element_type.100
  9.0 0.1 reshape.350
  9.1 1.7 fusion.25
  10.8 0.1 copy.19
  10.9 28.3 %all_to_all.16 = s32[256,1,32]{2,1,0:T(1,128)S(1)} all-to-all(s32[256,1,32]{2,1,0:T(1,128)S(1)} %copy.19), channel_id=1, replica_groups=mesh['rows'=32,'grp'=8] {'rows','grp'}, dimensions={0} | all-to-all | bytes 65536 | tf_op jit(solution)/shard_map/all_to_all | solution.py:14
  39.1 0.5 broadcast.355
  39.6 1.0 reduce.4
  40.6 0.1 eq.105
  40.7 19.4 %fusion.4 = bf16[8192,128]{1,0:T(8,128)(2,1)} fusion(bf16[1984,128]{1,0:T(8,128)(2,1)S(1)} %copy-done, s32[8192]{0:T(1024)S(1)} %eq.105), kind=kOutput, calls=%fused_computation.6 | convolution fusion | flops 4178051072 | bytes 2637824 | tf_op jit(solution)/shard_map/dot_general | solution.py:87
  60.2 5.7 %all-to-all-start.1 = ((bf16[256,32,128]{2,1,0:T(8,128)(2,1)}), bf16[256,32,128]{2,1,0:T(8,128)(2,1)S(1)}, u32[]{:S(2)}, u32[]{:S(2)}) async-start(bf16[256,32,128]{2,1,0:T(8,128)(2,1)} %bitcast.68), calls=%async_computation.1 | async-start | bytes 4194304 | tf_op jit(solution)/shard_map/all_to_all | solution.py:14
  65.9 0.3 fusion.89
  66.2 2.4 collective-permute-start
  68.6 0.9 collective-permute-done
  69.5 0.1 collective-permute-start.1
  69.6 4.6 %collective-permute-done.1 = f32[128,128]{1,0:T(8,128)S(1)} collective-permute-done((f32[128,128]{1,0:T(8,128)S(1)}, f32[128,128]{1,0:T(8,128)S(1)}, u32[]{:S(2)}, u32[]{:S(2)}) %collective-permute-start.1) | collective-permute-done | bytes 65568 | tf_op jit(solution)/shard_map/ppermute | solution.py:23
  74.2 1.3 collective-permute-start.2
  75.5 4.7 %collective-permute-done.2 = f32[128,128]{1,0:T(8,128)S(1)} collective-permute-done((f32[128,128]{1,0:T(8,128)S(1)}, f32[128,128]{1,0:T(8,128)S(1)}, u32[]{:S(2)}, u32[]{:S(2)}) %collective-permute-start.2) | collective-permute-done | bytes 65568 | tf_op jit(solution)/shard_map/ppermute | solution.py:23
  80.2 0.1 collective-permute-start.3
  80.3 32.7 %collective-permute-done.3 = f32[128,128]{1,0:T(8,128)S(1)} collective-permute-done((f32[128,128]{1,0:T(8,128)S(1)}, f32[128,128]{1,0:T(8,128)S(1)}, u32[]{:S(2)}, u32[]{:S(2)}) %collective-permute-start.3) | collective-permute-done | bytes 65568 | tf_op jit(solution)/shard_map/ppermute | solution.py:23
  113.0 1.4 collective-permute-start.4
  114.4 0.1 add.107
  114.5 4.7 %collective-permute-done.4 = f32[128,128]{1,0:T(8,128)S(1)} collective-permute-done((f32[128,128]{1,0:T(8,128)S(1)}, f32[128,128]{1,0:T(8,128)S(1)}, u32[]{:S(2)}, u32[]{:S(2)}) %collective-permute-start.4) | collective-permute-done | bytes 65568 | tf_op jit(solution)/shard_map/ppermute | solution.py:23
  119.2 4.7 %collective-permute-start.5 = (f32[128,128]{1,0:T(8,128)S(1)}, f32[128,128]{1,0:T(8,128)S(1)}, u32[]{:S(2)}, u32[]{:S(2)}) collective-permute-start(f32[128,128]{1,0:T(8,128)S(1)} %add.114), channel_id=1, source_target_pairs={{0,32},{8,40},{16,48},{24,56},{32,0},{40,8},{48,16},{56,24},{64,96... | collective-permute-start | bytes 196616 | tf_op jit(solution)/shard_map/ppermute | solution.py:23
  123.9 2.5 %collective-permute-done.5 = f32[128,128]{1,0:T(8,128)S(1)} collective-permute-done((f32[128,128]{1,0:T(8,128)S(1)}, f32[128,128]{1,0:T(8,128)S(1)}, u32[]{:S(2)}, u32[]{:S(2)}) %collective-permute-start.5) | collective-permute-done | bytes 65568 | tf_op jit(solution)/shard_map/ppermute | solution.py:23
  126.4 1.6 collective-permute-start.6
  128.0 1.6 collective-permute-done.6
  129.6 3.1 %collective-permute-start.7 = (f32[128,128]{1,0:T(8,128)S(1)}, f32[128,128]{1,0:T(8,128)S(1)}, u32[]{:S(2)}, u32[]{:S(2)}) collective-permute-start(f32[128,128]{1,0:T(8,128)S(1)} %add.116), channel_id=1, source_target_pairs={{0,128},{8,136},{16,144},{24,152},{32,160},{40,168},{48,176},{56,1... | collective-permute-start | bytes 196616 | tf_op jit(solution)/shard_map/ppermute | solution.py:23
  132.8 0.1 copy.21
  132.9 0.1 gt.16
  133.0 0.1 copy.20
  133.1 0.1 eq.108
  133.2 1.6 collective-permute-done.7
  134.8 14.9 %gather_fusion = bf16[4096,128]{1,0:T(8,128)(2,1)} fusion(bf16[8192,128]{1,0:T(8,128)(2,1)S(1)} %bitcast.66, s32[4096]{0:T(1024)S(1)} %broadcast_clamp_fusion), kind=kCustom, calls=%fused_computation | custom fusion | bytes 2113536 | tf_op jit(solution)/shard_map/gather | solution.py:91
  149.7 1.7 fusion.69
  151.4 1.9 fusion.67
  153.3 0.1 fusion.76
  153.4 0.4 fusion.65
  153.8 0.3 multiply_reduce_fusion.4
  154.1 0.2 multiply_reduce_fusion.3
  154.3 0.1 convert_bitcast_fusion.1
  154.4 0.6 fusion.63
  155.0 0.1 fusion.77
  155.1 0.4 fusion.61
  155.5 0.3 multiply_reduce_fusion.2
  155.8 0.2 multiply_reduce_fusion.1
  156.0 0.1 convert_bitcast_fusion
  156.1 0.6 fusion.59
  156.8 0.1 fusion.78
  156.8 0.4 fusion.57
  157.2 0.3 fusion.36
  157.5 0.1 multiply_add_fusion
  157.7 1.3 convolution_convert_fusion
  158.9 69.9 %all_to_all.17 = bf16[256,32,128]{2,1,0:T(8,128)(2,1)S(1)} all-to-all(bf16[256,32,128]{2,1,0:T(8,128)(2,1)S(1)} %bitcast.67), channel_id=1, replica_groups=mesh['rows'=32,'grp'=8] {'rows','grp'}, dimensions={0} | all-to-all | bytes 4194304 | tf_op jit(solution)/shard_map/all_to_all | solution.py:14
  228.9 11.0 %fusion = f32[1984,128]{1,0:T(8,128)} fusion(bf16[8192,128]{1,0:T(8,128)(2,1)S(1)} %bitcast.69, s32[8192]{0:T(1024)S(1)} %eq.105), kind=kOutput, calls=%fused_computation.2 | convolution fusion | flops 4177002496 | bytes 3145728 | tf_op jit(solution)/shard_map/st,sk->tk/dot_general | solution.py:120
  (38 shorter events, 0.3 us)
Async XLA Ops:
  0.6 40.1 %copy-start = (bf16[1984,128]{1,0:T(8,128)(2,1)S(1)}, bf16[1984,128]{1,0:T(8,128)(2,1)}, u32[]{:S(2)}) copy-start(bf16[1984,128]{1,0:T(8,128)(2,1)} %param.3) | copy-start | bytes 1523716
  5.5 3.3 %copy-start.3 = (s32[64,64]{1,0:T(8,128)S(1)}, s32[64,64]{1,0:T(8,128)}, u32[]{:S(2)}) copy-start(s32[64,64]{1,0:T(8,128)} %param.4) | copy-start | bytes 49156
  60.2 74.7 %all-to-all-start.1 = ((bf16[256,32,128]{2,1,0:T(8,128)(2,1)}), bf16[256,32,128]{2,1,0:T(8,128)(2,1)S(1)}, u32[]{:S(2)}, u32[]{:S(2)}) async-start(bf16[256,32,128]{2,1,0:T(8,128)(2,1)} %bitcast.68), calls=%async_computation.1 | async-start | bytes 4194304 | tf_op jit(solution)/shard_map/all_to_all | solution.py:14
  66.2 3.3 %collective-permute-start = (f32[128,128]{1,0:T(8,128)S(1)}, f32[128,128]{1,0:T(8,128)S(1)}, u32[]{:S(2)}, u32[]{:S(2)}) collective-permute-start(f32[128,128]{1,0:T(8,128)S(1)} %fusion.89), channel_id=1, source_target_pairs={{0,1},{1,0},{2,3},{3,2},{4,5},{5,4},{6,7},{7,6},{8,9},{9,8},{10,11... | collective-permute-start | bytes 196616 | tf_op jit(solution)/shard_map/ppermute | solution.py:23
  69.5 4.7 %collective-permute-start.1 = (f32[128,128]{1,0:T(8,128)S(1)}, f32[128,128]{1,0:T(8,128)S(1)}, u32[]{:S(2)}, u32[]{:S(2)}) collective-permute-start(f32[128,128]{1,0:T(8,128)S(1)} %add.110), channel_id=1, source_target_pairs={{0,2},{1,3},{2,0},{3,1},{4,6},{5,7},{6,4},{7,5},{8,10},{9,11},{10,... | collective-permute-start | bytes 196616 | tf_op jit(solution)/shard_map/ppermute | solution.py:23
  74.2 6.0 %collective-permute-start.2 = (f32[128,128]{1,0:T(8,128)S(1)}, f32[128,128]{1,0:T(8,128)S(1)}, u32[]{:S(2)}, u32[]{:S(2)}) collective-permute-start(f32[128,128]{1,0:T(8,128)S(1)} %add.111), channel_id=1, source_target_pairs={{0,4},{1,5},{2,6},{3,7},{4,0},{5,1},{6,2},{7,3},{8,12},{9,13},{10,... | collective-permute-start | bytes 196616 | tf_op jit(solution)/shard_map/ppermute | solution.py:23
  80.2 32.8 %collective-permute-start.3 = (f32[128,128]{1,0:T(8,128)S(1)}, f32[128,128]{1,0:T(8,128)S(1)}, u32[]{:S(2)}, u32[]{:S(2)}) collective-permute-start(f32[128,128]{1,0:T(8,128)S(1)} %add.112), channel_id=1, source_target_pairs={{0,8},{8,0},{16,24},{24,16},{32,40},{40,32},{48,56},{56,48},{64,72... | collective-permute-start | bytes 196616 | tf_op jit(solution)/shard_map/ppermute | solution.py:23
  113.0 6.2 %collective-permute-start.4 = (f32[128,128]{1,0:T(8,128)S(1)}, f32[128,128]{1,0:T(8,128)S(1)}, u32[]{:S(2)}, u32[]{:S(2)}) collective-permute-start(f32[128,128]{1,0:T(8,128)S(1)} %add.113), channel_id=1, source_target_pairs={{0,16},{8,24},{16,0},{24,8},{32,48},{40,56},{48,32},{56,40},{64,80... | collective-permute-start | bytes 196616 | tf_op jit(solution)/shard_map/ppermute | solution.py:23
  119.2 7.2 %collective-permute-start.5 = (f32[128,128]{1,0:T(8,128)S(1)}, f32[128,128]{1,0:T(8,128)S(1)}, u32[]{:S(2)}, u32[]{:S(2)}) collective-permute-start(f32[128,128]{1,0:T(8,128)S(1)} %add.114), channel_id=1, source_target_pairs={{0,32},{8,40},{16,48},{24,56},{32,0},{40,8},{48,16},{56,24},{64,96... | collective-permute-start | bytes 196616 | tf_op jit(solution)/shard_map/ppermute | solution.py:23
  126.4 3.2 %collective-permute-start.6 = (f32[128,128]{1,0:T(8,128)S(1)}, f32[128,128]{1,0:T(8,128)S(1)}, u32[]{:S(2)}, u32[]{:S(2)}) collective-permute-start(f32[128,128]{1,0:T(8,128)S(1)} %add.115), channel_id=1, source_target_pairs={{0,64},{8,72},{16,80},{24,88},{32,96},{40,104},{48,112},{56,120},{... | collective-permute-start | bytes 196616 | tf_op jit(solution)/shard_map/ppermute | solution.py:23
  129.6 5.2 %collective-permute-start.7 = (f32[128,128]{1,0:T(8,128)S(1)}, f32[128,128]{1,0:T(8,128)S(1)}, u32[]{:S(2)}, u32[]{:S(2)}) collective-permute-start(f32[128,128]{1,0:T(8,128)S(1)} %add.116), channel_id=1, source_target_pairs={{0,128},{8,136},{16,144},{24,152},{32,160},{40,168},{48,176},{56,1... | collective-permute-start | bytes 196616 | tf_op jit(solution)/shard_map/ppermute | solution.py:23
  149.7 3.6 %copy-start.4 = (s32[64]{0:T(128)S(1)}, s32[64]{0:T(128)}, u32[]{:S(2)}) copy-start(s32[64]{0:T(128)} %param.5) | copy-start | bytes 772
  149.7 3.7 %copy-start.1 = (bf16[4096,128]{1,0:T(8,128)(2,1)S(1)}, bf16[4096,128]{1,0:T(8,128)(2,1)}, u32[]{:S(2)}) copy-start(bf16[4096,128]{1,0:T(8,128)(2,1)} %gather_fusion) | copy-start | bytes 3145732
  157.7 71.2 %copy-start.2 = (f32[64,128]{1,0:T(8,128)}, f32[64,128]{1,0:T(8,128)S(1)}, u32[]{:S(2)}) copy-start(f32[64,128]{1,0:T(8,128)S(1)} %multiply_add_fusion) | copy-start | bytes 98308

commit v6 on v5

--- a/solution.py
+++ b/solution.py
@@ -1,6 +1,8 @@
 import jax
 import jax.numpy as jnp
 from jax import lax
+from jax.experimental import pallas as pl
+from jax.experimental.pallas import tpu as pltpu
 from jax.sharding import PartitionSpec as P
 
 ITERS = 3
@@ -23,6 +25,31 @@
             value = value + lax.ppermute(value, axis, partners)
             stride *= 2
     return value
+
+
+def gather_rows_kernel(index_ref, source_ref, out_ref):
+    def body(i, carry):
+        out_ref[pl.ds(i, 1), :] = source_ref[pl.ds(index_ref[i], 1), :]
+        return carry
+
+    lax.fori_loop(0, out_ref.shape[0], body, 0, unroll=8)
+
+
+def gather_rows(source, index):
+    count = index.shape[0]
+    rows, width = source.shape
+    wide = source.astype(jnp.float32)
+    picked = pl.pallas_call(
+        gather_rows_kernel,
+        grid_spec=pltpu.PrefetchScalarGridSpec(
+            num_scalar_prefetch=1,
+            grid=(1,),
+            in_specs=[pl.BlockSpec((rows, width), lambda i, index_ref: (0, 0))],
+            out_specs=pl.BlockSpec((count, width), lambda i, index_ref: (0, 0)),
+        ),
+        out_shape=jax.ShapeDtypeStruct((count, width), jnp.float32),
+    )(index, wide)
+    return picked.astype(source.dtype)
 
 
 def on_device(item_table, histories, counts):
@@ -88,8 +115,7 @@
     reply_rows = exchange(answered.reshape(devices, capacity, embed_width)).reshape(
         slots_total, embed_width
     )
-    fetched = reply_rows.astype(f32).at[slot_index].get(mode="promise_in_bounds")
-    fetched = fetched.astype(bf16).reshape(user_count, history_length, embed_width)
+    fetched = gather_rows(reply_rows, slot_index).reshape(user_count, history_length, embed_width)
     weights = live.astype(f32)
     narrow_weights = weights.astype(bf16)
     target = jnp.einsum("ul,ulk->uk", narrow_weights, fetched, preferred_element_type=f32)

time: 240 us -> 237 us (0.988)
  local copies, waits for them, and re-layouts: 16.6 us -> 1.57 us
  Pallas kernels: 0 us -> 10.1 us
  other arithmetic: 6.49 us -> 11.1 us
  matrix products: 44 us -> 41.5 us
    gather x1 -> x0, local copies, waits for them, and re-layouts: 14.9 us -> none  [on_device(): reply_rows.astype(f32).at[slot_index].get(mode='promise_in_bounds')]
    pallas_call x0 -> x1, Pallas kernels: none -> 10.1 us  [gather_rows(): pl.pallas_call(gather_rows_kernel, grid_spec=pltpu.PrefetchScalarGridSpec...]
    convert_element_type x0 -> x2, other arithmetic: none -> 4.04 us  [the longest x1 2.33 us: gather_rows(): wide = source.astype(jnp.float32)]
  transfers between devices with their start and end apart: 9 -> 9, of which waited for: 8 -> 8; matrix products, arithmetic and copies ran while one was open for 0% -> 1% of each run, Pallas kernels for 0% -> 0%
where the time goes in v6:
time: 237 us
  blocking collectives  98.2 us (41%)
  waiting for transfers between devices  52.8 us (22%)
  matrix products  41.5 us (18%)
  starting transfers between devices  20.4 us (9%)
  other arithmetic  11.1 us (5%)
  Pallas kernels  10.1 us (4%)
    all_to_all x2, blocking collectives, exchange(): return lax.all_to_all(values, ('rows', 'grp'), 0, 0, tiled=True)  98.2 us
    ppermute x8, waiting for transfers between devices, sum_over_devices(): value = value + lax.ppermute(value, axis, partners)  52.8 us
    dot_general x1, matrix products, on_device(): jnp.dot(picks, item_table, preferred_element_type=f32).astype(bf16)  19.4 us
    ppermute x8, starting transfers between devices, sum_over_devices(): value = value + lax.ppermute(value, axis, partners)  14.6 us
    dot_general x1, matrix products, on_device(): jnp.einsum('st,sk->tk', picks, arrived, preferred_element_type=f32)  11 us
    pallas_call x1, Pallas kernels, gather_rows(): pl.pallas_call(gather_rows_kernel, grid_spec=pltpu.PrefetchScalarGridSpec...  10.1 us
    all_to_all x1, starting transfers between devices, exchange(): return lax.all_to_all(values, ('rows', 'grp'), 0, 0, tiled=True)  5.72 us
  transfers between devices with their start and end apart: 9, of which 8 were waited for; matrix products, arithmetic and copies ran while one was open for 1% of the time, Pallas kernels for 0%

profile of v6, /device:TPU:1, one launch (start us, length us, event | category | flops | bytes accessed | tf_op | source)
XLA Modules:
  0.0 236.5 jit_solution(9859139933327331143)
XLA Ops:
  0.7 0.8 fusion.75
  1.5 0.1 lt.34
  1.6 0.8 multiply_subtract_fusion.2
  2.4 0.1 reshape.317
  2.4 1.4 fusion.56
  3.8 1.4 fusion.8
  5.3 0.1 broadcast_in_dim.44
  5.5 0.1 fusion.28
  5.6 3.2 %multiply_reduce_fusion = f32[64,64]{1,0:T(8,128)S(1)} fusion(f32[64,65]{1,0:T(8,128)S(1)} %fusion.73, bf16[64,1,256]{2,1,0:T(2,128)(2,1)S(1)} %copy.18, bf16[64,64,256]{2,1,0:T(8,128)(2,1)S(1)} %fusion.8, s32[64,64]{1,0:T(8,128)S(1)} %get-tuple-element.13, pred[64,64]{1,0:T(8,128)(4,1)S(1)} %get-tuple-element.17), kind=kOutput, calls=%fused_computation.28 | convolution fusion | flops 143200256 | bytes 2183424 | tf_op jit(solution)/shard_map/ujo,uko->ujk/dot_general | solution.py:83
  8.9 0.1 convert_element_type.88
  9.0 1.7 fusion.25
  10.7 0.1 copy.19
  10.8 28.3 %all_to_all.16 = s32[256,1,32]{2,1,0:T(1,128)S(1)} all-to-all(s32[256,1,32]{2,1,0:T(1,128)S(1)} %copy.19), channel_id=1, replica_groups=mesh['rows'=32,'grp'=8] {'rows','grp'}, dimensions={0} | all-to-all | bytes 65536 | tf_op jit(solution)/shard_map/all_to_all | solution.py:16
  39.1 0.5 broadcast.323
  39.6 1.0 reduce.4
  40.6 0.1 eq.102
  40.7 19.4 %fusion.4 = bf16[8192,128]{1,0:T(8,128)(2,1)} fusion(bf16[1984,128]{1,0:T(8,128)(2,1)S(1)} %copy-done, s32[8192]{0:T(1024)S(1)} %eq.102), kind=kOutput, calls=%fused_computation.5 | convolution fusion | flops 4178051072 | bytes 2637824 | tf_op jit(solution)/shard_map/dot_general | solution.py:114
  60.1 5.7 %all-to-all-start.1 = ((bf16[256,32,128]{2,1,0:T(8,128)(2,1)}), bf16[256,32,128]{2,1,0:T(8,128)(2,1)S(1)}, u32[]{:S(2)}, u32[]{:S(2)}) async-start(bf16[256,32,128]{2,1,0:T(8,128)(2,1)} %bitcast.65), calls=%async_computation.1 | async-start | bytes 4194304 | tf_op jit(solution)/shard_map/all_to_all | solution.py:16
  65.8 0.3 fusion.89
  66.2 2.4 %collective-permute-start = (f32[128,128]{1,0:T(8,128)S(1)}, f32[128,128]{1,0:T(8,128)S(1)}, u32[]{:S(2)}, u32[]{:S(2)}) collective-permute-start(f32[128,128]{1,0:T(8,128)S(1)} %fusion.89), channel_id=1, source_target_pairs={{0,1},{1,0},{2,3},{3,2},{4,5},{5,4},{6,7},{7,6},{8,9},{9,8},{10,11... | collective-permute-start | bytes 196616 | tf_op jit(solution)/shard_map/ppermute | solution.py:25
  68.6 0.9 collective-permute-done
  69.5 0.1 collective-permute-start.1
  69.6 4.6 %collective-permute-done.1 = f32[128,128]{1,0:T(8,128)S(1)} collective-permute-done((f32[128,128]{1,0:T(8,128)S(1)}, f32[128,128]{1,0:T(8,128)S(1)}, u32[]{:S(2)}, u32[]{:S(2)}) %collective-permute-start.1) | collective-permute-done | bytes 65568 | tf_op jit(solution)/shard_map/ppermute | solution.py:25
  74.2 1.3 collective-permute-start.2
  75.4 4.7 %collective-permute-done.2 = f32[128,128]{1,0:T(8,128)S(1)} collective-permute-done((f32[128,128]{1,0:T(8,128)S(1)}, f32[128,128]{1,0:T(8,128)S(1)}, u32[]{:S(2)}, u32[]{:S(2)}) %collective-permute-start.2) | collective-permute-done | bytes 65568 | tf_op jit(solution)/shard_map/ppermute | solution.py:25
  80.2 0.1 collective-permute-start.3
  80.3 32.7 %collective-permute-done.3 = f32[128,128]{1,0:T(8,128)S(1)} collective-permute-done((f32[128,128]{1,0:T(8,128)S(1)}, f32[128,128]{1,0:T(8,128)S(1)}, u32[]{:S(2)}, u32[]{:S(2)}) %collective-permute-start.3) | collective-permute-done | bytes 65568 | tf_op jit(solution)/shard_map/ppermute | solution.py:25
  112.9 1.4 collective-permute-start.4
  114.4 4.8 %collective-permute-done.4 = f32[128,128]{1,0:T(8,128)S(1)} collective-permute-done((f32[128,128]{1,0:T(8,128)S(1)}, f32[128,128]{1,0:T(8,128)S(1)}, u32[]{:S(2)}, u32[]{:S(2)}) %collective-permute-start.4) | collective-permute-done | bytes 65568 | tf_op jit(solution)/shard_map/ppermute | solution.py:25
  119.1 4.7 %collective-permute-start.5 = (f32[128,128]{1,0:T(8,128)S(1)}, f32[128,128]{1,0:T(8,128)S(1)}, u32[]{:S(2)}, u32[]{:S(2)}) collective-permute-start(f32[128,128]{1,0:T(8,128)S(1)} %add.88), channel_id=1, source_target_pairs={{0,32},{8,40},{16,48},{24,56},{32,0},{40,8},{48,16},{56,24},{64,96... | collective-permute-start | bytes 196616 | tf_op jit(solution)/shard_map/ppermute | solution.py:25
  123.8 2.5 %collective-permute-done.5 = f32[128,128]{1,0:T(8,128)S(1)} collective-permute-done((f32[128,128]{1,0:T(8,128)S(1)}, f32[128,128]{1,0:T(8,128)S(1)}, u32[]{:S(2)}, u32[]{:S(2)}) %collective-permute-start.5) | collective-permute-done | bytes 65568 | tf_op jit(solution)/shard_map/ppermute | solution.py:25
  126.3 1.6 collective-permute-start.6
  127.9 0.6 multiply_add_fusion.3.index_ref
  128.5 1.0 collective-permute-done.6
  129.6 3.1 %collective-permute-start.7 = (f32[128,128]{1,0:T(8,128)S(1)}, f32[128,128]{1,0:T(8,128)S(1)}, u32[]{:S(2)}, u32[]{:S(2)}) collective-permute-start(f32[128,128]{1,0:T(8,128)S(1)} %add.90), channel_id=1, source_target_pairs={{0,128},{8,136},{16,144},{24,152},{32,160},{40,168},{48,176},{56,1... | collective-permute-start | bytes 196616 | tf_op jit(solution)/shard_map/ppermute | solution.py:25
  132.7 0.1 copy.21
  132.8 0.1 gt.16
  133.0 0.1 copy.20
  133.1 0.1 eq.105
  133.1 1.6 collective-permute-done.7
  134.8 2.3 bitcast_convert_fusion.source_ref
  137.1 10.1 %shard_map.50 = f32[4096,128]{1,0:T(8,128)} custom-call(s32[4096]{0:T(1024)} %multiply_add_fusion.3.index_ref, f32[8192,128]{1,0:T(8,128)} %bitcast_convert_fusion.source_ref), custom_call_target="tpu_custom_call" | custom-call | tf_op jit(solution)/shard_map/pallas_call | solution.py:42
  147.2 1.7 convert_element_type.94
  148.9 0.4 fusion.69
  149.3 0.6 fusion.67
  149.9 0.1 fusion.76
  150.0 0.4 fusion.65
  150.4 0.3 multiply_reduce_fusion.4
  150.7 0.2 multiply_reduce_fusion.3
  150.9 0.1 convert_bitcast_fusion.1
  151.0 0.6 fusion.63
  151.7 0.1 fusion.77
  151.7 0.4 fusion.61
  152.1 0.3 multiply_reduce_fusion.2
  152.4 0.2 multiply_reduce_fusion.1
  152.6 0.1 convert_bitcast_fusion
  152.7 0.6 fusion.59
  153.4 0.1 fusion.78
  153.5 0.4 fusion.57
  153.9 0.3 fusion.36
  154.2 0.1 multiply_add_fusion
  154.3 1.3 convolution_convert_fusion
  155.6 69.9 %all_to_all.17 = bf16[256,32,128]{2,1,0:T(8,128)(2,1)S(1)} all-to-all(bf16[256,32,128]{2,1,0:T(8,128)(2,1)S(1)} %bitcast.64), channel_id=1, replica_groups=mesh['rows'=32,'grp'=8] {'rows','grp'}, dimensions={0} | all-to-all | bytes 4194304 | tf_op jit(solution)/shard_map/all_to_all | solution.py:16
  225.5 11.0 %fusion = f32[1984,128]{1,0:T(8,128)} fusion(bf16[8192,128]{1,0:T(8,128)(2,1)S(1)} %bitcast.66, s32[8192]{0:T(1024)S(1)} %eq.102), kind=kOutput, calls=%fused_computation.1 | convolution fusion | flops 4177002496 | bytes 3145728 | tf_op jit(solution)/shard_map/st,sk->tk/dot_general | solution.py:146
  (33 shorter events, 0.3 us)
Async XLA Ops:
  0.6 40.0 %copy-start = (bf16[1984,128]{1,0:T(8,128)(2,1)S(1)}, bf16[1984,128]{1,0:T(8,128)(2,1)}, u32[]{:S(2)}) copy-start(bf16[1984,128]{1,0:T(8,128)(2,1)} %param.3) | copy-start | bytes 1523716
  60.1 74.7 %all-to-all-start.1 = ((bf16[256,32,128]{2,1,0:T(8,128)(2,1)}), bf16[256,32,128]{2,1,0:T(8,128)(2,1)S(1)}, u32[]{:S(2)}, u32[]{:S(2)}) async-start(bf16[256,32,128]{2,1,0:T(8,128)(2,1)} %bitcast.65), calls=%async_computation.1 | async-start | bytes 4194304 | tf_op jit(solution)/shard_map/all_to_all | solution.py:16
  66.2 3.3 %collective-permute-start = (f32[128,128]{1,0:T(8,128)S(1)}, f32[128,128]{1,0:T(8,128)S(1)}, u32[]{:S(2)}, u32[]{:S(2)}) collective-permute-start(f32[128,128]{1,0:T(8,128)S(1)} %fusion.89), channel_id=1, source_target_pairs={{0,1},{1,0},{2,3},{3,2},{4,5},{5,4},{6,7},{7,6},{8,9},{9,8},{10,11... | collective-permute-start | bytes 196616 | tf_op jit(solution)/shard_map/ppermute | solution.py:25
  69.5 4.7 %collective-permute-start.1 = (f32[128,128]{1,0:T(8,128)S(1)}, f32[128,128]{1,0:T(8,128)S(1)}, u32[]{:S(2)}, u32[]{:S(2)}) collective-permute-start(f32[128,128]{1,0:T(8,128)S(1)} %add.84), channel_id=1, source_target_pairs={{0,2},{1,3},{2,0},{3,1},{4,6},{5,7},{6,4},{7,5},{8,10},{9,11},{10,... | collective-permute-start | bytes 196616 | tf_op jit(solution)/shard_map/ppermute | solution.py:25
  74.2 6.0 %collective-permute-start.2 = (f32[128,128]{1,0:T(8,128)S(1)}, f32[128,128]{1,0:T(8,128)S(1)}, u32[]{:S(2)}, u32[]{:S(2)}) collective-permute-start(f32[128,128]{1,0:T(8,128)S(1)} %add.85), channel_id=1, source_target_pairs={{0,4},{1,5},{2,6},{3,7},{4,0},{5,1},{6,2},{7,3},{8,12},{9,13},{10,... | collective-permute-start | bytes 196616 | tf_op jit(solution)/shard_map/ppermute | solution.py:25
  80.2 32.8 %collective-permute-start.3 = (f32[128,128]{1,0:T(8,128)S(1)}, f32[128,128]{1,0:T(8,128)S(1)}, u32[]{:S(2)}, u32[]{:S(2)}) collective-permute-start(f32[128,128]{1,0:T(8,128)S(1)} %add.86), channel_id=1, source_target_pairs={{0,8},{8,0},{16,24},{24,16},{32,40},{40,32},{48,56},{56,48},{64,72... | collective-permute-start | bytes 196616 | tf_op jit(solution)/shard_map/ppermute | solution.py:25
  112.9 6.2 %collective-permute-start.4 = (f32[128,128]{1,0:T(8,128)S(1)}, f32[128,128]{1,0:T(8,128)S(1)}, u32[]{:S(2)}, u32[]{:S(2)}) collective-permute-start(f32[128,128]{1,0:T(8,128)S(1)} %add.87), channel_id=1, source_target_pairs={{0,16},{8,24},{16,0},{24,8},{32,48},{40,56},{48,32},{56,40},{64,80... | collective-permute-start | bytes 196616 | tf_op jit(solution)/shard_map/ppermute | solution.py:25
  119.1 7.2 %collective-permute-start.5 = (f32[128,128]{1,0:T(8,128)S(1)}, f32[128,128]{1,0:T(8,128)S(1)}, u32[]{:S(2)}, u32[]{:S(2)}) collective-permute-start(f32[128,128]{1,0:T(8,128)S(1)} %add.88), channel_id=1, source_target_pairs={{0,32},{8,40},{16,48},{24,56},{32,0},{40,8},{48,16},{56,24},{64,96... | collective-permute-start | bytes 196616 | tf_op jit(solution)/shard_map/ppermute | solution.py:25
  126.3 3.2 %collective-permute-start.6 = (f32[128,128]{1,0:T(8,128)S(1)}, f32[128,128]{1,0:T(8,128)S(1)}, u32[]{:S(2)}, u32[]{:S(2)}) collective-permute-start(f32[128,128]{1,0:T(8,128)S(1)} %add.89), channel_id=1, source_target_pairs={{0,64},{8,72},{16,80},{24,88},{32,96},{40,104},{48,112},{56,120},{... | collective-permute-start | bytes 196616 | tf_op jit(solution)/shard_map/ppermute | solution.py:25
  129.6 5.2 %collective-permute-start.7 = (f32[128,128]{1,0:T(8,128)S(1)}, f32[128,128]{1,0:T(8,128)S(1)}, u32[]{:S(2)}, u32[]{:S(2)}) collective-permute-start(f32[128,128]{1,0:T(8,128)S(1)} %add.90), channel_id=1, source_target_pairs={{0,128},{8,136},{16,144},{24,152},{32,160},{40,168},{48,176},{56,1... | collective-permute-start | bytes 196616 | tf_op jit(solution)/shard_map/ppermute | solution.py:25
  147.2 2.8 %copy-start.2 = (s32[64]{0:T(128)S(1)}, s32[64]{0:T(128)}, u32[]{:S(2)}) copy-start(s32[64]{0:T(128)} %param.5) | copy-start | bytes 772
  154.3 71.2 %copy-start.1 = (f32[64,128]{1,0:T(8,128)}, f32[64,128]{1,0:T(8,128)S(1)}, u32[]{:S(2)}) copy-start(f32[64,128]{1,0:T(8,128)S(1)} %multiply_add_fusion) | copy-start | bytes 98308

commit v7 on v6

--- a/solution.py
+++ b/solution.py
@@ -28,11 +28,13 @@
 
 
 def gather_rows_kernel(index_ref, source_ref, out_ref):
-    def body(i, carry):
-        out_ref[pl.ds(i, 1), :] = source_ref[pl.ds(index_ref[i], 1), :]
+    def body(tile, carry):
+        first = pl.multiple_of(tile * 8, 8)
+        rows = [source_ref[pl.ds(index_ref[first + r], 1), :] for r in range(8)]
+        out_ref[pl.ds(first, 8), :] = jnp.concatenate(rows, axis=0)
         return carry
 
-    lax.fori_loop(0, out_ref.shape[0], body, 0, unroll=8)
+    lax.fori_loop(0, out_ref.shape[0] // 8, body, 0, unroll=2)
 
 
 def gather_rows(source, index):
@@ -109,9 +111,7 @@
     slot_index = owners.reshape(lookups) * capacity + ranks
 
     incoming = exchange(requests).reshape(slots_total)
-    table_ids = lax.broadcasted_iota(jnp.int32, (slots_total, table_rows), 1)
-    picks = (incoming[:, None] == table_ids).astype(bf16)
-    answered = jnp.dot(picks, item_table, preferred_element_type=f32).astype(bf16)
+    answered = gather_rows(item_table, incoming)
     reply_rows = exchange(answered.reshape(devices, capacity, embed_width)).reshape(
         slots_total, embed_width
     )
@@ -143,6 +143,8 @@
     partials = jnp.einsum("su,uk->sk", member, solution.astype(bf16), preferred_element_type=f32)
     partials = partials.astype(bf16).reshape(devices, capacity, embed_width)
     arrived = exchange(partials).reshape(slots_total, embed_width)
+    table_ids = lax.broadcasted_iota(jnp.int32, (slots_total, table_rows), 1)
+    picks = (incoming[:, None] == table_ids).astype(bf16)
     item_rhs = jnp.einsum("st,sk->tk", picks, arrived, preferred_element_type=f32)
     return (solution, item_rhs)
 

time: 237 us -> 236 us (level)
  blocking collectives: 98.2 us -> 69.7 us
  matrix products: 41.5 us -> 22.1 us
  starting transfers between devices: 20.4 us -> 36 us
  Pallas kernels: 10.1 us -> 22.9 us
  waiting for transfers between devices: 52.8 us -> 64.7 us
  other arithmetic: 11.1 us -> 15.8 us
    all_to_all x2 -> x1, blocking collectives: 98.2 us -> 69.7 us  [exchange(): return lax.all_to_all(values, ('rows', 'grp'), 0, 0, tiled=True)]
    dot_general x1 -> x0, matrix products: 19.4 us -> none  [on_device(): jnp.dot(picks, item_table, preferred_element_type=f32).astype(bf16)]
    all_to_all x1 -> x2, starting transfers between devices: 5.72 us -> 21.2 us  [exchange(): return lax.all_to_all(values, ('rows', 'grp'), 0, 0, tiled=True)]
    pallas_call x1 -> x2, Pallas kernels: 10.1 us -> 22.9 us  [gather_rows(): pl.pallas_call(gather_rows_kernel, grid_spec=pltpu.PrefetchScalarGridSpec...]
    all_to_all x1 -> x2, waiting for transfers between devices: 0.01 us -> 11.8 us  [exchange(): return lax.all_to_all(values, ('rows', 'grp'), 0, 0, tiled=True)]
    convert_element_type x1 -> x2, other arithmetic: 1.71 us -> 5.43 us  [gather_rows(): return picked.astype(source.dtype)]
  transfers between devices with their start and end apart: 9 -> 10, of which waited for: 8 -> 9; matrix products, arithmetic and copies ran while one was open for 1% -> 1% of each run, Pallas kernels for 0% -> 0%
where the time goes in v7:
time: 236 us; the launch traced here: 235 us
  blocking collectives  69.7 us (30%)
  waiting for transfers between devices  64.7 us (27%)
  starting transfers between devices  36 us (15%)
  Pallas kernels  22.9 us (10%)
  matrix products  22.1 us (9%)
  other arithmetic  15.8 us (7%)
  local copies, waits for them, and re-layouts  2.82 us (1%)
    all_to_all x1, blocking collectives, exchange(): return lax.all_to_all(values, ('rows', 'grp'), 0, 0, tiled=True)  69.7 us
    ppermute x8, waiting for transfers between devices, sum_over_devices(): value = value + lax.ppermute(value, axis, partners)  53 us
    pallas_call x2, Pallas kernels, gather_rows(): pl.pallas_call(gather_rows_kernel, grid_spec=pltpu.PrefetchScalarGridSpec...  22.9 us
    all_to_all x2, starting transfers between devices, exchange(): return lax.all_to_all(values, ('rows', 'grp'), 0, 0, tiled=True)  21.2 us
    ppermute x8, starting transfers between devices, sum_over_devices(): value = value + lax.ppermute(value, axis, partners)  14.8 us
    all_to_all x2, waiting for transfers between devices, exchange(): return lax.all_to_all(values, ('rows', 'grp'), 0, 0, tiled=True)  11.8 us
    dot_general x1, matrix products, on_device(): jnp.einsum('st,sk->tk', picks, arrived, preferred_element_type=f32)  11 us
    convert_element_type x2, other arithmetic, gather_rows(): return picked.astype(source.dtype)  5.43 us
  transfers between devices with their start and end apart: 10, of which 9 were waited for; matrix products, arithmetic and copies ran while one was open for 1% of the time, Pallas kernels for 0%

profile of v7, /device:TPU:1, one launch (start us, length us, event | category | flops | bytes accessed | tf_op | source)
XLA Modules:
  0.0 234.9 jit_solution(6864873766575677283)
XLA Ops:
  0.7 0.7 fusion.72
  1.4 0.1 lt.34
  1.5 0.8 multiply_subtract_fusion.2
  2.4 1.4 fusion.53
  3.8 1.4 fusion.5
  5.4 0.1 fusion.25
  5.6 3.2 %multiply_reduce_fusion = f32[64,64]{1,0:T(8,128)S(1)} fusion(f32[64,65]{1,0:T(8,128)S(1)} %fusion.70, bf16[64,1,256]{2,1,0:T(2,128)(2,1)S(1)} %copy.18, bf16[64,64,256]{2,1,0:T(8,128)(2,1)S(1)} %fusion.5, s32[64,64]{1,0:T(8,128)S(1)} %get-tuple-element.13, pred[64,64]{1,0:T(8,128)(4,1)S(1)} %get-tuple-element.17), kind=kOutput, calls=%fused_computation.25 | convolution fusion | flops 143200256 | bytes 2183424 | tf_op jit(solution)/shard_map/ujo,uko->ujk/dot_general | solution.py:85
  8.9 1.7 fusion.22
  10.6 0.7 copy.19
  11.4 15.7 %all-to-all-start = ((s32[256,1,32]{2,1,0:T(1,128)}), s32[256,1,32]{2,1,0:T(1,128)S(1)}, u32[]{:S(2)}, u32[]{:S(2)}) async-start(s32[256,1,32]{2,1,0:T(1,128)} %copy.19), calls=%async_computation | async-start | bytes 262144 | tf_op jit(solution)/shard_map/all_to_all | solution.py:16
  27.1 1.0 convert_element_type.94.source_ref
  28.1 11.8 %all-to-all-done = s32[256,1,32]{2,1,0:T(1,128)S(1)} async-done(((s32[256,1,32]{2,1,0:T(1,128)}), s32[256,1,32]{2,1,0:T(1,128)S(1)}, u32[]{:S(2)}, u32[]{:S(2)}) %all-to-all-start) | async-done | bytes 32800 | tf_op jit(solution)/shard_map/all_to_all | solution.py:16
  39.8 0.5 broadcast.323
  40.4 1.0 reduce.4
  41.3 0.7 reshape.323.index_ref
  42.0 13.8 %shard_map.50 = f32[8192,128]{1,0:T(8,128)} custom-call(s32[8192]{0:T(1024)} %reshape.323.index_ref, f32[1984,128]{1,0:T(8,128)} %convert_element_type.94.source_ref), custom_call_target="tpu_custom_call" | custom-call | tf_op jit(solution)/shard_map/pallas_call | solution.py:44
  55.8 3.7 %convert_element_type.95 = bf16[8192,128]{1,0:T(8,128)(2,1)} convert(f32[8192,128]{1,0:T(8,128)} %shard_map.50) | non-fusion elementwise | flops 1048576 | bytes 6291456 | tf_op jit(solution)/shard_map/convert_element_type | solution.py:54
  59.5 5.6 %all-to-all-start.1 = ((bf16[256,32,128]{2,1,0:T(8,128)(2,1)}), bf16[256,32,128]{2,1,0:T(8,128)(2,1)S(1)}, u32[]{:S(2)}, u32[]{:S(2)}) async-start(bf16[256,32,128]{2,1,0:T(8,128)(2,1)} %bitcast.63), calls=%async_computation.1 | async-start | bytes 4194304 | tf_op jit(solution)/shard_map/all_to_all | solution.py:16
  65.1 0.3 fusion.86
  65.4 2.4 %collective-permute-start = (f32[128,128]{1,0:T(8,128)S(1)}, f32[128,128]{1,0:T(8,128)S(1)}, u32[]{:S(2)}, u32[]{:S(2)}) collective-permute-start(f32[128,128]{1,0:T(8,128)S(1)} %fusion.86), channel_id=1, source_target_pairs={{0,1},{1,0},{2,3},{3,2},{4,5},{5,4},{6,7},{7,6},{8,9},{9,8},{10,11... | collective-permute-start | bytes 196616 | tf_op jit(solution)/shard_map/ppermute | solution.py:25
  67.8 0.9 collective-permute-done
  68.7 0.1 collective-permute-start.1
  68.8 4.6 %collective-permute-done.1 = f32[128,128]{1,0:T(8,128)S(1)} collective-permute-done((f32[128,128]{1,0:T(8,128)S(1)}, f32[128,128]{1,0:T(8,128)S(1)}, u32[]{:S(2)}, u32[]{:S(2)}) %collective-permute-start.1) | collective-permute-done | bytes 65568 | tf_op jit(solution)/shard_map/ppermute | solution.py:25
  73.4 1.3 collective-permute-start.2
  74.6 4.7 %collective-permute-done.2 = f32[128,128]{1,0:T(8,128)S(1)} collective-permute-done((f32[128,128]{1,0:T(8,128)S(1)}, f32[128,128]{1,0:T(8,128)S(1)}, u32[]{:S(2)}, u32[]{:S(2)}) %collective-permute-start.2) | collective-permute-done | bytes 65568 | tf_op jit(solution)/shard_map/ppermute | solution.py:25
  79.4 0.1 collective-permute-start.3
  79.5 32.7 %collective-permute-done.3 = f32[128,128]{1,0:T(8,128)S(1)} collective-permute-done((f32[128,128]{1,0:T(8,128)S(1)}, f32[128,128]{1,0:T(8,128)S(1)}, u32[]{:S(2)}, u32[]{:S(2)}) %collective-permute-start.3) | collective-permute-done | bytes 65568 | tf_op jit(solution)/shard_map/ppermute | solution.py:25
  112.2 1.4 collective-permute-start.4
  113.6 4.8 %collective-permute-done.4 = f32[128,128]{1,0:T(8,128)S(1)} collective-permute-done((f32[128,128]{1,0:T(8,128)S(1)}, f32[128,128]{1,0:T(8,128)S(1)}, u32[]{:S(2)}, u32[]{:S(2)}) %collective-permute-start.4) | collective-permute-done | bytes 65568 | tf_op jit(solution)/shard_map/ppermute | solution.py:25
  118.4 4.7 %collective-permute-start.5 = (f32[128,128]{1,0:T(8,128)S(1)}, f32[128,128]{1,0:T(8,128)S(1)}, u32[]{:S(2)}, u32[]{:S(2)}) collective-permute-start(f32[128,128]{1,0:T(8,128)S(1)} %add.88), channel_id=1, source_target_pairs={{0,32},{8,40},{16,48},{24,56},{32,0},{40,8},{48,16},{56,24},{64,96... | collective-permute-start | bytes 196616 | tf_op jit(solution)/shard_map/ppermute | solution.py:25
  123.0 2.5 %collective-permute-done.5 = f32[128,128]{1,0:T(8,128)S(1)} collective-permute-done((f32[128,128]{1,0:T(8,128)S(1)}, f32[128,128]{1,0:T(8,128)S(1)}, u32[]{:S(2)}, u32[]{:S(2)}) %collective-permute-start.5) | collective-permute-done | bytes 65568 | tf_op jit(solution)/shard_map/ppermute | solution.py:25
  125.5 1.6 collective-permute-start.6
  127.1 0.6 multiply_add_fusion.3.index_ref
  127.7 1.0 collective-permute-done.6
  128.8 3.3 %collective-permute-start.7 = (f32[128,128]{1,0:T(8,128)S(1)}, f32[128,128]{1,0:T(8,128)S(1)}, u32[]{:S(2)}, u32[]{:S(2)}) collective-permute-start(f32[128,128]{1,0:T(8,128)S(1)} %add.90), channel_id=1, source_target_pairs={{0,128},{8,136},{16,144},{24,152},{32,160},{40,168},{48,176},{56,1... | collective-permute-start | bytes 196616 | tf_op jit(solution)/shard_map/ppermute | solution.py:25
  132.1 0.1 copy.21
  132.2 0.1 gt.16
  132.4 0.1 copy.20
  132.5 0.1 eq.102
  132.6 1.8 collective-permute-done.7
  134.4 2.3 bitcast_convert_fusion.source_ref
  136.7 9.1 %shard_map.51 = f32[4096,128]{1,0:T(8,128)} custom-call(s32[4096]{0:T(1024)} %multiply_add_fusion.3.index_ref, f32[8192,128]{1,0:T(8,128)} %bitcast_convert_fusion.source_ref), custom_call_target="tpu_custom_call" | custom-call | tf_op jit(solution)/shard_map/pallas_call | solution.py:44
  145.8 1.7 convert_element_type.98
  147.5 0.4 fusion.66
  147.9 0.6 fusion.64
  148.6 0.1 fusion.73
  148.7 0.4 fusion.62
  149.1 0.3 multiply_reduce_fusion.4
  149.4 0.2 multiply_reduce_fusion.3
  149.6 0.1 convert_bitcast_fusion.1
  149.7 0.6 fusion.60
  150.3 0.1 fusion.74
  150.4 0.4 fusion.58
  150.8 0.3 multiply_reduce_fusion.2
  151.1 0.2 multiply_reduce_fusion.1
  151.3 0.1 convert_bitcast_fusion
  151.4 0.6 fusion.56
  152.0 0.1 fusion.75
  152.1 0.4 fusion.54
  152.5 0.3 fusion.33
  152.8 0.1 multiply_add_fusion
  152.9 1.3 convolution_convert_fusion
  154.2 69.7 %all_to_all.16 = bf16[256,32,128]{2,1,0:T(8,128)(2,1)S(1)} all-to-all(bf16[256,32,128]{2,1,0:T(8,128)(2,1)S(1)} %bitcast.64), channel_id=1, replica_groups=mesh['rows'=32,'grp'=8] {'rows','grp'}, dimensions={0} | all-to-all | bytes 4194304 | tf_op jit(solution)/shard_map/all_to_all | solution.py:16
  223.9 11.0 %fusion = f32[1984,128]{1,0:T(8,128)} fusion(bf16[8192,128]{1,0:T(8,128)(2,1)S(1)} %bitcast.65, s32[8192]{0:T(1024)S(1)} %copy-done.1), kind=kOutput, calls=%fused_computation.1 | convolution fusion | flops 4177002496 | bytes 3145728 | tf_op jit(solution)/shard_map/st,sk->tk/dot_general | solution.py:148
  (38 shorter events, 0.6 us)
Async XLA Ops:
  8.9 18.1 %copy-start = (bf16[1984,128]{1,0:T(8,128)(2,1)S(1)}, bf16[1984,128]{1,0:T(8,128)(2,1)}, u32[]{:S(2)}) copy-start(bf16[1984,128]{1,0:T(8,128)(2,1)} %param.3) | copy-start | bytes 1523716
  11.4 28.5 %all-to-all-start = ((s32[256,1,32]{2,1,0:T(1,128)}), s32[256,1,32]{2,1,0:T(1,128)S(1)}, u32[]{:S(2)}, u32[]{:S(2)}) async-start(s32[256,1,32]{2,1,0:T(1,128)} %copy.19), calls=%async_computation | async-start | bytes 262144 | tf_op jit(solution)/shard_map/all_to_all | solution.py:16
  59.5 74.9 %all-to-all-start.1 = ((bf16[256,32,128]{2,1,0:T(8,128)(2,1)}), bf16[256,32,128]{2,1,0:T(8,128)(2,1)S(1)}, u32[]{:S(2)}, u32[]{:S(2)}) async-start(bf16[256,32,128]{2,1,0:T(8,128)(2,1)} %bitcast.63), calls=%async_computation.1 | async-start | bytes 4194304 | tf_op jit(solution)/shard_map/all_to_all | solution.py:16
  65.4 3.3 %collective-permute-start = (f32[128,128]{1,0:T(8,128)S(1)}, f32[128,128]{1,0:T(8,128)S(1)}, u32[]{:S(2)}, u32[]{:S(2)}) collective-permute-start(f32[128,128]{1,0:T(8,128)S(1)} %fusion.86), channel_id=1, source_target_pairs={{0,1},{1,0},{2,3},{3,2},{4,5},{5,4},{6,7},{7,6},{8,9},{9,8},{10,11... | collective-permute-start | bytes 196616 | tf_op jit(solution)/shard_map/ppermute | solution.py:25
  68.7 4.7 %collective-permute-start.1 = (f32[128,128]{1,0:T(8,128)S(1)}, f32[128,128]{1,0:T(8,128)S(1)}, u32[]{:S(2)}, u32[]{:S(2)}) collective-permute-start(f32[128,128]{1,0:T(8,128)S(1)} %add.84), channel_id=1, source_target_pairs={{0,2},{1,3},{2,0},{3,1},{4,6},{5,7},{6,4},{7,5},{8,10},{9,11},{10,... | collective-permute-start | bytes 196616 | tf_op jit(solution)/shard_map/ppermute | solution.py:25
  73.4 6.0 %collective-permute-start.2 = (f32[128,128]{1,0:T(8,128)S(1)}, f32[128,128]{1,0:T(8,128)S(1)}, u32[]{:S(2)}, u32[]{:S(2)}) collective-permute-start(f32[128,128]{1,0:T(8,128)S(1)} %add.85), channel_id=1, source_target_pairs={{0,4},{1,5},{2,6},{3,7},{4,0},{5,1},{6,2},{7,3},{8,12},{9,13},{10,... | collective-permute-start | bytes 196616 | tf_op jit(solution)/shard_map/ppermute | solution.py:25
  79.4 32.8 %collective-permute-start.3 = (f32[128,128]{1,0:T(8,128)S(1)}, f32[128,128]{1,0:T(8,128)S(1)}, u32[]{:S(2)}, u32[]{:S(2)}) collective-permute-start(f32[128,128]{1,0:T(8,128)S(1)} %add.86), channel_id=1, source_target_pairs={{0,8},{8,0},{16,24},{24,16},{32,40},{40,32},{48,56},{56,48},{64,72... | collective-permute-start | bytes 196616 | tf_op jit(solution)/shard_map/ppermute | solution.py:25
  112.2 6.2 %collective-permute-start.4 = (f32[128,128]{1,0:T(8,128)S(1)}, f32[128,128]{1,0:T(8,128)S(1)}, u32[]{:S(2)}, u32[]{:S(2)}) collective-permute-start(f32[128,128]{1,0:T(8,128)S(1)} %add.87), channel_id=1, source_target_pairs={{0,16},{8,24},{16,0},{24,8},{32,48},{40,56},{48,32},{56,40},{64,80... | collective-permute-start | bytes 196616 | tf_op jit(solution)/shard_map/ppermute | solution.py:25
  118.4 7.2 %collective-permute-start.5 = (f32[128,128]{1,0:T(8,128)S(1)}, f32[128,128]{1,0:T(8,128)S(1)}, u32[]{:S(2)}, u32[]{:S(2)}) collective-permute-start(f32[128,128]{1,0:T(8,128)S(1)} %add.88), channel_id=1, source_target_pairs={{0,32},{8,40},{16,48},{24,56},{32,0},{40,8},{48,16},{56,24},{64,96... | collective-permute-start | bytes 196616 | tf_op jit(solution)/shard_map/ppermute | solution.py:25
  125.5 3.2 %collective-permute-start.6 = (f32[128,128]{1,0:T(8,128)S(1)}, f32[128,128]{1,0:T(8,128)S(1)}, u32[]{:S(2)}, u32[]{:S(2)}) collective-permute-start(f32[128,128]{1,0:T(8,128)S(1)} %add.89), channel_id=1, source_target_pairs={{0,64},{8,72},{16,80},{24,88},{32,96},{40,104},{48,112},{56,120},{... | collective-permute-start | bytes 196616 | tf_op jit(solution)/shard_map/ppermute | solution.py:25
  128.8 5.5 %collective-permute-start.7 = (f32[128,128]{1,0:T(8,128)S(1)}, f32[128,128]{1,0:T(8,128)S(1)}, u32[]{:S(2)}, u32[]{:S(2)}) collective-permute-start(f32[128,128]{1,0:T(8,128)S(1)} %add.90), channel_id=1, source_target_pairs={{0,128},{8,136},{16,144},{24,152},{32,160},{40,168},{48,176},{56,1... | collective-permute-start | bytes 196616 | tf_op jit(solution)/shard_map/ppermute | solution.py:25
  145.8 2.8 %copy-start.3 = (s32[64]{0:T(128)S(1)}, s32[64]{0:T(128)}, u32[]{:S(2)}) copy-start(s32[64]{0:T(128)} %param.5) | copy-start | bytes 772
  152.9 71.0 %copy-start.2 = (f32[64,128]{1,0:T(8,128)}, f32[64,128]{1,0:T(8,128)S(1)}, u32[]{:S(2)}) copy-start(f32[64,128]{1,0:T(8,128)S(1)} %multiply_add_fusion) | copy-start | bytes 98308
  154.2 69.7 %copy-start.1 = (s32[8192]{0:T(1024)S(1)}, s32[8192]{0:T(1024)}, u32[]{:S(2)}) copy-start(s32[8192]{0:T(1024)} %reshape.323.index_ref) | copy-start | bytes 98308

commit v8 on v7

--- a/solution.py
+++ b/solution.py
@@ -27,14 +27,17 @@
     return value
 
 
+GATHER_TILE = 16
+
+
 def gather_rows_kernel(index_ref, source_ref, out_ref):
     def body(tile, carry):
-        first = pl.multiple_of(tile * 8, 8)
-        rows = [source_ref[pl.ds(index_ref[first + r], 1), :] for r in range(8)]
-        out_ref[pl.ds(first, 8), :] = jnp.concatenate(rows, axis=0)
+        first = pl.multiple_of(tile * GATHER_TILE, GATHER_TILE)
+        rows = [source_ref[pl.ds(index_ref[first + r], 1), :] for r in range(GATHER_TILE)]
+        out_ref[pl.ds(first, GATHER_TILE), :] = jnp.concatenate(rows, axis=0).astype(out_ref.dtype)
         return carry
 
-    lax.fori_loop(0, out_ref.shape[0] // 8, body, 0, unroll=2)
+    lax.fori_loop(0, out_ref.shape[0] // GATHER_TILE, body, 0)
 
 
 def gather_rows(source, index):
@@ -49,9 +52,9 @@
             in_specs=[pl.BlockSpec((rows, width), lambda i, index_ref: (0, 0))],
             out_specs=pl.BlockSpec((count, width), lambda i, index_ref: (0, 0)),
         ),
-        out_shape=jax.ShapeDtypeStruct((count, width), jnp.float32),
+        out_shape=jax.ShapeDtypeStruct((count, width), source.dtype),
     )(index, wide)
-    return picked.astype(source.dtype)
+    return picked
 
 
 def on_device(item_table, histories, counts):

time: 236 us -> 232 us (0.983)
  other arithmetic: 15.8 us -> 10.4 us
  matrix products: 22.1 us -> 24.6 us
    convert_element_type x2 -> x0, other arithmetic: 5.43 us -> none  [gather_rows(): return picked.astype(source.dtype)]
where the time goes in v8:
time: 232 us; the launch traced here: 231 us
  blocking collectives  69.7 us (30%)
  waiting for transfers between devices  64.7 us (28%)
  starting transfers between devices  36 us (16%)
  matrix products  24.6 us (11%)
  Pallas kernels  22 us (9%)
  other arithmetic  10.4 us (4%)
  local copies, waits for them, and re-layouts  2.87 us (1%)
    all_to_all x1, blocking collectives, exchange(): return lax.all_to_all(values, ('rows', 'grp'), 0, 0, tiled=True)  69.7 us
    ppermute x8, waiting for transfers between devices, sum_over_devices(): value = value + lax.ppermute(value, axis, partners)  53 us
    pallas_call x2, Pallas kernels, gather_rows(): pl.pallas_call(gather_rows_kernel, grid_spec=pltpu.PrefetchScalarGridSpec...  22 us
    all_to_all x2, starting transfers between devices, exchange(): return lax.all_to_all(values, ('rows', 'grp'), 0, 0, tiled=True)  21.2 us
    ppermute x8, starting transfers between devices, sum_over_devices(): value = value + lax.ppermute(value, axis, partners)  14.8 us
    all_to_all x2, waiting for transfers between devices, exchange(): return lax.all_to_all(values, ('rows', 'grp'), 0, 0, tiled=True)  11.8 us
    dot_general x1, matrix products, on_device(): jnp.einsum('st,sk->tk', picks, arrived, preferred_element_type=f32)  11 us
  transfers between devices with their start and end apart: 10, of which 9 were waited for; matrix products, arithmetic and copies ran while one was open for 1% of the time, Pallas kernels for 0%

profile of v8, /device:TPU:1, one launch (start us, length us, event | category | flops | bytes accessed | tf_op | source)
XLA Modules:
  0.0 231.1 jit_solution(1969372773374203501)
XLA Ops:
  0.7 0.7 fusion.72
  1.4 0.1 lt.34
  1.5 0.8 multiply_subtract_fusion.2
  2.3 0.1 reshape.321
  2.4 1.4 fusion.53
  3.8 1.4 fusion.5
  5.2 0.1 broadcast_in_dim.44
  5.4 0.1 fusion.25
  5.6 3.2 %multiply_reduce_fusion = f32[64,64]{1,0:T(8,128)S(1)} fusion(f32[64,65]{1,0:T(8,128)S(1)} %fusion.70, bf16[64,1,256]{2,1,0:T(2,128)(2,1)S(1)} %copy.18, bf16[64,64,256]{2,1,0:T(8,128)(2,1)S(1)} %fusion.5, s32[64,64]{1,0:T(8,128)S(1)} %get-tuple-element.13, pred[64,64]{1,0:T(8,128)(4,1)S(1)} %get-tuple-element.17), kind=kOutput, calls=%fused_computation.25 | convolution fusion | flops 143200256 | bytes 2183424 | tf_op jit(solution)/shard_map/ujo,uko->ujk/dot_general | solution.py:88
  8.9 1.7 fusion.22
  10.6 0.8 copy.19
  11.4 15.7 %all-to-all-start = ((s32[256,1,32]{2,1,0:T(1,128)}), s32[256,1,32]{2,1,0:T(1,128)S(1)}, u32[]{:S(2)}, u32[]{:S(2)}) async-start(s32[256,1,32]{2,1,0:T(1,128)} %copy.19), calls=%async_computation | async-start | bytes 262144 | tf_op jit(solution)/shard_map/all_to_all | solution.py:16
  27.1 1.0 convert_element_type.88.source_ref
  28.1 11.8 %all-to-all-done = s32[256,1,32]{2,1,0:T(1,128)S(1)} async-done(((s32[256,1,32]{2,1,0:T(1,128)}), s32[256,1,32]{2,1,0:T(1,128)S(1)}, u32[]{:S(2)}, u32[]{:S(2)}) %all-to-all-start) | async-done | bytes 32800 | tf_op jit(solution)/shard_map/all_to_all | solution.py:16
  39.9 0.5 broadcast.323
  40.4 1.0 reduce.4
  41.3 0.7 reshape.323.index_ref
  42.0 13.2 %shard_map.50 = bf16[8192,128]{1,0:T(8,128)(2,1)} custom-call(s32[8192]{0:T(1024)} %reshape.323.index_ref, f32[1984,128]{1,0:T(8,128)} %convert_element_type.88.source_ref), custom_call_target="tpu_custom_call" | custom-call | tf_op jit(solution)/shard_map/pallas_call | solution.py:47
  55.2 5.5 %all-to-all-start.1 = ((bf16[256,32,128]{2,1,0:T(8,128)(2,1)}), bf16[256,32,128]{2,1,0:T(8,128)(2,1)S(1)}, u32[]{:S(2)}, u32[]{:S(2)}) async-start(bf16[256,32,128]{2,1,0:T(8,128)(2,1)} %bitcast.63), calls=%async_computation.1 | async-start | bytes 4194304 | tf_op jit(solution)/shard_map/all_to_all | solution.py:16
  60.8 0.3 fusion.86
  61.1 2.4 %collective-permute-start = (f32[128,128]{1,0:T(8,128)S(1)}, f32[128,128]{1,0:T(8,128)S(1)}, u32[]{:S(2)}, u32[]{:S(2)}) collective-permute-start(f32[128,128]{1,0:T(8,128)S(1)} %fusion.86), channel_id=1, source_target_pairs={{0,1},{1,0},{2,3},{3,2},{4,5},{5,4},{6,7},{7,6},{8,9},{9,8},{10,11... | collective-permute-start | bytes 196616 | tf_op jit(solution)/shard_map/ppermute | solution.py:25
  63.5 0.9 collective-permute-done
  64.4 0.1 collective-permute-start.1
  64.5 4.6 %collective-permute-done.1 = f32[128,128]{1,0:T(8,128)S(1)} collective-permute-done((f32[128,128]{1,0:T(8,128)S(1)}, f32[128,128]{1,0:T(8,128)S(1)}, u32[]{:S(2)}, u32[]{:S(2)}) %collective-permute-start.1) | collective-permute-done | bytes 65568 | tf_op jit(solution)/shard_map/ppermute | solution.py:25
  69.1 1.2 collective-permute-start.2
  70.3 4.8 %collective-permute-done.2 = f32[128,128]{1,0:T(8,128)S(1)} collective-permute-done((f32[128,128]{1,0:T(8,128)S(1)}, f32[128,128]{1,0:T(8,128)S(1)}, u32[]{:S(2)}, u32[]{:S(2)}) %collective-permute-start.2) | collective-permute-done | bytes 65568 | tf_op jit(solution)/shard_map/ppermute | solution.py:25
  75.1 0.1 collective-permute-start.3
  75.2 32.7 %collective-permute-done.3 = f32[128,128]{1,0:T(8,128)S(1)} collective-permute-done((f32[128,128]{1,0:T(8,128)S(1)}, f32[128,128]{1,0:T(8,128)S(1)}, u32[]{:S(2)}, u32[]{:S(2)}) %collective-permute-start.3) | collective-permute-done | bytes 65568 | tf_op jit(solution)/shard_map/ppermute | solution.py:25
  107.9 1.4 collective-permute-start.4
  109.3 4.8 %collective-permute-done.4 = f32[128,128]{1,0:T(8,128)S(1)} collective-permute-done((f32[128,128]{1,0:T(8,128)S(1)}, f32[128,128]{1,0:T(8,128)S(1)}, u32[]{:S(2)}, u32[]{:S(2)}) %collective-permute-start.4) | collective-permute-done | bytes 65568 | tf_op jit(solution)/shard_map/ppermute | solution.py:25
  114.1 4.7 %collective-permute-start.5 = (f32[128,128]{1,0:T(8,128)S(1)}, f32[128,128]{1,0:T(8,128)S(1)}, u32[]{:S(2)}, u32[]{:S(2)}) collective-permute-start(f32[128,128]{1,0:T(8,128)S(1)} %add.88), channel_id=1, source_target_pairs={{0,32},{8,40},{16,48},{24,56},{32,0},{40,8},{48,16},{56,24},{64,96... | collective-permute-start | bytes 196616 | tf_op jit(solution)/shard_map/ppermute | solution.py:25
  118.7 2.5 %collective-permute-done.5 = f32[128,128]{1,0:T(8,128)S(1)} collective-permute-done((f32[128,128]{1,0:T(8,128)S(1)}, f32[128,128]{1,0:T(8,128)S(1)}, u32[]{:S(2)}, u32[]{:S(2)}) %collective-permute-start.5) | collective-permute-done | bytes 65568 | tf_op jit(solution)/shard_map/ppermute | solution.py:25
  121.3 1.6 collective-permute-start.6
  122.8 0.6 multiply_add_fusion.3.index_ref
  123.5 1.0 collective-permute-done.6
  124.5 3.3 %collective-permute-start.7 = (f32[128,128]{1,0:T(8,128)S(1)}, f32[128,128]{1,0:T(8,128)S(1)}, u32[]{:S(2)}, u32[]{:S(2)}) collective-permute-start(f32[128,128]{1,0:T(8,128)S(1)} %add.90), channel_id=1, source_target_pairs={{0,128},{8,136},{16,144},{24,152},{32,160},{40,168},{48,176},{56,1... | collective-permute-start | bytes 196616 | tf_op jit(solution)/shard_map/ppermute | solution.py:25
  127.8 0.1 copy.21
  128.0 0.1 gt.16
  128.1 0.1 copy.20
  128.2 0.1 eq.102
  128.3 1.8 collective-permute-done.7
  130.1 2.3 %bitcast_convert_fusion.source_ref = f32[8192,128]{1,0:T(8,128)} fusion(bf16[256,32,128]{2,1,0:T(8,128)(2,1)S(1)} %all-to-all-done.1), kind=kLoop, calls=%fused_computation.21 | loop fusion | flops 1048576 | bytes 6291456 | tf_op jit(solution)/shard_map/convert_element_type | solution.py:46
  132.4 8.8 %shard_map.51 = bf16[4096,128]{1,0:T(8,128)(2,1)} custom-call(s32[4096]{0:T(1024)} %multiply_add_fusion.3.index_ref, f32[8192,128]{1,0:T(8,128)} %bitcast_convert_fusion.source_ref), custom_call_target="tpu_custom_call" | custom-call | tf_op jit(solution)/shard_map/pallas_call | solution.py:47
  141.2 1.7 fusion.66
  142.9 1.9 fusion.64
  144.8 0.1 fusion.73
  144.9 0.4 fusion.62
  145.2 0.3 multiply_reduce_fusion.4
  145.6 0.2 multiply_reduce_fusion.3
  145.8 0.1 convert_bitcast_fusion.1
  145.9 0.6 fusion.60
  146.5 0.1 fusion.74
  146.6 0.4 fusion.58
  147.0 0.3 multiply_reduce_fusion.2
  147.3 0.2 multiply_reduce_fusion.1
  147.5 0.1 convert_bitcast_fusion
  147.6 0.6 fusion.56
  148.2 0.1 fusion.75
  148.3 0.4 fusion.54
  148.7 0.3 fusion.33
  149.0 0.1 multiply_add_fusion
  149.1 1.3 convolution_convert_fusion
  150.4 69.7 %all_to_all.16 = bf16[256,32,128]{2,1,0:T(8,128)(2,1)S(1)} all-to-all(bf16[256,32,128]{2,1,0:T(8,128)(2,1)S(1)} %bitcast.64), channel_id=1, replica_groups=mesh['rows'=32,'grp'=8] {'rows','grp'}, dimensions={0} | all-to-all | bytes 4194304 | tf_op jit(solution)/shard_map/all_to_all | solution.py:16
  220.1 11.0 %fusion = f32[1984,128]{1,0:T(8,128)} fusion(bf16[8192,128]{1,0:T(8,128)(2,1)S(1)} %bitcast.65, s32[8192]{0:T(1024)S(1)} %copy-done.2), kind=kOutput, calls=%fused_computation.1 | convolution fusion | flops 4177002496 | bytes 3145728 | tf_op jit(solution)/shard_map/st,sk->tk/dot_general | solution.py:151
  (38 shorter events, 0.4 us)
Async XLA Ops:
  8.9 18.1 %copy-start = (bf16[1984,128]{1,0:T(8,128)(2,1)S(1)}, bf16[1984,128]{1,0:T(8,128)(2,1)}, u32[]{:S(2)}) copy-start(bf16[1984,128]{1,0:T(8,128)(2,1)} %param.3) | copy-start | bytes 1523716
  11.4 28.5 %all-to-all-start = ((s32[256,1,32]{2,1,0:T(1,128)}), s32[256,1,32]{2,1,0:T(1,128)S(1)}, u32[]{:S(2)}, u32[]{:S(2)}) async-start(s32[256,1,32]{2,1,0:T(1,128)} %copy.19), calls=%async_computation | async-start | bytes 262144 | tf_op jit(solution)/shard_map/all_to_all | solution.py:16
  55.2 74.8 %all-to-all-start.1 = ((bf16[256,32,128]{2,1,0:T(8,128)(2,1)}), bf16[256,32,128]{2,1,0:T(8,128)(2,1)S(1)}, u32[]{:S(2)}, u32[]{:S(2)}) async-start(bf16[256,32,128]{2,1,0:T(8,128)(2,1)} %bitcast.63), calls=%async_computation.1 | async-start | bytes 4194304 | tf_op jit(solution)/shard_map/all_to_all | solution.py:16
  61.1 3.3 %collective-permute-start = (f32[128,128]{1,0:T(8,128)S(1)}, f32[128,128]{1,0:T(8,128)S(1)}, u32[]{:S(2)}, u32[]{:S(2)}) collective-permute-start(f32[128,128]{1,0:T(8,128)S(1)} %fusion.86), channel_id=1, source_target_pairs={{0,1},{1,0},{2,3},{3,2},{4,5},{5,4},{6,7},{7,6},{8,9},{9,8},{10,11... | collective-permute-start | bytes 196616 | tf_op jit(solution)/shard_map/ppermute | solution.py:25
  64.4 4.7 %collective-permute-start.1 = (f32[128,128]{1,0:T(8,128)S(1)}, f32[128,128]{1,0:T(8,128)S(1)}, u32[]{:S(2)}, u32[]{:S(2)}) collective-permute-start(f32[128,128]{1,0:T(8,128)S(1)} %add.84), channel_id=1, source_target_pairs={{0,2},{1,3},{2,0},{3,1},{4,6},{5,7},{6,4},{7,5},{8,10},{9,11},{10,... | collective-permute-start | bytes 196616 | tf_op jit(solution)/shard_map/ppermute | solution.py:25
  69.1 6.0 %collective-permute-start.2 = (f32[128,128]{1,0:T(8,128)S(1)}, f32[128,128]{1,0:T(8,128)S(1)}, u32[]{:S(2)}, u32[]{:S(2)}) collective-permute-start(f32[128,128]{1,0:T(8,128)S(1)} %add.85), channel_id=1, source_target_pairs={{0,4},{1,5},{2,6},{3,7},{4,0},{5,1},{6,2},{7,3},{8,12},{9,13},{10,... | collective-permute-start | bytes 196616 | tf_op jit(solution)/shard_map/ppermute | solution.py:25
  75.1 32.8 %collective-permute-start.3 = (f32[128,128]{1,0:T(8,128)S(1)}, f32[128,128]{1,0:T(8,128)S(1)}, u32[]{:S(2)}, u32[]{:S(2)}) collective-permute-start(f32[128,128]{1,0:T(8,128)S(1)} %add.86), channel_id=1, source_target_pairs={{0,8},{8,0},{16,24},{24,16},{32,40},{40,32},{48,56},{56,48},{64,72... | collective-permute-start | bytes 196616 | tf_op jit(solution)/shard_map/ppermute | solution.py:25
  107.9 6.2 %collective-permute-start.4 = (f32[128,128]{1,0:T(8,128)S(1)}, f32[128,128]{1,0:T(8,128)S(1)}, u32[]{:S(2)}, u32[]{:S(2)}) collective-permute-start(f32[128,128]{1,0:T(8,128)S(1)} %add.87), channel_id=1, source_target_pairs={{0,16},{8,24},{16,0},{24,8},{32,48},{40,56},{48,32},{56,40},{64,80... | collective-permute-start | bytes 196616 | tf_op jit(solution)/shard_map/ppermute | solution.py:25
  114.1 7.2 %collective-permute-start.5 = (f32[128,128]{1,0:T(8,128)S(1)}, f32[128,128]{1,0:T(8,128)S(1)}, u32[]{:S(2)}, u32[]{:S(2)}) collective-permute-start(f32[128,128]{1,0:T(8,128)S(1)} %add.88), channel_id=1, source_target_pairs={{0,32},{8,40},{16,48},{24,56},{32,0},{40,8},{48,16},{56,24},{64,96... | collective-permute-start | bytes 196616 | tf_op jit(solution)/shard_map/ppermute | solution.py:25
  121.3 3.2 %collective-permute-start.6 = (f32[128,128]{1,0:T(8,128)S(1)}, f32[128,128]{1,0:T(8,128)S(1)}, u32[]{:S(2)}, u32[]{:S(2)}) collective-permute-start(f32[128,128]{1,0:T(8,128)S(1)} %add.89), channel_id=1, source_target_pairs={{0,64},{8,72},{16,80},{24,88},{32,96},{40,104},{48,112},{56,120},{... | collective-permute-start | bytes 196616 | tf_op jit(solution)/shard_map/ppermute | solution.py:25
  124.5 5.5 %collective-permute-start.7 = (f32[128,128]{1,0:T(8,128)S(1)}, f32[128,128]{1,0:T(8,128)S(1)}, u32[]{:S(2)}, u32[]{:S(2)}) collective-permute-start(f32[128,128]{1,0:T(8,128)S(1)} %add.90), channel_id=1, source_target_pairs={{0,128},{8,136},{16,144},{24,152},{32,160},{40,168},{48,176},{56,1... | collective-permute-start | bytes 196616 | tf_op jit(solution)/shard_map/ppermute | solution.py:25
  141.2 3.6 %copy-start.4 = (s32[64]{0:T(128)S(1)}, s32[64]{0:T(128)}, u32[]{:S(2)}) copy-start(s32[64]{0:T(128)} %param.5) | copy-start | bytes 772
  141.2 3.7 %copy-start.1 = (bf16[4096,128]{1,0:T(8,128)(2,1)S(1)}, bf16[4096,128]{1,0:T(8,128)(2,1)}, u32[]{:S(2)}) copy-start(bf16[4096,128]{1,0:T(8,128)(2,1)} %shard_map.51) | copy-start | bytes 3145732
  149.1 71.0 %copy-start.3 = (f32[64,128]{1,0:T(8,128)}, f32[64,128]{1,0:T(8,128)S(1)}, u32[]{:S(2)}) copy-start(f32[64,128]{1,0:T(8,128)S(1)} %multiply_add_fusion) | copy-start | bytes 98308
  150.4 69.7 %copy-start.2 = (s32[8192]{0:T(1024)S(1)}, s32[8192]{0:T(1024)}, u32[]{:S(2)}) copy-start(s32[8192]{0:T(1024)} %reshape.323.index_ref) | copy-start | bytes 98308

commit v9 on v8

--- a/solution.py
+++ b/solution.py
@@ -37,7 +37,7 @@
         out_ref[pl.ds(first, GATHER_TILE), :] = jnp.concatenate(rows, axis=0).astype(out_ref.dtype)
         return carry
 
-    lax.fori_loop(0, out_ref.shape[0] // GATHER_TILE, body, 0)
+    lax.fori_loop(0, out_ref.shape[0] // GATHER_TILE, body, 0, unroll=4)
 
 
 def gather_rows(source, index):

time: 232 us -> 229 us (0.987)
  Pallas kernels: 22 us -> 19.1 us
    pallas_call x2, Pallas kernels: 22 us -> 19.1 us  [gather_rows(): pl.pallas_call(gather_rows_kernel, grid_spec=pltpu.PrefetchScalarGridSpec...]
where the time goes in v9:
time: 229 us; the launch traced here: 228 us
  blocking collectives  69.7 us (30%)
  waiting for transfers between devices  64.7 us (28%)
  starting transfers between devices  36 us (16%)
  matrix products  24.6 us (11%)
  Pallas kernels  19.1 us (8%)
  other arithmetic  10.4 us (5%)
  local copies, waits for them, and re-layouts  2.87 us (1%)
    all_to_all x1, blocking collectives, exchange(): return lax.all_to_all(values, ('rows', 'grp'), 0, 0, tiled=True)  69.7 us
    ppermute x8, waiting for transfers between devices, sum_over_devices(): value = value + lax.ppermute(value, axis, partners)  52.9 us
    all_to_all x2, starting transfers between devices, exchange(): return lax.all_to_all(values, ('rows', 'grp'), 0, 0, tiled=True)  21.2 us
    pallas_call x2, Pallas kernels, gather_rows(): pl.pallas_call(gather_rows_kernel, grid_spec=pltpu.PrefetchScalarGridSpec...  19.1 us
    ppermute x8, starting transfers between devices, sum_over_devices(): value = value + lax.ppermute(value, axis, partners)  14.8 us
    all_to_all x2, waiting for transfers between devices, exchange(): return lax.all_to_all(values, ('rows', 'grp'), 0, 0, tiled=True)  11.8 us
    dot_general x1, matrix products, on_device(): jnp.einsum('st,sk->tk', picks, arrived, preferred_element_type=f32)  11 us
  transfers between devices with their start and end apart: 10, of which 9 were waited for; matrix products, arithmetic and copies ran while one was open for 1% of the time, Pallas kernels for 0%

profile of v9, /device:TPU:1, one launch (start us, length us, event | category | flops | bytes accessed | tf_op | source)
XLA Modules:
  0.0 228.3 jit_solution(17231420452281694320)
XLA Ops:
  0.7 0.7 fusion.72
  1.4 0.1 lt.34
  1.5 0.8 multiply_subtract_fusion.2
  2.3 0.1 reshape.321
  2.4 1.4 fusion.53
  3.8 1.4 fusion.5
  5.2 0.1 broadcast_in_dim.44
  5.4 0.1 fusion.25
  5.6 3.2 %multiply_reduce_fusion = f32[64,64]{1,0:T(8,128)S(1)} fusion(f32[64,65]{1,0:T(8,128)S(1)} %fusion.70, bf16[64,1,256]{2,1,0:T(2,128)(2,1)S(1)} %copy.18, bf16[64,64,256]{2,1,0:T(8,128)(2,1)S(1)} %fusion.5, s32[64,64]{1,0:T(8,128)S(1)} %get-tuple-element.13, pred[64,64]{1,0:T(8,128)(4,1)S(1)} %get-tuple-element.17), kind=kOutput, calls=%fused_computation.25 | convolution fusion | flops 143200256 | bytes 2183424 | tf_op jit(solution)/shard_map/ujo,uko->ujk/dot_general | solution.py:88
  8.9 1.7 fusion.22
  10.6 0.8 copy.19
  11.4 15.7 %all-to-all-start = ((s32[256,1,32]{2,1,0:T(1,128)}), s32[256,1,32]{2,1,0:T(1,128)S(1)}, u32[]{:S(2)}, u32[]{:S(2)}) async-start(s32[256,1,32]{2,1,0:T(1,128)} %copy.19), calls=%async_computation | async-start | bytes 262144 | tf_op jit(solution)/shard_map/all_to_all | solution.py:16
  27.1 1.0 convert_element_type.88.source_ref
  28.1 11.8 %all-to-all-done = s32[256,1,32]{2,1,0:T(1,128)S(1)} async-done(((s32[256,1,32]{2,1,0:T(1,128)}), s32[256,1,32]{2,1,0:T(1,128)S(1)}, u32[]{:S(2)}, u32[]{:S(2)}) %all-to-all-start) | async-done | bytes 32800 | tf_op jit(solution)/shard_map/all_to_all | solution.py:16
  39.9 0.5 broadcast.323
  40.4 1.0 reduce.4
  41.3 0.7 reshape.323.index_ref
  42.0 11.3 %shard_map.50 = bf16[8192,128]{1,0:T(8,128)(2,1)} custom-call(s32[8192]{0:T(1024)} %reshape.323.index_ref, f32[1984,128]{1,0:T(8,128)} %convert_element_type.88.source_ref), custom_call_target="tpu_custom_call" | custom-call | tf_op jit(solution)/shard_map/pallas_call | solution.py:47
  53.3 5.5 %all-to-all-start.1 = ((bf16[256,32,128]{2,1,0:T(8,128)(2,1)}), bf16[256,32,128]{2,1,0:T(8,128)(2,1)S(1)}, u32[]{:S(2)}, u32[]{:S(2)}) async-start(bf16[256,32,128]{2,1,0:T(8,128)(2,1)} %bitcast.63), calls=%async_computation.1 | async-start | bytes 4194304 | tf_op jit(solution)/shard_map/all_to_all | solution.py:16
  58.9 0.3 fusion.86
  59.2 2.4 %collective-permute-start = (f32[128,128]{1,0:T(8,128)S(1)}, f32[128,128]{1,0:T(8,128)S(1)}, u32[]{:S(2)}, u32[]{:S(2)}) collective-permute-start(f32[128,128]{1,0:T(8,128)S(1)} %fusion.86), channel_id=1, source_target_pairs={{0,1},{1,0},{2,3},{3,2},{4,5},{5,4},{6,7},{7,6},{8,9},{9,8},{10,11... | collective-permute-start | bytes 196616 | tf_op jit(solution)/shard_map/ppermute | solution.py:25
  61.6 0.9 collective-permute-done
  62.5 0.1 collective-permute-start.1
  62.6 4.6 %collective-permute-done.1 = f32[128,128]{1,0:T(8,128)S(1)} collective-permute-done((f32[128,128]{1,0:T(8,128)S(1)}, f32[128,128]{1,0:T(8,128)S(1)}, u32[]{:S(2)}, u32[]{:S(2)}) %collective-permute-start.1) | collective-permute-done | bytes 65568 | tf_op jit(solution)/shard_map/ppermute | solution.py:25
  67.2 1.3 collective-permute-start.2
  68.5 4.7 %collective-permute-done.2 = f32[128,128]{1,0:T(8,128)S(1)} collective-permute-done((f32[128,128]{1,0:T(8,128)S(1)}, f32[128,128]{1,0:T(8,128)S(1)}, u32[]{:S(2)}, u32[]{:S(2)}) %collective-permute-start.2) | collective-permute-done | bytes 65568 | tf_op jit(solution)/shard_map/ppermute | solution.py:25
  73.2 0.1 collective-permute-start.3
  73.3 32.7 %collective-permute-done.3 = f32[128,128]{1,0:T(8,128)S(1)} collective-permute-done((f32[128,128]{1,0:T(8,128)S(1)}, f32[128,128]{1,0:T(8,128)S(1)}, u32[]{:S(2)}, u32[]{:S(2)}) %collective-permute-start.3) | collective-permute-done | bytes 65568 | tf_op jit(solution)/shard_map/ppermute | solution.py:25
  106.0 1.4 collective-permute-start.4
  107.4 4.8 %collective-permute-done.4 = f32[128,128]{1,0:T(8,128)S(1)} collective-permute-done((f32[128,128]{1,0:T(8,128)S(1)}, f32[128,128]{1,0:T(8,128)S(1)}, u32[]{:S(2)}, u32[]{:S(2)}) %collective-permute-start.4) | collective-permute-done | bytes 65568 | tf_op jit(solution)/shard_map/ppermute | solution.py:25
  112.2 4.7 %collective-permute-start.5 = (f32[128,128]{1,0:T(8,128)S(1)}, f32[128,128]{1,0:T(8,128)S(1)}, u32[]{:S(2)}, u32[]{:S(2)}) collective-permute-start(f32[128,128]{1,0:T(8,128)S(1)} %add.88), channel_id=1, source_target_pairs={{0,32},{8,40},{16,48},{24,56},{32,0},{40,8},{48,16},{56,24},{64,96... | collective-permute-start | bytes 196616 | tf_op jit(solution)/shard_map/ppermute | solution.py:25
  116.9 2.5 %collective-permute-done.5 = f32[128,128]{1,0:T(8,128)S(1)} collective-permute-done((f32[128,128]{1,0:T(8,128)S(1)}, f32[128,128]{1,0:T(8,128)S(1)}, u32[]{:S(2)}, u32[]{:S(2)}) %collective-permute-start.5) | collective-permute-done | bytes 65568 | tf_op jit(solution)/shard_map/ppermute | solution.py:25
  119.4 1.6 collective-permute-start.6
  121.0 0.6 multiply_add_fusion.3.index_ref
  121.6 1.0 collective-permute-done.6
  122.6 3.3 %collective-permute-start.7 = (f32[128,128]{1,0:T(8,128)S(1)}, f32[128,128]{1,0:T(8,128)S(1)}, u32[]{:S(2)}, u32[]{:S(2)}) collective-permute-start(f32[128,128]{1,0:T(8,128)S(1)} %add.90), channel_id=1, source_target_pairs={{0,128},{8,136},{16,144},{24,152},{32,160},{40,168},{48,176},{56,1... | collective-permute-start | bytes 196616 | tf_op jit(solution)/shard_map/ppermute | solution.py:25
  125.9 0.1 copy.21
  126.1 0.1 gt.16
  126.2 0.1 copy.20
  126.3 0.1 eq.102
  126.4 1.8 collective-permute-done.7
  128.2 2.3 %bitcast_convert_fusion.source_ref = f32[8192,128]{1,0:T(8,128)} fusion(bf16[256,32,128]{2,1,0:T(8,128)(2,1)S(1)} %all-to-all-done.1), kind=kLoop, calls=%fused_computation.21 | loop fusion | flops 1048576 | bytes 6291456 | tf_op jit(solution)/shard_map/convert_element_type | solution.py:46
  130.5 7.8 %shard_map.51 = bf16[4096,128]{1,0:T(8,128)(2,1)} custom-call(s32[4096]{0:T(1024)} %multiply_add_fusion.3.index_ref, f32[8192,128]{1,0:T(8,128)} %bitcast_convert_fusion.source_ref), custom_call_target="tpu_custom_call" | custom-call | tf_op jit(solution)/shard_map/pallas_call | solution.py:47
  138.4 1.7 fusion.66
  140.1 1.9 fusion.64
  141.9 0.1 fusion.73
  142.0 0.4 fusion.62
  142.4 0.3 multiply_reduce_fusion.4
  142.7 0.2 multiply_reduce_fusion.3
  142.9 0.1 convert_bitcast_fusion.1
  143.0 0.6 fusion.60
  143.7 0.1 fusion.74
  143.7 0.4 fusion.58
  144.1 0.3 multiply_reduce_fusion.2
  144.4 0.2 multiply_reduce_fusion.1
  144.6 0.1 convert_bitcast_fusion
  144.8 0.6 fusion.56
  145.4 0.1 fusion.75
  145.5 0.4 fusion.54
  145.9 0.3 fusion.33
  146.2 0.1 multiply_add_fusion
  146.3 1.3 convolution_convert_fusion
  147.6 69.7 %all_to_all.16 = bf16[256,32,128]{2,1,0:T(8,128)(2,1)S(1)} all-to-all(bf16[256,32,128]{2,1,0:T(8,128)(2,1)S(1)} %bitcast.64), channel_id=1, replica_groups=mesh['rows'=32,'grp'=8] {'rows','grp'}, dimensions={0} | all-to-all | bytes 4194304 | tf_op jit(solution)/shard_map/all_to_all | solution.py:16
  217.3 11.0 %fusion = f32[1984,128]{1,0:T(8,128)} fusion(bf16[8192,128]{1,0:T(8,128)(2,1)S(1)} %bitcast.65, s32[8192]{0:T(1024)S(1)} %copy-done.2), kind=kOutput, calls=%fused_computation.1 | convolution fusion | flops 4177002496 | bytes 3145728 | tf_op jit(solution)/shard_map/st,sk->tk/dot_general | solution.py:151
  (38 shorter events, 0.4 us)
Async XLA Ops:
  8.9 18.1 %copy-start = (bf16[1984,128]{1,0:T(8,128)(2,1)S(1)}, bf16[1984,128]{1,0:T(8,128)(2,1)}, u32[]{:S(2)}) copy-start(bf16[1984,128]{1,0:T(8,128)(2,1)} %param.3) | copy-start | bytes 1523716
  11.4 28.5 %all-to-all-start = ((s32[256,1,32]{2,1,0:T(1,128)}), s32[256,1,32]{2,1,0:T(1,128)S(1)}, u32[]{:S(2)}, u32[]{:S(2)}) async-start(s32[256,1,32]{2,1,0:T(1,128)} %copy.19), calls=%async_computation | async-start | bytes 262144 | tf_op jit(solution)/shard_map/all_to_all | solution.py:16
  53.3 74.8 %all-to-all-start.1 = ((bf16[256,32,128]{2,1,0:T(8,128)(2,1)}), bf16[256,32,128]{2,1,0:T(8,128)(2,1)S(1)}, u32[]{:S(2)}, u32[]{:S(2)}) async-start(bf16[256,32,128]{2,1,0:T(8,128)(2,1)} %bitcast.63), calls=%async_computation.1 | async-start | bytes 4194304 | tf_op jit(solution)/shard_map/all_to_all | solution.py:16
  59.2 3.3 %collective-permute-start = (f32[128,128]{1,0:T(8,128)S(1)}, f32[128,128]{1,0:T(8,128)S(1)}, u32[]{:S(2)}, u32[]{:S(2)}) collective-permute-start(f32[128,128]{1,0:T(8,128)S(1)} %fusion.86), channel_id=1, source_target_pairs={{0,1},{1,0},{2,3},{3,2},{4,5},{5,4},{6,7},{7,6},{8,9},{9,8},{10,11... | collective-permute-start | bytes 196616 | tf_op jit(solution)/shard_map/ppermute | solution.py:25
  62.5 4.7 %collective-permute-start.1 = (f32[128,128]{1,0:T(8,128)S(1)}, f32[128,128]{1,0:T(8,128)S(1)}, u32[]{:S(2)}, u32[]{:S(2)}) collective-permute-start(f32[128,128]{1,0:T(8,128)S(1)} %add.84), channel_id=1, source_target_pairs={{0,2},{1,3},{2,0},{3,1},{4,6},{5,7},{6,4},{7,5},{8,10},{9,11},{10,... | collective-permute-start | bytes 196616 | tf_op jit(solution)/shard_map/ppermute | solution.py:25
  67.2 6.0 %collective-permute-start.2 = (f32[128,128]{1,0:T(8,128)S(1)}, f32[128,128]{1,0:T(8,128)S(1)}, u32[]{:S(2)}, u32[]{:S(2)}) collective-permute-start(f32[128,128]{1,0:T(8,128)S(1)} %add.85), channel_id=1, source_target_pairs={{0,4},{1,5},{2,6},{3,7},{4,0},{5,1},{6,2},{7,3},{8,12},{9,13},{10,... | collective-permute-start | bytes 196616 | tf_op jit(solution)/shard_map/ppermute | solution.py:25
  73.2 32.8 %collective-permute-start.3 = (f32[128,128]{1,0:T(8,128)S(1)}, f32[128,128]{1,0:T(8,128)S(1)}, u32[]{:S(2)}, u32[]{:S(2)}) collective-permute-start(f32[128,128]{1,0:T(8,128)S(1)} %add.86), channel_id=1, source_target_pairs={{0,8},{8,0},{16,24},{24,16},{32,40},{40,32},{48,56},{56,48},{64,72... | collective-permute-start | bytes 196616 | tf_op jit(solution)/shard_map/ppermute | solution.py:25
  106.0 6.2 %collective-permute-start.4 = (f32[128,128]{1,0:T(8,128)S(1)}, f32[128,128]{1,0:T(8,128)S(1)}, u32[]{:S(2)}, u32[]{:S(2)}) collective-permute-start(f32[128,128]{1,0:T(8,128)S(1)} %add.87), channel_id=1, source_target_pairs={{0,16},{8,24},{16,0},{24,8},{32,48},{40,56},{48,32},{56,40},{64,80... | collective-permute-start | bytes 196616 | tf_op jit(solution)/shard_map/ppermute | solution.py:25
  112.2 7.2 %collective-permute-start.5 = (f32[128,128]{1,0:T(8,128)S(1)}, f32[128,128]{1,0:T(8,128)S(1)}, u32[]{:S(2)}, u32[]{:S(2)}) collective-permute-start(f32[128,128]{1,0:T(8,128)S(1)} %add.88), channel_id=1, source_target_pairs={{0,32},{8,40},{16,48},{24,56},{32,0},{40,8},{48,16},{56,24},{64,96... | collective-permute-start | bytes 196616 | tf_op jit(solution)/shard_map/ppermute | solution.py:25
  119.4 3.2 %collective-permute-start.6 = (f32[128,128]{1,0:T(8,128)S(1)}, f32[128,128]{1,0:T(8,128)S(1)}, u32[]{:S(2)}, u32[]{:S(2)}) collective-permute-start(f32[128,128]{1,0:T(8,128)S(1)} %add.89), channel_id=1, source_target_pairs={{0,64},{8,72},{16,80},{24,88},{32,96},{40,104},{48,112},{56,120},{... | collective-permute-start | bytes 196616 | tf_op jit(solution)/shard_map/ppermute | solution.py:25
  122.6 5.5 %collective-permute-start.7 = (f32[128,128]{1,0:T(8,128)S(1)}, f32[128,128]{1,0:T(8,128)S(1)}, u32[]{:S(2)}, u32[]{:S(2)}) collective-permute-start(f32[128,128]{1,0:T(8,128)S(1)} %add.90), channel_id=1, source_target_pairs={{0,128},{8,136},{16,144},{24,152},{32,160},{40,168},{48,176},{56,1... | collective-permute-start | bytes 196616 | tf_op jit(solution)/shard_map/ppermute | solution.py:25
  138.4 3.6 %copy-start.4 = (s32[64]{0:T(128)S(1)}, s32[64]{0:T(128)}, u32[]{:S(2)}) copy-start(s32[64]{0:T(128)} %param.5) | copy-start | bytes 772
  138.4 3.7 %copy-start.1 = (bf16[4096,128]{1,0:T(8,128)(2,1)S(1)}, bf16[4096,128]{1,0:T(8,128)(2,1)}, u32[]{:S(2)}) copy-start(bf16[4096,128]{1,0:T(8,128)(2,1)} %shard_map.51) | copy-start | bytes 3145732
  146.3 71.0 %copy-start.3 = (f32[64,128]{1,0:T(8,128)}, f32[64,128]{1,0:T(8,128)S(1)}, u32[]{:S(2)}) copy-start(f32[64,128]{1,0:T(8,128)S(1)} %multiply_add_fusion) | copy-start | bytes 98308
  147.6 69.7 %copy-start.2 = (s32[8192]{0:T(1024)S(1)}, s32[8192]{0:T(1024)}, u32[]{:S(2)}) copy-start(s32[8192]{0:T(1024)} %reshape.323.index_ref) | copy-start | bytes 98308

commit v10 on v9

--- a/solution.py
+++ b/solution.py
@@ -40,10 +40,9 @@
     lax.fori_loop(0, out_ref.shape[0] // GATHER_TILE, body, 0, unroll=4)
 
 
-def gather_rows(source, index):
+def gather_rows(wide, index, dtype):
     count = index.shape[0]
-    rows, width = source.shape
-    wide = source.astype(jnp.float32)
+    rows, width = wide.shape
     picked = pl.pallas_call(
         gather_rows_kernel,
         grid_spec=pltpu.PrefetchScalarGridSpec(
@@ -52,7 +51,7 @@
             in_specs=[pl.BlockSpec((rows, width), lambda i, index_ref: (0, 0))],
             out_specs=pl.BlockSpec((count, width), lambda i, index_ref: (0, 0)),
         ),
-        out_shape=jax.ShapeDtypeStruct((count, width), source.dtype),
+        out_shape=jax.ShapeDtypeStruct((count, width), dtype),
     )(index, wide)
     return picked
 
@@ -72,7 +71,6 @@
     local_gram = lax.dot_general(
         item_table, item_table, (((0,), (0,)), ((), ())), preferred_element_type=f32
     )
-    gramian = sum_over_devices(local_gram)
 
     positions = lax.broadcasted_iota(jnp.int32, (user_count, history_length), 1)
     live = positions < counts[:, None]
@@ -111,14 +109,39 @@
     slot_user = slots[:, 2].reshape(slots_total)
     slot_used = slots[:, 3].reshape(slots_total)
 
-    slot_index = owners.reshape(lookups) * capacity + ranks
 
-    incoming = exchange(requests).reshape(slots_total)
-    answered = gather_rows(item_table, incoming)
-    reply_rows = exchange(answered.reshape(devices, capacity, embed_width)).reshape(
-        slots_total, embed_width
+    gram_width = embed_width * embed_width // devices
+    outgoing = jnp.concatenate(
+        [requests.astype(f32), local_gram.reshape(devices, gram_width)], axis=1
     )
-    fetched = gather_rows(reply_rows, slot_index).reshape(user_count, history_length, embed_width)
+    received = exchange(outgoing)
+    incoming = received[:, :capacity].astype(jnp.int32).reshape(slots_total)
+    gram_slice = jnp.sum(received[:, capacity:], axis=0)
+    high = lax.optimization_barrier(gram_slice.astype(bf16))
+    rest = gram_slice - high.astype(f32)
+    middle = lax.optimization_barrier(rest.astype(bf16))
+    low = (rest - middle.astype(f32)).astype(bf16)
+    pieces = jnp.concatenate([high, middle, low], axis=0)
+    extra_rows = -(-pieces.shape[0] // embed_width)
+    pieces = jnp.pad(pieces, (0, extra_rows * embed_width - pieces.shape[0]))
+    source_rows = jnp.concatenate(
+        [item_table.astype(f32), pieces.astype(f32).reshape(extra_rows, embed_width)], axis=0
+    )
+    reply_capacity = capacity + extra_rows
+    piece_ids = jnp.broadcast_to(
+        table_rows + jnp.arange(extra_rows, dtype=jnp.int32), (devices, extra_rows)
+    )
+    wanted = jnp.concatenate([incoming.reshape(devices, capacity), piece_ids], axis=1)
+    answered = gather_rows(source_rows, wanted.reshape(devices * reply_capacity), bf16)
+    replies = exchange(answered.reshape(devices, reply_capacity, embed_width))
+    parts = replies[:, capacity:].reshape(devices, extra_rows * embed_width)[:, : 3 * gram_width]
+    parts = parts.astype(f32).reshape(devices, 3, gram_width)
+    gramian = ((parts[:, 0] + parts[:, 1]) + parts[:, 2]).reshape(embed_width, embed_width)
+    reply_rows = replies.reshape(devices * reply_capacity, embed_width)
+    slot_index = owners.reshape(lookups) * reply_capacity + ranks
+    fetched = gather_rows(reply_rows.astype(f32), slot_index, bf16).reshape(
+        user_count, history_length, embed_width
+    )
     weights = live.astype(f32)
     narrow_weights = weights.astype(bf16)
     target = jnp.einsum("ul,ulk->uk", narrow_weights, fetched, preferred_element_type=f32)

time: 229 us -> 222 us (0.969)
  blocking collectives: 69.7 us -> 0 us
  waiting for transfers between devices: 64.7 us -> 130 us
  starting transfers between devices: 36 us -> 27.6 us
  local copies, waits for them, and re-layouts: 2.87 us -> 9.78 us
  other arithmetic: 10.4 us -> 8.07 us
    all_to_all x2 -> x3, waiting for transfers between devices: 11.8 us -> 130 us  [exchange(): return lax.all_to_all(values, ('rows', 'grp'), 0, 0, tiled=True)]
    all_to_all x1 -> x0, blocking collectives: 69.7 us -> none  [exchange(): return lax.all_to_all(values, ('rows', 'grp'), 0, 0, tiled=True)]
    ppermute x8 -> x0, waiting for transfers between devices: 52.9 us -> none  [sum_over_devices(): value = value + lax.ppermute(value, axis, partners)]
    ppermute x8 -> x0, starting transfers between devices: 14.8 us -> none  [sum_over_devices(): value = value + lax.ppermute(value, axis, partners)]
    all_to_all x2 -> x3, starting transfers between devices: 21.2 us -> 27.6 us  [exchange(): return lax.all_to_all(values, ('rows', 'grp'), 0, 0, tiled=True)]
    reshape x2 -> x5, local copies, waits for them, and re-layouts: 0.78 us -> 5.74 us  [the longest x1 4.72 us: on_device(): replies = exchange(answered.reshape(devices, reply_capacity, embed_width))]
    convert_element_type x2 -> x4, other arithmetic: 3.37 us -> 0.03 us  [the longest x1 0.01 us: on_device(): incoming = received[:, :capacity].astype(jnp.int32).reshape(slots_total)]
    convert_element_type x0 -> x2, local copies, waits for them, and re-layouts: none -> 2.8 us  [the longest x1 2.71 us: on_device(): reply_rows.astype(f32)]
  transfers between devices with their start and end apart: 10 -> 3, of which waited for: 9 -> 3; matrix products, arithmetic and copies ran while one was open for 1% -> 1% of each run, Pallas kernels for 0% -> 0%
where the time goes in v10:
time: 222 us
  waiting for transfers between devices  130 us (59%)
  starting transfers between devices  27.6 us (12%)
  matrix products  25.9 us (12%)
  Pallas kernels  19.7 us (9%)
  local copies, waits for them, and re-layouts  9.78 us (4%)
  other arithmetic  8.07 us (4%)
    all_to_all x3, waiting for transfers between devices, exchange(): return lax.all_to_all(values, ('rows', 'grp'), 0, 0, tiled=True)  130 us
    all_to_all x3, starting transfers between devices, exchange(): return lax.all_to_all(values, ('rows', 'grp'), 0, 0, tiled=True)  27.6 us
    pallas_call x2, Pallas kernels, gather_rows(): pl.pallas_call(gather_rows_kernel, grid_spec=pltpu.PrefetchScalarGridSpec...  19.7 us
    dot_general x1, matrix products, on_device(): jnp.einsum('st,sk->tk', picks, arrived, preferred_element_type=f32)  11 us
    reshape x1, local copies, waits for them, and re-layouts, on_device(): replies = exchange(answered.reshape(devices, reply_capacity, embed_width))  4.72 us
  transfers between devices with their start and end apart: 3, of which 3 were waited for; matrix products, arithmetic and copies ran while one was open for 1% of the time, Pallas kernels for 0%

profile of v10, /device:TPU:1, one launch (start us, length us, event | category | flops | bytes accessed | tf_op | source)
XLA Modules:
  0.0 221.7 jit_solution(10014575281943399141)
XLA Ops:
  0.7 0.8 fusion.74
  1.5 0.1 lt.34
  1.6 0.8 multiply_subtract_fusion.2
  2.4 0.1 reshape.345
  2.4 1.4 fusion.53
  3.8 1.4 fusion.5
  5.3 0.1 broadcast_in_dim.47
  5.4 0.3 fusion.95
  5.7 0.1 reshape.347
  5.8 0.1 reshape.346
  5.9 0.1 fusion.25
  6.0 0.1 copy.29
  6.1 3.2 %multiply_reduce_fusion = f32[64,64]{1,0:T(8,128)S(1)} fusion(f32[64,65]{1,0:T(8,128)S(1)} %fusion.72, bf16[64,1,256]{2,1,0:T(2,128)(2,1)S(1)} %copy.29, bf16[64,64,256]{2,1,0:T(8,128)(2,1)S(1)} %fusion.5, s32[64,64]{1,0:T(8,128)S(1)} %get-tuple-element.13, pred[64,64]{1,0:T(8,128)(4,1)S(1)} %get-tuple-element.17), kind=kOutput, calls=%fused_computation.24 | convolution fusion | flops 143200256 | bytes 2183424 | tf_op jit(solution)/shard_map/ujo,uko->ujk/dot_general | solution.py:86
  9.3 0.1 convert_element_type.111
  9.4 1.7 fusion.22
  11.1 0.1 copy.30
  11.2 0.8 pad_maximum_fusion
  12.0 15.7 %all-to-all-start = ((f32[256,1,96]{2,1,0:T(1,128)}), f32[256,1,96]{2,1,0:T(1,128)S(1)}, u32[]{:S(2)}, u32[]{:S(2)}) async-start(f32[256,1,96]{2,1,0:T(1,128)} %bitcast.5), calls=%async_computation | async-start | bytes 262144 | tf_op jit(solution)/shard_map/all_to_all | solution.py:16
  27.7 0.1 pad.11.clone
  27.7 12.6 %all-to-all-done = f32[256,1,96]{2,1,0:T(1,128)S(1)} async-done(((f32[256,1,96]{2,1,0:T(1,128)}), f32[256,1,96]{2,1,0:T(1,128)S(1)}, u32[]{:S(2)}, u32[]{:S(2)}) %all-to-all-start) | async-done | bytes 98336 | tf_op jit(solution)/shard_map/all_to_all | solution.py:16
  40.4 0.1 slice_reduce_fusion
  40.6 0.1 fusion.87
  40.7 0.8 reshape.348.index_ref
  41.4 1.0 maximum_convert_fusion.source_ref
  42.4 11.8 %shard_map.50 = bf16[8704,128]{1,0:T(8,128)(2,1)} custom-call(s32[8704]{0:T(1024)} %reshape.348.index_ref, f32[1986,128]{1,0:T(8,128)} %maximum_convert_fusion.source_ref), custom_call_target="tpu_custom_call" | custom-call | tf_op jit(solution)/shard_map/pallas_call | solution.py:46
  54.3 4.7 %reshape.350 = bf16[256,34,128]{2,1,0:T(8,128)(2,1)} reshape(bf16[8704,128]{1,0:T(8,128)(2,1)} %shard_map.50) | data formatting | bytes 4456448 | tf_op jit(solution)/shard_map/reshape | solution.py:136
  59.0 5.5 %all-to-all-start.1 = ((bf16[256,34,128]{2,1,0:T(8,128)(2,1)}), bf16[256,34,128]{2,1,0:T(8,128)(2,1)S(1)}, u32[]{:S(2)}, u32[]{:S(2)}) async-start(bf16[256,34,128]{2,1,0:T(8,128)(2,1)} %reshape.350), calls=%async_computation.1 | async-start | bytes 5242880 | tf_op jit(solution)/shard_map/all_to_all | solution.py:16
  64.6 0.1 copy.35
  64.7 0.1 gt.16
  64.8 0.1 copy.34
  64.9 0.1 eq.105
  65.0 0.6 multiply_add_fusion.3.index_ref
  65.6 63.6 %all-to-all-done.1 = bf16[256,34,128]{2,1,0:T(8,128)(2,1)S(1)} async-done(((bf16[256,34,128]{2,1,0:T(8,128)(2,1)}), bf16[256,34,128]{2,1,0:T(8,128)(2,1)S(1)}, u32[]{:S(2)}, u32[]{:S(2)}) %all-to-all-start.1) | async-done | bytes 2228256 | tf_op jit(solution)/shard_map/all_to_all | solution.py:16
  129.3 0.1 slice.48
  129.3 0.1 copy.50
  129.5 0.1 copy.33
  129.6 0.1 add.80
  129.7 2.7 %reshape.357.source_ref = f32[8704,128]{1,0:T(8,128)} reshape(bf16[256,34,128]{2,1,0:T(8,128)(2,1)S(1)} %all-to-all-done.1) | data formatting | bytes 6684672 | tf_op jit(solution)/shard_map/convert_element_type | solution.py:142
  132.4 7.9 %shard_map.51 = bf16[4096,128]{1,0:T(8,128)(2,1)} custom-call(s32[4096]{0:T(1024)} %multiply_add_fusion.3.index_ref, f32[8704,128]{1,0:T(8,128)} %reshape.357.source_ref), custom_call_target="tpu_custom_call" | custom-call | tf_op jit(solution)/shard_map/pallas_call | solution.py:46
  140.3 1.7 fusion.68
  142.0 1.9 fusion.66
  143.9 0.1 fusion.75
  144.0 0.0 copy-done.1
  144.0 0.4 fusion.64
  144.4 0.3 multiply_reduce_fusion.4
  144.7 0.2 multiply_reduce_fusion.3
  144.9 0.1 convert_bitcast_fusion.1
  145.0 0.6 fusion.62
  145.6 0.1 fusion.76
  145.7 0.4 fusion.60
  146.1 0.3 multiply_reduce_fusion.2
  146.4 0.2 multiply_reduce_fusion.1
  146.6 0.1 convert_bitcast_fusion
  146.7 0.6 fusion.58
  147.3 0.1 fusion.77
  147.4 0.4 fusion.56
  147.8 0.3 fusion.33
  148.1 0.1 multiply_add_fusion
  148.2 0.0 copy-start.2
  148.2 2.6 %convolution_convert_fusion = bf16[8192,128]{1,0:T(8,128)(2,1)} fusion(s32[8192]{0:T(1024)S(1)} %eq.105, pred[8192]{0:T(1024)(128)(4,1)S(1)} %gt.16, f32[64,128]{1,0:T(8,128)S(1)} %multiply_add_fusion), kind=kOutput, calls=%fused_computation.3 | convolution fusion | flops 136323072 | bytes 2170880 | tf_op jit(solution)/shard_map/su,uk->sk/dot_general | solution.py:169
  150.9 6.4 %all-to-all-start.2 = ((bf16[256,32,128]{2,1,0:T(8,128)(2,1)}), bf16[256,32,128]{2,1,0:T(8,128)(2,1)S(1)}, u32[]{:S(2)}, u32[]{:S(2)}) async-start(bf16[256,32,128]{2,1,0:T(8,128)(2,1)} %bitcast.32), calls=%async_computation.2 | async-start | bytes 4194304 | tf_op jit(solution)/shard_map/all_to_all | solution.py:16
  157.3 0.1 eq.102
  157.4 53.3 %all-to-all-done.2 = bf16[256,32,128]{2,1,0:T(8,128)(2,1)S(1)} async-done(((bf16[256,32,128]{2,1,0:T(8,128)(2,1)}), bf16[256,32,128]{2,1,0:T(8,128)(2,1)S(1)}, u32[]{:S(2)}, u32[]{:S(2)}) %all-to-all-start.2) | async-done | bytes 2097184 | tf_op jit(solution)/shard_map/all_to_all | solution.py:16
  210.7 11.0 %fusion = f32[1984,128]{1,0:T(8,128)} fusion(bf16[8192,128]{1,0:T(8,128)(2,1)S(1)} %bitcast.72, s32[8192]{0:T(1024)S(1)} %eq.102), kind=kOutput, calls=%fused_computation.1 | convolution fusion | flops 4177002496 | bytes 3145728 | tf_op jit(solution)/shard_map/st,sk->tk/dot_general | solution.py:174
  (31 shorter events, 0.2 us)
Async XLA Ops:
  0.6 4.7 %copy-start = (bf16[1984,128]{1,0:T(8,128)(2,1)S(1)}, bf16[1984,128]{1,0:T(8,128)(2,1)}, u32[]{:S(2)}) copy-start(bf16[1984,128]{1,0:T(8,128)(2,1)} %param.3) | copy-start | bytes 1523716
  12.0 28.4 %all-to-all-start = ((f32[256,1,96]{2,1,0:T(1,128)}), f32[256,1,96]{2,1,0:T(1,128)S(1)}, u32[]{:S(2)}, u32[]{:S(2)}) async-start(f32[256,1,96]{2,1,0:T(1,128)} %bitcast.5), calls=%async_computation | async-start | bytes 262144 | tf_op jit(solution)/shard_map/all_to_all | solution.py:16
  59.0 70.3 %all-to-all-start.1 = ((bf16[256,34,128]{2,1,0:T(8,128)(2,1)}), bf16[256,34,128]{2,1,0:T(8,128)(2,1)S(1)}, u32[]{:S(2)}, u32[]{:S(2)}) async-start(bf16[256,34,128]{2,1,0:T(8,128)(2,1)} %reshape.350), calls=%async_computation.1 | async-start | bytes 5242880 | tf_op jit(solution)/shard_map/all_to_all | solution.py:16
  140.3 3.6 %copy-start.3 = (s32[64]{0:T(128)S(1)}, s32[64]{0:T(128)}, u32[]{:S(2)}) copy-start(s32[64]{0:T(128)} %param.5) | copy-start | bytes 772
  140.3 3.7 %copy-start.1 = (bf16[4096,128]{1,0:T(8,128)(2,1)S(1)}, bf16[4096,128]{1,0:T(8,128)(2,1)}, u32[]{:S(2)}) copy-start(bf16[4096,128]{1,0:T(8,128)(2,1)} %shard_map.51) | copy-start | bytes 3145732
  148.2 2.6 %copy-start.2 = (f32[64,128]{1,0:T(8,128)}, f32[64,128]{1,0:T(8,128)S(1)}, u32[]{:S(2)}) copy-start(f32[64,128]{1,0:T(8,128)S(1)} %multiply_add_fusion) | copy-start | bytes 98308
  150.9 59.8 %all-to-all-start.2 = ((bf16[256,32,128]{2,1,0:T(8,128)(2,1)}), bf16[256,32,128]{2,1,0:T(8,128)(2,1)S(1)}, u32[]{:S(2)}, u32[]{:S(2)}) async-start(bf16[256,32,128]{2,1,0:T(8,128)(2,1)} %bitcast.32), calls=%async_computation.2 | async-start | bytes 4194304 | tf_op jit(solution)/shard_map/all_to_all | solution.py:16

commit v11 on v10

--- a/solution.py
+++ b/solution.py
@@ -54,6 +54,39 @@
         out_shape=jax.ShapeDtypeStruct((count, width), dtype),
     )(index, wide)
     return picked
+
+
+def answer_kernel(index_ref, source_ref, out_ref):
+    chunks, depth, _ = out_ref.shape
+    capacity = index_ref.shape[0] // chunks
+    table_rows = source_ref.shape[0] - (depth - capacity)
+    extra = source_ref[pl.ds(table_rows, depth - capacity), :].astype(out_ref.dtype)
+
+    def body(chunk, carry):
+        for start in range(0, capacity, GATHER_TILE):
+            first = chunk * capacity + start
+            rows = [source_ref[pl.ds(index_ref[first + r], 1), :] for r in range(GATHER_TILE)]
+            out_ref[chunk, pl.ds(start, GATHER_TILE), :] = jnp.concatenate(rows, axis=0).astype(
+                out_ref.dtype
+            )
+        out_ref[chunk, pl.ds(capacity, depth - capacity), :] = extra
+        return carry
+
+    lax.fori_loop(0, chunks, body, 0, unroll=2)
+
+
+def answer_rows(wide, index, chunks, depth, dtype):
+    rows, width = wide.shape
+    return pl.pallas_call(
+        answer_kernel,
+        grid_spec=pltpu.PrefetchScalarGridSpec(
+            num_scalar_prefetch=1,
+            grid=(1,),
+            in_specs=[pl.BlockSpec((rows, width), lambda i, index_ref: (0, 0))],
+            out_specs=pl.BlockSpec((chunks, depth, width), lambda i, index_ref: (0, 0, 0)),
+        ),
+        out_shape=jax.ShapeDtypeStruct((chunks, depth, width), dtype),
+    )(index, wide)
 
 
 def on_device(item_table, histories, counts):
@@ -128,12 +161,8 @@
         [item_table.astype(f32), pieces.astype(f32).reshape(extra_rows, embed_width)], axis=0
     )
     reply_capacity = capacity + extra_rows
-    piece_ids = jnp.broadcast_to(
-        table_rows + jnp.arange(extra_rows, dtype=jnp.int32), (devices, extra_rows)
-    )
-    wanted = jnp.concatenate([incoming.reshape(devices, capacity), piece_ids], axis=1)
-    answered = gather_rows(source_rows, wanted.reshape(devices * reply_capacity), bf16)
-    replies = exchange(answered.reshape(devices, reply_capacity, embed_width))
+    answered = answer_rows(source_rows, incoming, devices, reply_capacity, bf16)
+    replies = exchange(answered)
     parts = replies[:, capacity:].reshape(devices, extra_rows * embed_width)[:, : 3 * gram_width]
     parts = parts.astype(f32).reshape(devices, 3, gram_width)
     gramian = ((parts[:, 0] + parts[:, 1]) + parts[:, 2]).reshape(embed_width, embed_width)

time: 222 us -> 215 us (0.968)
  blocking collectives: 0 us -> 87.9 us
  waiting for transfers between devices: 130 us -> 63.6 us
  starting transfers between devices: 27.6 us -> 5.55 us
  local copies, waits for them, and re-layouts: 9.78 us -> 4.86 us
    all_to_all x0 -> x2, blocking collectives: none -> 87.9 us  [exchange(): return lax.all_to_all(values, ('rows', 'grp'), 0, 0, tiled=True)]
    all_to_all x3 -> x1, waiting for transfers between devices: 130 us -> 63.6 us  [exchange(): return lax.all_to_all(values, ('rows', 'grp'), 0, 0, tiled=True)]
    all_to_all x3 -> x1, starting transfers between devices: 27.6 us -> 5.55 us  [exchange(): return lax.all_to_all(values, ('rows', 'grp'), 0, 0, tiled=True)]
    pallas_call x2 -> x1, Pallas kernels: 19.7 us -> 7.92 us  [gather_rows(): pl.pallas_call(gather_rows_kernel, grid_spec=pltpu.PrefetchScalarGridSpec...]
    pallas_call x0 -> x1, Pallas kernels: none -> 11.3 us  [answer_rows(): pl.pallas_call(answer_kernel, grid_spec=pltpu.PrefetchScalarGridSpec(num_...]
    reshape x2 -> x1, local copies, waits for them, and re-layouts: 5.47 us -> 0.71 us  [on_device(): incoming = received[:, :capacity].astype(jnp.int32).reshape(slots_total)]
  transfers between devices with their start and end apart: 3 -> 1, of which waited for: 3 -> 1; matrix products, arithmetic and copies ran while one was open for 1% -> 0% of each run, Pallas kernels for 0% -> 0%
where the time goes in v11:
time: 215 us; the launch traced here: 214 us
  blocking collectives  87.9 us (41%)
  waiting for transfers between devices  63.6 us (30%)
  matrix products  24.6 us (11%)
  Pallas kernels  19.2 us (9%)
  other arithmetic  7.4 us (3%)
  starting transfers between devices  5.55 us (3%)
  local copies, waits for them, and re-layouts  4.86 us (2%)
    all_to_all x2, blocking collectives, exchange(): return lax.all_to_all(values, ('rows', 'grp'), 0, 0, tiled=True)  87.9 us
    all_to_all x1, waiting for transfers between devices, exchange(): return lax.all_to_all(values, ('rows', 'grp'), 0, 0, tiled=True)  63.6 us
    pallas_call x1, Pallas kernels, answer_rows(): pl.pallas_call(answer_kernel, grid_spec=pltpu.PrefetchScalarGridSpec(num_...  11.3 us
    dot_general x1, matrix products, on_device(): jnp.einsum('st,sk->tk', picks, arrived, preferred_element_type=f32)  11 us
    pallas_call x1, Pallas kernels, gather_rows(): pl.pallas_call(gather_rows_kernel, grid_spec=pltpu.PrefetchScalarGridSpec...  7.92 us
    all_to_all x1, starting transfers between devices, exchange(): return lax.all_to_all(values, ('rows', 'grp'), 0, 0, tiled=True)  5.55 us
  transfers between devices with their start and end apart: 1, of which 1 were waited for; matrix products, arithmetic and copies ran while one was open for 0% of the time, Pallas kernels for 0%

profile of v11, /device:TPU:1, one launch (start us, length us, event | category | flops | bytes accessed | tf_op | source)
XLA Modules:
  0.0 214.1 jit_solution(8980401040193416829)
XLA Ops:
  0.6 0.0 copy-start
  0.7 0.8 fusion.74
  1.5 0.1 lt.34
  1.6 0.8 multiply_subtract_fusion.2
  2.4 0.1 reshape.342
  2.4 1.4 fusion.53
  3.8 1.4 fusion.5
  5.3 0.1 broadcast_in_dim.44
  5.4 0.0 copy-done
  5.4 0.3 fusion.95
  5.7 0.1 reshape.344
  5.8 0.1 reshape.343
  5.9 0.1 fusion.25
  6.0 0.1 copy.27
  6.1 3.2 %multiply_reduce_fusion = f32[64,64]{1,0:T(8,128)S(1)} fusion(f32[64,65]{1,0:T(8,128)S(1)} %fusion.72, bf16[64,1,256]{2,1,0:T(2,128)(2,1)S(1)} %copy.27, bf16[64,64,256]{2,1,0:T(8,128)(2,1)S(1)} %fusion.5, s32[64,64]{1,0:T(8,128)S(1)} %get-tuple-element.13, pred[64,64]{1,0:T(8,128)(4,1)S(1)} %get-tuple-element.17), kind=kOutput, calls=%fused_computation.24 | convolution fusion | flops 143200256 | bytes 2183424 | tf_op jit(solution)/shard_map/ujo,uko->ujk/dot_general | solution.py:119
  9.3 0.1 convert_element_type.111
  9.4 1.7 fusion.22
  11.1 0.1 copy.28
  11.2 0.1 pad_maximum_fusion
  11.3 28.3 %all_to_all.22 = f32[256,1,96]{2,1,0:T(1,128)S(1)} all-to-all(f32[256,1,96]{2,1,0:T(1,128)S(1)} %bitcast.88), channel_id=1, replica_groups=mesh['rows'=32,'grp'=8] {'rows','grp'}, dimensions={0} | all-to-all | bytes 196608 | tf_op jit(solution)/shard_map/all_to_all | solution.py:16
  39.6 0.1 slice_reduce_fusion
  39.7 0.7 reshape.345.index_ref
  40.5 0.1 fusion.87
  40.6 1.0 maximum_convert_fusion.source_ref
  41.6 11.3 %shard_map.50 = bf16[256,34,128]{2,1,0:T(8,128)(2,1)} custom-call(s32[8192]{0:T(1024)} %reshape.345.index_ref, f32[1986,128]{1,0:T(8,128)} %maximum_convert_fusion.source_ref), custom_call_target="tpu_custom_call" | custom-call | tf_op jit(solution)/shard_map/pallas_call | solution.py:80
  52.9 5.5 %all-to-all-start.1 = ((bf16[256,34,128]{2,1,0:T(8,128)(2,1)}), bf16[256,34,128]{2,1,0:T(8,128)(2,1)S(1)}, u32[]{:S(2)}, u32[]{:S(2)}) async-start(bf16[256,34,128]{2,1,0:T(8,128)(2,1)} %shard_map.50), calls=%async_computation.1 | async-start | bytes 5242880 | tf_op jit(solution)/shard_map/all_to_all | solution.py:16
  58.5 0.1 copy.33
  58.6 0.1 gt.16
  58.7 0.1 copy.32
  58.8 0.1 eq.102
  58.9 0.6 multiply_add_fusion.3.index_ref
  59.5 63.6 %all-to-all-done.1 = bf16[256,34,128]{2,1,0:T(8,128)(2,1)S(1)} async-done(((bf16[256,34,128]{2,1,0:T(8,128)(2,1)}), bf16[256,34,128]{2,1,0:T(8,128)(2,1)S(1)}, u32[]{:S(2)}, u32[]{:S(2)}) %all-to-all-start.1) | async-done | bytes 2228256 | tf_op jit(solution)/shard_map/all_to_all | solution.py:16
  123.2 0.1 slice.48
  123.3 0.1 copy.48
  123.4 0.1 copy.31
  123.5 0.1 add.76
  123.6 2.7 %reshape.353.source_ref = f32[8704,128]{1,0:T(8,128)} reshape(bf16[256,34,128]{2,1,0:T(8,128)(2,1)S(1)} %all-to-all-done.1) | data formatting | bytes 6684672 | tf_op jit(solution)/shard_map/convert_element_type | solution.py:171
  126.3 7.9 %shard_map.51 = bf16[4096,128]{1,0:T(8,128)(2,1)} custom-call(s32[4096]{0:T(1024)} %multiply_add_fusion.3.index_ref, f32[8704,128]{1,0:T(8,128)} %reshape.353.source_ref), custom_call_target="tpu_custom_call" | custom-call | tf_op jit(solution)/shard_map/pallas_call | solution.py:46
  134.3 1.7 fusion.68
  135.9 1.9 fusion.66
  137.8 0.0 copy-done.4
  137.8 0.1 fusion.75
  137.9 0.0 copy-done.1
  137.9 0.4 fusion.64
  138.3 0.3 multiply_reduce_fusion.4
  138.6 0.2 multiply_reduce_fusion.3
  138.8 0.1 convert_bitcast_fusion.1
  138.9 0.6 fusion.62
  139.5 0.1 fusion.76
  139.6 0.4 fusion.60
  140.0 0.3 multiply_reduce_fusion.2
  140.3 0.2 multiply_reduce_fusion.1
  140.5 0.1 convert_bitcast_fusion
  140.6 0.6 fusion.58
  141.3 0.1 fusion.77
  141.3 0.4 fusion.56
  141.7 0.3 fusion.33
  142.1 0.1 multiply_add_fusion
  142.2 0.0 copy-start.3
  142.2 1.3 convolution_convert_fusion
  143.5 0.0 copy-start.2
  143.5 59.6 %all_to_all.23 = bf16[256,32,128]{2,1,0:T(8,128)(2,1)S(1)} all-to-all(bf16[256,32,128]{2,1,0:T(8,128)(2,1)S(1)} %bitcast.72), channel_id=1, replica_groups=mesh['rows'=32,'grp'=8] {'rows','grp'}, dimensions={0} | all-to-all | bytes 4194304 | tf_op jit(solution)/shard_map/all_to_all | solution.py:16
  203.1 0.0 copy-done.2
  203.1 11.0 %fusion = f32[1984,128]{1,0:T(8,128)} fusion(bf16[8192,128]{1,0:T(8,128)(2,1)S(1)} %bitcast.73, s32[8192]{0:T(1024)S(1)} %copy-done.2), kind=kOutput, calls=%fused_computation.1 | convolution fusion | flops 4177002496 | bytes 3145728 | tf_op jit(solution)/shard_map/st,sk->tk/dot_general | solution.py:203
  (26 shorter events, 0.2 us)
Async XLA Ops:
  0.6 4.7 %copy-start = (bf16[1984,128]{1,0:T(8,128)(2,1)S(1)}, bf16[1984,128]{1,0:T(8,128)(2,1)}, u32[]{:S(2)}) copy-start(bf16[1984,128]{1,0:T(8,128)(2,1)} %param.3) | copy-start | bytes 1523716
  52.9 70.3 %all-to-all-start.1 = ((bf16[256,34,128]{2,1,0:T(8,128)(2,1)}), bf16[256,34,128]{2,1,0:T(8,128)(2,1)S(1)}, u32[]{:S(2)}, u32[]{:S(2)}) async-start(bf16[256,34,128]{2,1,0:T(8,128)(2,1)} %shard_map.50), calls=%async_computation.1 | async-start | bytes 5242880 | tf_op jit(solution)/shard_map/all_to_all | solution.py:16
  134.2 3.6 %copy-start.4 = (s32[64]{0:T(128)S(1)}, s32[64]{0:T(128)}, u32[]{:S(2)}) copy-start(s32[64]{0:T(128)} %param.5) | copy-start | bytes 772
  134.2 3.7 %copy-start.1 = (bf16[4096,128]{1,0:T(8,128)(2,1)S(1)}, bf16[4096,128]{1,0:T(8,128)(2,1)}, u32[]{:S(2)}) copy-start(bf16[4096,128]{1,0:T(8,128)(2,1)} %shard_map.51) | copy-start | bytes 3145732
  142.2 60.9 %copy-start.3 = (f32[64,128]{1,0:T(8,128)}, f32[64,128]{1,0:T(8,128)S(1)}, u32[]{:S(2)}) copy-start(f32[64,128]{1,0:T(8,128)S(1)} %multiply_add_fusion) | copy-start | bytes 98308
  143.5 59.6 %copy-start.2 = (s32[8192]{0:T(1024)S(1)}, s32[8192]{0:T(1024)}, u32[]{:S(2)}) copy-start(s32[8192]{0:T(1024)} %reshape.345.index_ref) | copy-start | bytes 98308

commit v12 on v11

--- a/solution.py
+++ b/solution.py
@@ -37,7 +37,7 @@
         out_ref[pl.ds(first, GATHER_TILE), :] = jnp.concatenate(rows, axis=0).astype(out_ref.dtype)
         return carry
 
-    lax.fori_loop(0, out_ref.shape[0] // GATHER_TILE, body, 0, unroll=4)
+    lax.fori_loop(0, out_ref.shape[0] // GATHER_TILE, body, 0, unroll=8)
 
 
 def gather_rows(wide, index, dtype):
@@ -72,7 +72,7 @@
         out_ref[chunk, pl.ds(capacity, depth - capacity), :] = extra
         return carry
 
-    lax.fori_loop(0, chunks, body, 0, unroll=2)
+    lax.fori_loop(0, chunks, body, 0, unroll=4)
 
 
 def answer_rows(wide, index, chunks, depth, dtype):
@@ -120,7 +120,7 @@
     slot_ids = lax.broadcasted_iota(jnp.int32, (history_length, history_length + 1), 0)
     other_ids = lax.broadcasted_iota(jnp.int32, (history_length, history_length + 1), 1)
     counted = ((other_ids < slot_ids) | (other_ids == history_length)).astype(f32)
-    ranks = jnp.sum(same * counted[None], axis=2).astype(jnp.int32).reshape(lookups)
+    ranks = jnp.einsum("ujk,jk->uj", same, counted).astype(jnp.int32).reshape(lookups)
 
     flat_rows = local_rows.reshape(lookups, 1)
     row_high = flat_rows // 32

time: 215 us -> 214 us (level)
  no operation moved by 1% of the time
where the time goes in v12:
time: 214 us; the launch traced here: 213 us
  blocking collectives  87.9 us (41%)
  waiting for transfers between devices  63.6 us (30%)
  matrix products  24 us (11%)
  Pallas kernels  18.6 us (9%)
  other arithmetic  7.41 us (3%)
  starting transfers between devices  5.56 us (3%)
  local copies, waits for them, and re-layouts  4.93 us (2%)
    all_to_all x2, blocking collectives, exchange(): return lax.all_to_all(values, ('rows', 'grp'), 0, 0, tiled=True)  87.9 us
    all_to_all x1, waiting for transfers between devices, exchange(): return lax.all_to_all(values, ('rows', 'grp'), 0, 0, tiled=True)  63.6 us
    dot_general x1, matrix products, on_device(): jnp.einsum('st,sk->tk', picks, arrived, preferred_element_type=f32)  11 us
    pallas_call x1, Pallas kernels, answer_rows(): pl.pallas_call(answer_kernel, grid_spec=pltpu.PrefetchScalarGridSpec(num_...  10.9 us
    pallas_call x1, Pallas kernels, gather_rows(): pl.pallas_call(gather_rows_kernel, grid_spec=pltpu.PrefetchScalarGridSpec...  7.75 us
    all_to_all x1, starting transfers between devices, exchange(): return lax.all_to_all(values, ('rows', 'grp'), 0, 0, tiled=True)  5.56 us
  transfers between devices with their start and end apart: 1, of which 1 were waited for; matrix products, arithmetic and copies ran while one was open for 0% of the time, Pallas kernels for 0%

profile of v12, /device:TPU:1, one launch (start us, length us, event | category | flops | bytes accessed | tf_op | source)
XLA Modules:
  0.0 213.0 jit_solution(4903773030028486778)
XLA Ops:
  0.6 0.0 copy-start
  0.7 0.8 fusion.74
  1.5 0.1 lt.30
  1.6 0.8 multiply_subtract_fusion.2
  2.4 0.1 reshape.314
  2.4 1.4 fusion.51
  3.8 1.4 fusion.5
  5.3 0.1 broadcast_in_dim.43
  5.4 0.0 copy-done
  5.4 0.3 fusion.95
  5.7 0.1 reshape.317
  5.8 0.1 reshape.316
  5.9 0.1 fusion.27
  6.0 0.1 copy.27
  6.1 1.9 fusion.3
  8.0 0.8 fusion.15
  8.8 0.1 copy.36
  8.9 0.1 reshape.315
  9.0 1.7 fusion.24
  10.7 0.1 copy.28
  10.8 0.1 pad_maximum_fusion
  10.9 28.3 %all_to_all.22 = f32[256,1,96]{2,1,0:T(1,128)S(1)} all-to-all(f32[256,1,96]{2,1,0:T(1,128)S(1)} %bitcast.96), channel_id=1, replica_groups=mesh['rows'=32,'grp'=8] {'rows','grp'}, dimensions={0} | all-to-all | bytes 196608 | tf_op jit(solution)/shard_map/all_to_all | solution.py:16
  39.2 0.1 slice_reduce_fusion
  39.3 0.7 reshape.318.index_ref
  40.0 0.1 fusion.87
  40.1 1.0 maximum_convert_fusion.source_ref
  41.2 10.9 %shard_map.50 = bf16[256,34,128]{2,1,0:T(8,128)(2,1)} custom-call(s32[8192]{0:T(1024)} %reshape.318.index_ref, f32[1986,128]{1,0:T(8,128)} %maximum_convert_fusion.source_ref), custom_call_target="tpu_custom_call" | custom-call | tf_op jit(solution)/shard_map/pallas_call | solution.py:80
  52.0 5.6 %all-to-all-start.1 = ((bf16[256,34,128]{2,1,0:T(8,128)(2,1)}), bf16[256,34,128]{2,1,0:T(8,128)(2,1)S(1)}, u32[]{:S(2)}, u32[]{:S(2)}) async-start(bf16[256,34,128]{2,1,0:T(8,128)(2,1)} %shard_map.50), calls=%async_computation.1 | async-start | bytes 5242880 | tf_op jit(solution)/shard_map/all_to_all | solution.py:16
  57.6 0.1 copy.33
  57.7 0.1 gt.16
  57.9 0.1 copy.32
  58.0 0.1 eq.102
  58.1 0.6 multiply_add_fusion.3.index_ref
  58.7 63.6 %all-to-all-done.1 = bf16[256,34,128]{2,1,0:T(8,128)(2,1)S(1)} async-done(((bf16[256,34,128]{2,1,0:T(8,128)(2,1)}), bf16[256,34,128]{2,1,0:T(8,128)(2,1)S(1)}, u32[]{:S(2)}, u32[]{:S(2)}) %all-to-all-start.1) | async-done | bytes 2228256 | tf_op jit(solution)/shard_map/all_to_all | solution.py:16
  122.3 0.1 slice.48
  122.4 0.1 copy.51
  122.6 0.1 copy.31
  122.6 0.1 add.76
  122.7 2.7 %reshape.326.source_ref = f32[8704,128]{1,0:T(8,128)} reshape(bf16[256,34,128]{2,1,0:T(8,128)(2,1)S(1)} %all-to-all-done.1) | data formatting | bytes 6684672 | tf_op jit(solution)/shard_map/convert_element_type | solution.py:171
  125.4 7.8 %shard_map.51 = bf16[4096,128]{1,0:T(8,128)(2,1)} custom-call(s32[4096]{0:T(1024)} %multiply_add_fusion.3.index_ref, f32[8704,128]{1,0:T(8,128)} %reshape.326.source_ref), custom_call_target="tpu_custom_call" | custom-call | tf_op jit(solution)/shard_map/pallas_call | solution.py:46
  133.2 1.7 fusion.68
  134.9 1.9 fusion.66
  136.8 0.1 fusion.75
  136.8 0.0 copy-done.1
  136.9 0.4 fusion.64
  137.3 0.3 multiply_reduce_fusion.3
  137.6 0.2 multiply_reduce_fusion.2
  137.8 0.1 convert_bitcast_fusion.1
  137.9 0.6 fusion.62
  138.5 0.1 fusion.76
  138.6 0.4 fusion.60
  139.0 0.3 multiply_reduce_fusion.1
  139.3 0.2 multiply_reduce_fusion
  139.5 0.1 convert_bitcast_fusion
  139.6 0.6 fusion.58
  140.2 0.1 fusion.77
  140.3 0.4 fusion.56
  140.7 0.3 fusion.35
  141.0 0.1 multiply_add_fusion
  141.1 0.0 copy-start.3
  141.1 1.3 convolution_convert_fusion
  142.4 0.0 copy-start.2
  142.4 59.6 %all_to_all.23 = bf16[256,32,128]{2,1,0:T(8,128)(2,1)S(1)} all-to-all(bf16[256,32,128]{2,1,0:T(8,128)(2,1)S(1)} %bitcast.80), channel_id=1, replica_groups=mesh['rows'=32,'grp'=8] {'rows','grp'}, dimensions={0} | all-to-all | bytes 4194304 | tf_op jit(solution)/shard_map/all_to_all | solution.py:16
  202.0 11.0 %fusion = f32[1984,128]{1,0:T(8,128)} fusion(bf16[8192,128]{1,0:T(8,128)(2,1)S(1)} %bitcast.81, s32[8192]{0:T(1024)S(1)} %copy-done.2), kind=kOutput, calls=%fused_computation.1 | convolution fusion | flops 4177002496 | bytes 3145728 | tf_op jit(solution)/shard_map/st,sk->tk/dot_general | solution.py:203
  (28 shorter events, 0.2 us)
Async XLA Ops:
  0.6 4.7 %copy-start = (bf16[1984,128]{1,0:T(8,128)(2,1)S(1)}, bf16[1984,128]{1,0:T(8,128)(2,1)}, u32[]{:S(2)}) copy-start(bf16[1984,128]{1,0:T(8,128)(2,1)} %param.3) | copy-start | bytes 1523716
  52.0 70.3 %all-to-all-start.1 = ((bf16[256,34,128]{2,1,0:T(8,128)(2,1)}), bf16[256,34,128]{2,1,0:T(8,128)(2,1)S(1)}, u32[]{:S(2)}, u32[]{:S(2)}) async-start(bf16[256,34,128]{2,1,0:T(8,128)(2,1)} %shard_map.50), calls=%async_computation.1 | async-start | bytes 5242880 | tf_op jit(solution)/shard_map/all_to_all | solution.py:16
  133.2 3.6 %copy-start.4 = (s32[64]{0:T(128)S(1)}, s32[64]{0:T(128)}, u32[]{:S(2)}) copy-start(s32[64]{0:T(128)} %param.5) | copy-start | bytes 772
  133.2 3.7 %copy-start.1 = (bf16[4096,128]{1,0:T(8,128)(2,1)S(1)}, bf16[4096,128]{1,0:T(8,128)(2,1)}, u32[]{:S(2)}) copy-start(bf16[4096,128]{1,0:T(8,128)(2,1)} %shard_map.51) | copy-start | bytes 3145732
  141.1 60.9 %copy-start.3 = (f32[64,128]{1,0:T(8,128)}, f32[64,128]{1,0:T(8,128)S(1)}, u32[]{:S(2)}) copy-start(f32[64,128]{1,0:T(8,128)S(1)} %multiply_add_fusion) | copy-start | bytes 98308
  142.4 59.6 %copy-start.2 = (s32[8192]{0:T(1024)S(1)}, s32[8192]{0:T(1024)}, u32[]{:S(2)}) copy-start(s32[8192]{0:T(1024)} %reshape.318.index_ref) | copy-start | bytes 98308

commit v13 on v12

--- a/solution.py
+++ b/solution.py
@@ -87,6 +87,36 @@
         ),
         out_shape=jax.ShapeDtypeStruct((chunks, depth, width), dtype),
     )(index, wide)
+
+
+def fetch_kernel(owner_ref, rank_ref, source_ref, out_ref, wide_ref):
+    wide_ref[...] = source_ref[...].astype(jnp.float32)
+
+    def body(tile, carry):
+        first = pl.multiple_of(tile * GATHER_TILE, GATHER_TILE)
+        rows = [
+            wide_ref[owner_ref[first + r], pl.ds(rank_ref[first + r], 1), :]
+            for r in range(GATHER_TILE)
+        ]
+        out_ref[pl.ds(first, GATHER_TILE), :] = jnp.concatenate(rows, axis=0).astype(out_ref.dtype)
+        return carry
+
+    lax.fori_loop(0, out_ref.shape[0] // GATHER_TILE, body, 0, unroll=8)
+
+
+def fetch_rows(source, owner, rank):
+    count = owner.shape[0]
+    return pl.pallas_call(
+        fetch_kernel,
+        grid_spec=pltpu.PrefetchScalarGridSpec(
+            num_scalar_prefetch=2,
+            grid=(1,),
+            in_specs=[pl.BlockSpec(source.shape, lambda i, owner_ref, rank_ref: (0, 0, 0))],
+            out_specs=pl.BlockSpec((count, source.shape[2]), lambda i, owner_ref, rank_ref: (0, 0)),
+            scratch_shapes=[pltpu.VMEM(source.shape, jnp.float32)],
+        ),
+        out_shape=jax.ShapeDtypeStruct((count, source.shape[2]), source.dtype),
+    )(owner, rank, source)
 
 
 def on_device(item_table, histories, counts):
@@ -166,9 +196,7 @@
     parts = replies[:, capacity:].reshape(devices, extra_rows * embed_width)[:, : 3 * gram_width]
     parts = parts.astype(f32).reshape(devices, 3, gram_width)
     gramian = ((parts[:, 0] + parts[:, 1]) + parts[:, 2]).reshape(embed_width, embed_width)
-    reply_rows = replies.reshape(devices * reply_capacity, embed_width)
-    slot_index = owners.reshape(lookups) * reply_capacity + ranks
-    fetched = gather_rows(reply_rows.astype(f32), slot_index, bf16).reshape(
+    fetched = fetch_rows(replies, owners.reshape(lookups), ranks).reshape(
         user_count, history_length, embed_width
     )
     weights = live.astype(f32)

time: 214 us -> 216 us (level)
  Pallas kernels: 18.6 us -> 22.1 us
    pallas_call x1, Pallas kernels: 7.75 us -> 11.2 us  [fetch_rows(): pl.pallas_call(fetch_kernel, grid_spec=pltpu.PrefetchScalarGridSpec(num_s...]
    convert_element_type x1 -> x0, local copies, waits for them, and re-layouts: 2.71 us -> none  [on_device(): reply_rows.astype(f32)]
where the time goes in v13:
time: 216 us; the launch traced here: 215 us
  blocking collectives  87.9 us (41%)
  waiting for transfers between devices  64.2 us (30%)
  matrix products  24 us (11%)
  Pallas kernels  22.1 us (10%)
  other arithmetic  6.81 us (3%)
  starting transfers between devices  5.56 us (3%)
  local copies, waits for them, and re-layouts  3.53 us (2%)
    all_to_all x2, blocking collectives, exchange(): return lax.all_to_all(values, ('rows', 'grp'), 0, 0, tiled=True)  87.9 us
    all_to_all x1, waiting for transfers between devices, exchange(): return lax.all_to_all(values, ('rows', 'grp'), 0, 0, tiled=True)  64.2 us
    pallas_call x1, Pallas kernels, fetch_rows(): pl.pallas_call(fetch_kernel, grid_spec=pltpu.PrefetchScalarGridSpec(num_s...  11.2 us
    dot_general x1, matrix products, on_device(): jnp.einsum('st,sk->tk', picks, arrived, preferred_element_type=f32)  11 us
    pallas_call x1, Pallas kernels, answer_rows(): pl.pallas_call(answer_kernel, grid_spec=pltpu.PrefetchScalarGridSpec(num_...  10.9 us
    all_to_all x1, starting transfers between devices, exchange(): return lax.all_to_all(values, ('rows', 'grp'), 0, 0, tiled=True)  5.56 us
  transfers between devices with their start and end apart: 1, of which 1 were waited for; matrix products, arithmetic and copies ran while one was open for 0% of the time, Pallas kernels for 0%

profile of v13, /device:TPU:1, one launch (start us, length us, event | category | flops | bytes accessed | tf_op | source)
XLA Modules:
  0.0 215.1 jit_solution(16754874718243261335)
XLA Ops:
  0.6 0.0 copy-start.1
  0.7 0.8 fusion.74
  1.5 0.1 lt.30
  1.6 0.8 multiply_subtract_fusion.2
  2.4 0.1 reshape.311.owner_ref
  2.4 1.4 fusion.51
  3.9 1.4 fusion.5
  5.3 0.1 broadcast_in_dim.43
  5.4 0.0 copy-done.1
  5.4 0.3 fusion.95
  5.7 0.1 reshape.314
  5.8 0.1 reshape.313
  5.9 0.1 fusion.27
  6.0 0.1 copy.27
  6.1 1.9 fusion.3
  8.0 0.8 fusion.15
  8.8 0.1 copy.36
  8.9 0.1 reshape.312.rank_ref
  9.0 0.0 copy-done.5
  9.0 1.7 fusion.24
  10.7 0.1 copy.28
  10.8 0.1 pad_maximum_fusion
  10.9 28.3 %all_to_all.22 = f32[256,1,96]{2,1,0:T(1,128)S(1)} all-to-all(f32[256,1,96]{2,1,0:T(1,128)S(1)} %bitcast.96), channel_id=1, replica_groups=mesh['rows'=32,'grp'=8] {'rows','grp'}, dimensions={0} | all-to-all | bytes 196608 | tf_op jit(solution)/shard_map/all_to_all | solution.py:16
  39.2 0.1 slice_reduce_fusion
  39.3 0.7 reshape.315.index_ref
  40.1 0.1 fusion.87
  40.1 1.0 maximum_convert_fusion.source_ref
  41.2 10.9 %shard_map.50 = bf16[256,34,128]{2,1,0:T(8,128)(2,1)} custom-call(s32[8192]{0:T(1024)} %reshape.315.index_ref, f32[1986,128]{1,0:T(8,128)} %maximum_convert_fusion.source_ref), custom_call_target="tpu_custom_call" | custom-call | tf_op jit(solution)/shard_map/pallas_call | solution.py:80
  52.1 5.6 %all-to-all-start.1 = ((bf16[256,34,128]{2,1,0:T(8,128)(2,1)}), bf16[256,34,128]{2,1,0:T(8,128)(2,1)S(1)}, u32[]{:S(2)}, u32[]{:S(2)}) async-start(bf16[256,34,128]{2,1,0:T(8,128)(2,1)} %shard_map.50), calls=%async_computation.1 | async-start | bytes 5242880 | tf_op jit(solution)/shard_map/all_to_all | solution.py:16
  57.6 0.1 copy.33
  57.8 0.1 gt.16
  57.9 0.1 copy.32
  58.0 0.1 eq.102
  58.1 64.2 %all-to-all-done.1.source_ref = bf16[256,34,128]{2,1,0:T(8,128)(2,1)S(1)} async-done(((bf16[256,34,128]{2,1,0:T(8,128)(2,1)}), bf16[256,34,128]{2,1,0:T(8,128)(2,1)S(1)}, u32[]{:S(2)}, u32[]{:S(2)}) %all-to-all-start.1) | async-done | bytes 2228256 | tf_op jit(solution)/shard_map/all_to_all | solution.py:16
  122.3 0.1 slice.48
  122.4 0.1 copy.51
  122.5 1.3 copy-done
  123.8 11.2 %shard_map.51 = bf16[4096,128]{1,0:T(8,128)(2,1)} custom-call(s32[4096]{0:T(1024)} %copy-done.5, s32[4096]{0:T(1024)} %copy-done.6, bf16[256,34,128]{2,1,0:T(8,128)(2,1)} %copy-done), custom_call_target="tpu_custom_call" | custom-call | tf_op jit(solution)/shard_map/pallas_call | solution.py:109
  135.0 1.7 fusion.68
  136.7 1.9 fusion.66
  138.6 0.1 fusion.75
  138.7 0.0 copy-done.2
  138.7 0.4 fusion.64
  139.1 0.1 copy.31
  139.2 0.1 add.72
  139.3 0.3 multiply_reduce_fusion.3
  139.6 0.2 multiply_reduce_fusion.2
  139.8 0.1 convert_bitcast_fusion.1
  139.9 0.6 fusion.62
  140.5 0.1 fusion.76
  140.6 0.4 fusion.60
  141.0 0.3 multiply_reduce_fusion.1
  141.3 0.2 multiply_reduce_fusion
  141.5 0.1 convert_bitcast_fusion
  141.6 0.6 fusion.58
  142.3 0.1 fusion.77
  142.4 0.4 fusion.56
  142.8 0.3 fusion.35
  143.1 0.1 multiply_add_fusion
  143.2 0.0 copy-start.4
  143.2 1.3 convolution_convert_fusion
  144.5 0.0 copy-start.3
  144.5 59.6 %all_to_all.23 = bf16[256,32,128]{2,1,0:T(8,128)(2,1)S(1)} all-to-all(bf16[256,32,128]{2,1,0:T(8,128)(2,1)S(1)} %bitcast.80), channel_id=1, replica_groups=mesh['rows'=32,'grp'=8] {'rows','grp'}, dimensions={0} | all-to-all | bytes 4194304 | tf_op jit(solution)/shard_map/all_to_all | solution.py:16
  204.1 11.0 %fusion = f32[1984,128]{1,0:T(8,128)} fusion(bf16[8192,128]{1,0:T(8,128)(2,1)S(1)} %bitcast.81, s32[8192]{0:T(1024)S(1)} %copy-done.3), kind=kOutput, calls=%fused_computation.1 | convolution fusion | flops 4177002496 | bytes 3145728 | tf_op jit(solution)/shard_map/st,sk->tk/dot_general | solution.py:231
  (32 shorter events, 0.2 us)
Async XLA Ops:
  0.6 4.7 %copy-start.1 = (bf16[1984,128]{1,0:T(8,128)(2,1)S(1)}, bf16[1984,128]{1,0:T(8,128)(2,1)}, u32[]{:S(2)}) copy-start(bf16[1984,128]{1,0:T(8,128)(2,1)} %param.3) | copy-start | bytes 1523716
  2.4 6.6 %copy-start.5 = (s32[4096]{0:T(1024)}, s32[4096]{0:T(1024)S(1)}, u32[]{:S(2)}) copy-start(s32[4096]{0:T(1024)S(1)} %reshape.311.owner_ref) | copy-start | bytes 49156
  9.0 1.7 copy-start.6
  52.1 70.3 %all-to-all-start.1 = ((bf16[256,34,128]{2,1,0:T(8,128)(2,1)}), bf16[256,34,128]{2,1,0:T(8,128)(2,1)S(1)}, u32[]{:S(2)}, u32[]{:S(2)}) async-start(bf16[256,34,128]{2,1,0:T(8,128)(2,1)} %shard_map.50), calls=%async_computation.1 | async-start | bytes 5242880 | tf_op jit(solution)/shard_map/all_to_all | solution.py:16
  122.3 1.5 copy-start
  123.8 14.8 %copy-start.7 = (s32[64]{0:T(128)S(1)}, s32[64]{0:T(128)}, u32[]{:S(2)}) copy-start(s32[64]{0:T(128)} %param.5) | copy-start | bytes 772
  135.0 3.7 %copy-start.2 = (bf16[4096,128]{1,0:T(8,128)(2,1)S(1)}, bf16[4096,128]{1,0:T(8,128)(2,1)}, u32[]{:S(2)}) copy-start(bf16[4096,128]{1,0:T(8,128)(2,1)} %shard_map.51) | copy-start | bytes 3145732
  143.2 60.9 %copy-start.4 = (f32[64,128]{1,0:T(8,128)}, f32[64,128]{1,0:T(8,128)S(1)}, u32[]{:S(2)}) copy-start(f32[64,128]{1,0:T(8,128)S(1)} %multiply_add_fusion) | copy-start | bytes 98308
  144.5 59.6 %copy-start.3 = (s32[8192]{0:T(1024)S(1)}, s32[8192]{0:T(1024)}, u32[]{:S(2)}) copy-start(s32[8192]{0:T(1024)} %reshape.315.index_ref) | copy-start | bytes 98308

commit v14 on v12

--- a/solution.py
+++ b/solution.py
@@ -198,9 +198,9 @@
     partials = jnp.einsum("su,uk->sk", member, solution.astype(bf16), preferred_element_type=f32)
     partials = partials.astype(bf16).reshape(devices, capacity, embed_width)
     arrived = exchange(partials).reshape(slots_total, embed_width)
-    table_ids = lax.broadcasted_iota(jnp.int32, (slots_total, table_rows), 1)
-    picks = (incoming[:, None] == table_ids).astype(bf16)
-    item_rhs = jnp.einsum("st,sk->tk", picks, arrived, preferred_element_type=f32)
+    table_ids = lax.broadcasted_iota(jnp.int32, (table_rows, slots_total), 0)
+    picks = (table_ids == incoming[None, :]).astype(bf16)
+    item_rhs = jnp.dot(picks, arrived, preferred_element_type=f32)
     return (solution, item_rhs)
 
 

time: 214 us -> 214 us (level)
  no operation moved by 1% of the time
where the time goes in v14:
time: 214 us; the launch traced here: 213 us
  blocking collectives  87.9 us (41%)
  waiting for transfers between devices  63.6 us (30%)
  matrix products  24 us (11%)
  Pallas kernels  18.6 us (9%)
  other arithmetic  7.41 us (3%)
  starting transfers between devices  5.56 us (3%)
  local copies, waits for them, and re-layouts  4.93 us (2%)
    all_to_all x2, blocking collectives, exchange(): return lax.all_to_all(values, ('rows', 'grp'), 0, 0, tiled=True)  87.9 us
    all_to_all x1, waiting for transfers between devices, exchange(): return lax.all_to_all(values, ('rows', 'grp'), 0, 0, tiled=True)  63.6 us
    dot_general x1, matrix products, on_device(): item_rhs = jnp.dot(picks, arrived, preferred_element_type=f32)  11 us
    pallas_call x1, Pallas kernels, answer_rows(): pl.pallas_call(answer_kernel, grid_spec=pltpu.PrefetchScalarGridSpec(num_...  10.9 us
    pallas_call x1, Pallas kernels, gather_rows(): pl.pallas_call(gather_rows_kernel, grid_spec=pltpu.PrefetchScalarGridSpec...  7.75 us
    all_to_all x1, starting transfers between devices, exchange(): return lax.all_to_all(values, ('rows', 'grp'), 0, 0, tiled=True)  5.56 us
  transfers between devices with their start and end apart: 1, of which 1 were waited for; matrix products, arithmetic and copies ran while one was open for 0% of the time, Pallas kernels for 0%

profile of v14, /device:TPU:1, one launch (start us, length us, event | category | flops | bytes accessed | tf_op | source)
XLA Modules:
  0.0 213.0 jit_solution(16727931307741689945)
XLA Ops:
  0.6 0.0 copy-start
  0.7 0.8 fusion.74
  1.5 0.1 lt.30
  1.6 0.8 multiply_subtract_fusion.2
  2.4 0.1 reshape.314
  2.4 1.4 fusion.51
  3.8 1.4 fusion.5
  5.3 0.1 broadcast_in_dim.43
  5.4 0.3 fusion.95
  5.7 0.1 reshape.317
  5.8 0.1 reshape.316
  5.9 0.1 fusion.27
  6.0 0.1 copy.20
  6.1 1.9 fusion.3
  8.0 0.8 fusion.15
  8.8 0.1 copy.29
  8.9 0.1 reshape.315
  9.0 1.7 fusion.24
  10.7 0.1 copy.21
  10.8 0.1 pad_maximum_fusion
  10.9 28.3 %all_to_all.22 = f32[256,1,96]{2,1,0:T(1,128)S(1)} all-to-all(f32[256,1,96]{2,1,0:T(1,128)S(1)} %bitcast.96), channel_id=1, replica_groups=mesh['rows'=32,'grp'=8] {'rows','grp'}, dimensions={0} | all-to-all | bytes 196608 | tf_op jit(solution)/shard_map/all_to_all | solution.py:16
  39.2 0.1 slice_reduce_fusion
  39.3 0.7 reshape.318.index_ref
  40.0 0.1 fusion.87
  40.1 1.0 maximum_convert_fusion.source_ref
  41.2 10.9 %shard_map.50 = bf16[256,34,128]{2,1,0:T(8,128)(2,1)} custom-call(s32[8192]{0:T(1024)} %reshape.318.index_ref, f32[1986,128]{1,0:T(8,128)} %maximum_convert_fusion.source_ref), custom_call_target="tpu_custom_call" | custom-call | tf_op jit(solution)/shard_map/pallas_call | solution.py:80
  52.0 5.6 %all-to-all-start.1 = ((bf16[256,34,128]{2,1,0:T(8,128)(2,1)}), bf16[256,34,128]{2,1,0:T(8,128)(2,1)S(1)}, u32[]{:S(2)}, u32[]{:S(2)}) async-start(bf16[256,34,128]{2,1,0:T(8,128)(2,1)} %shard_map.50), calls=%async_computation.1 | async-start | bytes 5242880 | tf_op jit(solution)/shard_map/all_to_all | solution.py:16
  57.6 0.1 copy.26
  57.7 0.1 gt.16
  57.9 0.1 copy.25
  58.0 0.1 eq.102
  58.1 0.6 multiply_add_fusion.3.index_ref
  58.7 63.6 %all-to-all-done.1 = bf16[256,34,128]{2,1,0:T(8,128)(2,1)S(1)} async-done(((bf16[256,34,128]{2,1,0:T(8,128)(2,1)}), bf16[256,34,128]{2,1,0:T(8,128)(2,1)S(1)}, u32[]{:S(2)}, u32[]{:S(2)}) %all-to-all-start.1) | async-done | bytes 2228256 | tf_op jit(solution)/shard_map/all_to_all | solution.py:16
  122.3 0.1 slice.48
  122.4 0.1 copy.44
  122.6 0.1 copy.24
  122.6 0.1 add.76
  122.7 2.7 %reshape.326.source_ref = f32[8704,128]{1,0:T(8,128)} reshape(bf16[256,34,128]{2,1,0:T(8,128)(2,1)S(1)} %all-to-all-done.1) | data formatting | bytes 6684672 | tf_op jit(solution)/shard_map/convert_element_type | solution.py:171
  125.4 7.8 %shard_map.51 = bf16[4096,128]{1,0:T(8,128)(2,1)} custom-call(s32[4096]{0:T(1024)} %multiply_add_fusion.3.index_ref, f32[8704,128]{1,0:T(8,128)} %reshape.326.source_ref), custom_call_target="tpu_custom_call" | custom-call | tf_op jit(solution)/shard_map/pallas_call | solution.py:46
  133.2 1.7 fusion.68
  134.9 1.9 fusion.66
  136.8 0.1 fusion.75
  136.8 0.0 copy-done.1
  136.9 0.4 fusion.64
  137.3 0.3 multiply_reduce_fusion.3
  137.6 0.2 multiply_reduce_fusion.2
  137.8 0.1 convert_bitcast_fusion.1
  137.9 0.6 fusion.62
  138.5 0.1 fusion.76
  138.6 0.4 fusion.60
  139.0 0.3 multiply_reduce_fusion.1
  139.3 0.2 multiply_reduce_fusion
  139.5 0.1 convert_bitcast_fusion
  139.6 0.6 fusion.58
  140.2 0.1 fusion.77
  140.3 0.4 fusion.56
  140.7 0.3 fusion.35
  141.0 0.1 multiply_add_fusion
  141.1 0.0 copy-start.3
  141.1 1.3 convolution_convert_fusion
  142.4 0.0 copy-start.2
  142.4 59.6 %all_to_all.23 = bf16[256,32,128]{2,1,0:T(8,128)(2,1)S(1)} all-to-all(bf16[256,32,128]{2,1,0:T(8,128)(2,1)S(1)} %bitcast.80), channel_id=1, replica_groups=mesh['rows'=32,'grp'=8] {'rows','grp'}, dimensions={0} | all-to-all | bytes 4194304 | tf_op jit(solution)/shard_map/all_to_all | solution.py:16
  202.0 0.0 copy-done.2
  202.0 11.0 %fusion = f32[1984,128]{1,0:T(8,128)} fusion(bf16[8192,128]{1,0:T(8,128)(2,1)S(1)} %bitcast.81, s32[8192]{0:T(1024)S(1)} %copy-done.2), kind=kOutput, calls=%fused_computation.1 | convolution fusion | flops 4177002496 | bytes 3145728 | tf_op jit(solution)/shard_map/dot_general | solution.py:203
  (28 shorter events, 0.2 us)
Async XLA Ops:
  0.6 4.7 %copy-start = (bf16[1984,128]{1,0:T(8,128)(2,1)S(1)}, bf16[1984,128]{1,0:T(8,128)(2,1)}, u32[]{:S(2)}) copy-start(bf16[1984,128]{1,0:T(8,128)(2,1)} %param.3) | copy-start | bytes 1523716
  52.0 70.3 %all-to-all-start.1 = ((bf16[256,34,128]{2,1,0:T(8,128)(2,1)}), bf16[256,34,128]{2,1,0:T(8,128)(2,1)S(1)}, u32[]{:S(2)}, u32[]{:S(2)}) async-start(bf16[256,34,128]{2,1,0:T(8,128)(2,1)} %shard_map.50), calls=%async_computation.1 | async-start | bytes 5242880 | tf_op jit(solution)/shard_map/all_to_all | solution.py:16
  133.2 3.6 %copy-start.4 = (s32[64]{0:T(128)S(1)}, s32[64]{0:T(128)}, u32[]{:S(2)}) copy-start(s32[64]{0:T(128)} %param.5) | copy-start | bytes 772
  133.2 3.7 %copy-start.1 = (bf16[4096,128]{1,0:T(8,128)(2,1)S(1)}, bf16[4096,128]{1,0:T(8,128)(2,1)}, u32[]{:S(2)}) copy-start(bf16[4096,128]{1,0:T(8,128)(2,1)} %shard_map.51) | copy-start | bytes 3145732
  141.1 60.9 %copy-start.3 = (f32[64,128]{1,0:T(8,128)}, f32[64,128]{1,0:T(8,128)S(1)}, u32[]{:S(2)}) copy-start(f32[64,128]{1,0:T(8,128)S(1)} %multiply_add_fusion) | copy-start | bytes 98308
  142.4 59.6 %copy-start.2 = (s32[8192]{0:T(1024)S(1)}, s32[8192]{0:T(1024)}, u32[]{:S(2)}) copy-start(s32[8192]{0:T(1024)} %reshape.318.index_ref) | copy-start | bytes 98308

commit v15 on v14

--- a/solution.py
+++ b/solution.py
@@ -163,6 +163,8 @@
     reply_capacity = capacity + extra_rows
     answered = answer_rows(source_rows, incoming, devices, reply_capacity, bf16)
     replies = exchange(answered)
+    table_ids = lax.broadcasted_iota(jnp.int32, (table_rows, slots_total), 0)
+    picks = lax.optimization_barrier((table_ids == incoming[None, :]).astype(bf16))
     parts = replies[:, capacity:].reshape(devices, extra_rows * embed_width)[:, : 3 * gram_width]
     parts = parts.astype(f32).reshape(devices, 3, gram_width)
     gramian = ((parts[:, 0] + parts[:, 1]) + parts[:, 2]).reshape(embed_width, embed_width)
@@ -198,8 +200,6 @@
     partials = jnp.einsum("su,uk->sk", member, solution.astype(bf16), preferred_element_type=f32)
     partials = partials.astype(bf16).reshape(devices, capacity, embed_width)
     arrived = exchange(partials).reshape(slots_total, embed_width)
-    table_ids = lax.broadcasted_iota(jnp.int32, (table_rows, slots_total), 0)
-    picks = (table_ids == incoming[None, :]).astype(bf16)
     item_rhs = jnp.dot(picks, arrived, preferred_element_type=f32)
     return (solution, item_rhs)
 

time: 214 us -> 220 us (1.028)
  blocking collectives: 87.9 us -> 28.3 us
  waiting for transfers between devices: 63.6 us -> 100 us
  other arithmetic: 7.41 us -> 24.3 us
  starting transfers between devices: 5.56 us -> 11.9 us
  matrix products: 24 us -> 29.9 us
    all_to_all x2 -> x1, blocking collectives: 87.9 us -> 28.3 us  [exchange(): return lax.all_to_all(values, ('rows', 'grp'), 0, 0, tiled=True)]
    all_to_all x1 -> x2, waiting for transfers between devices: 63.6 us -> 100 us  [exchange(): return lax.all_to_all(values, ('rows', 'grp'), 0, 0, tiled=True)]
    convert_element_type x0 -> x1, other arithmetic: none -> 16.9 us  [on_device(): (table_ids == incoming[None, :]).astype(bf16)]
    all_to_all x1 -> x2, starting transfers between devices: 5.56 us -> 11.9 us  [exchange(): return lax.all_to_all(values, ('rows', 'grp'), 0, 0, tiled=True)]
    dot_general x1, matrix products: 11 us -> 15.6 us  [on_device(): item_rhs = jnp.dot(picks, arrived, preferred_element_type=f32)]
  transfers between devices with their start and end apart: 1 -> 2, of which waited for: 1 -> 2; matrix products, arithmetic and copies ran while one was open for 0% -> 8% of each run, Pallas kernels for 0% -> 0%
where the time goes in v15:
time: 220 us; the launch traced here: 219 us
  waiting for transfers between devices  100 us (45%)
  matrix products  29.9 us (14%)
  blocking collectives  28.3 us (13%)
  other arithmetic  24.3 us (11%)
  Pallas kernels  18.6 us (8%)
  starting transfers between devices  11.9 us (5%)
  local copies, waits for them, and re-layouts  4.93 us (2%)
    all_to_all x2, waiting for transfers between devices, exchange(): return lax.all_to_all(values, ('rows', 'grp'), 0, 0, tiled=True)  100 us
    all_to_all x1, blocking collectives, exchange(): return lax.all_to_all(values, ('rows', 'grp'), 0, 0, tiled=True)  28.3 us
    convert_element_type x1, other arithmetic, on_device(): (table_ids == incoming[None, :]).astype(bf16)  16.9 us
    dot_general x1, matrix products, on_device(): item_rhs = jnp.dot(picks, arrived, preferred_element_type=f32)  15.6 us
    all_to_all x2, starting transfers between devices, exchange(): return lax.all_to_all(values, ('rows', 'grp'), 0, 0, tiled=True)  11.9 us
    pallas_call x1, Pallas kernels, answer_rows(): pl.pallas_call(answer_kernel, grid_spec=pltpu.PrefetchScalarGridSpec(num_...  10.9 us
    pallas_call x1, Pallas kernels, gather_rows(): pl.pallas_call(gather_rows_kernel, grid_spec=pltpu.PrefetchScalarGridSpec...  7.75 us
  transfers between devices with their start and end apart: 2, of which 2 were waited for; matrix products, arithmetic and copies ran while one was open for 8% of the time, Pallas kernels for 0%

profile of v15, /device:TPU:1, one launch (start us, length us, event | category | flops | bytes accessed | tf_op | source)
XLA Modules:
  0.0 219.1 jit_solution(3038875015997279591)
XLA Ops:
  0.7 0.8 fusion.73
  1.5 0.1 lt.30
  1.6 0.8 multiply_subtract_fusion.2
  2.4 0.1 reshape.314
  2.4 1.4 fusion.50
  3.8 1.4 fusion.4
  5.3 0.1 broadcast_in_dim.43
  5.4 0.3 fusion.94
  5.7 0.1 reshape.317
  5.8 0.1 reshape.316
  5.9 0.1 fusion.26
  6.0 0.1 copy.20
  6.1 1.9 fusion.2
  8.0 0.8 fusion.14
  8.8 0.1 copy.29
  8.9 0.1 reshape.315
  9.0 1.7 fusion.23
  10.7 0.1 copy.21
  10.8 0.1 pad_maximum_fusion
  10.9 28.3 %all_to_all.22 = f32[256,1,96]{2,1,0:T(1,128)S(1)} all-to-all(f32[256,1,96]{2,1,0:T(1,128)S(1)} %bitcast.96), channel_id=1, replica_groups=mesh['rows'=32,'grp'=8] {'rows','grp'}, dimensions={0} | all-to-all | bytes 196608 | tf_op jit(solution)/shard_map/all_to_all | solution.py:16
  39.2 0.1 slice_reduce_fusion
  39.3 0.7 reshape.318.index_ref
  40.0 0.1 fusion.86
  40.1 1.0 maximum_convert_fusion.source_ref
  41.2 10.9 %shard_map.50 = bf16[256,34,128]{2,1,0:T(8,128)(2,1)} custom-call(s32[8192]{0:T(1024)} %reshape.318.index_ref, f32[1986,128]{1,0:T(8,128)} %maximum_convert_fusion.source_ref), custom_call_target="tpu_custom_call" | custom-call | tf_op jit(solution)/shard_map/pallas_call | solution.py:80
  52.0 5.6 %all-to-all-start.1 = ((bf16[256,34,128]{2,1,0:T(8,128)(2,1)}), bf16[256,34,128]{2,1,0:T(8,128)(2,1)S(1)}, u32[]{:S(2)}, u32[]{:S(2)}) async-start(bf16[256,34,128]{2,1,0:T(8,128)(2,1)} %shard_map.50), calls=%async_computation.1 | async-start | bytes 5242880 | tf_op jit(solution)/shard_map/all_to_all | solution.py:16
  57.6 0.1 copy.26
  57.7 0.1 gt.16
  57.9 0.1 copy.25
  58.0 0.1 eq.102
  58.1 0.6 multiply_add_fusion.3.index_ref
  58.7 63.6 %all-to-all-done.1 = bf16[256,34,128]{2,1,0:T(8,128)(2,1)S(1)} async-done(((bf16[256,34,128]{2,1,0:T(8,128)(2,1)}), bf16[256,34,128]{2,1,0:T(8,128)(2,1)S(1)}, u32[]{:S(2)}, u32[]{:S(2)}) %all-to-all-start.1) | async-done | bytes 2228256 | tf_op jit(solution)/shard_map/all_to_all | solution.py:16
  122.3 0.1 slice.48
  122.4 0.1 copy.44
  122.6 0.1 copy.24
  122.6 0.1 add.76
  122.7 2.7 %reshape.326.source_ref = f32[8704,128]{1,0:T(8,128)} reshape(bf16[256,34,128]{2,1,0:T(8,128)(2,1)S(1)} %all-to-all-done.1) | data formatting | bytes 6684672 | tf_op jit(solution)/shard_map/convert_element_type | solution.py:173
  125.4 7.8 %shard_map.51 = bf16[4096,128]{1,0:T(8,128)(2,1)} custom-call(s32[4096]{0:T(1024)} %multiply_add_fusion.3.index_ref, f32[8704,128]{1,0:T(8,128)} %reshape.326.source_ref), custom_call_target="tpu_custom_call" | custom-call | tf_op jit(solution)/shard_map/pallas_call | solution.py:46
  133.2 1.7 fusion.67
  134.9 1.9 fusion.65
  136.8 0.0 copy-done.4
  136.8 0.1 fusion.74
  136.8 0.0 copy-done.1
  136.9 0.4 fusion.63
  137.3 0.3 multiply_reduce_fusion.3
  137.6 0.2 multiply_reduce_fusion.2
  137.8 0.1 convert_bitcast_fusion.1
  137.9 0.6 fusion.61
  138.5 0.1 fusion.75
  138.6 0.4 fusion.59
  139.0 0.3 multiply_reduce_fusion.1
  139.3 0.2 multiply_reduce_fusion
  139.5 0.1 convert_bitcast_fusion
  139.6 0.6 fusion.57
  140.2 0.1 fusion.76
  140.3 0.4 fusion.55
  140.7 0.3 fusion.34
  141.0 0.1 multiply_add_fusion
  141.1 0.0 copy-start.3
  141.1 2.6 %convolution_convert_fusion = bf16[8192,128]{1,0:T(8,128)(2,1)} fusion(s32[8192]{0:T(1024)S(1)} %eq.102, pred[8192]{0:T(1024)(128)(4,1)S(1)} %gt.16, f32[64,128]{1,0:T(8,128)S(1)} %multiply_add_fusion), kind=kOutput, calls=%fused_computation.2 | convolution fusion | flops 136323072 | bytes 2170880 | tf_op jit(solution)/shard_map/su,uk->sk/dot_general | solution.py:200
  143.7 6.4 %all-to-all-start.2 = ((bf16[256,32,128]{2,1,0:T(8,128)(2,1)}), bf16[256,32,128]{2,1,0:T(8,128)(2,1)S(1)}, u32[]{:S(2)}, u32[]{:S(2)}) async-start(bf16[256,32,128]{2,1,0:T(8,128)(2,1)} %bitcast.35), calls=%async_computation.2 | async-start | bytes 4194304 | tf_op jit(solution)/shard_map/all_to_all | solution.py:16
  150.1 16.9 %fusion = bf16[1984,8192]{1,0:T(8,128)(2,1)} fusion(s32[8192]{0:T(1024)S(1)} %copy-done.2), kind=kLoop, calls=%fused_computation.1 | loop fusion | flops 32505856 | bytes 32538624 | tf_op jit(solution)/shard_map/convert_element_type | solution.py:167
  167.0 36.5 %all-to-all-done.2 = bf16[256,32,128]{2,1,0:T(8,128)(2,1)S(1)} async-done(((bf16[256,32,128]{2,1,0:T(8,128)(2,1)}), bf16[256,32,128]{2,1,0:T(8,128)(2,1)S(1)}, u32[]{:S(2)}, u32[]{:S(2)}) %all-to-all-start.2) | async-done | bytes 2097184 | tf_op jit(solution)/shard_map/all_to_all | solution.py:16
  203.5 15.6 %fusion.95 = f32[1984,128]{1,0:T(8,128)} fusion(bf16[1984,8192]{1,0:T(8,128)(2,1)} %fusion, bf16[8192,128]{1,0:T(8,128)(2,1)S(1)} %bitcast.81), kind=kOutput, calls=%fused_computation.153 | convolution fusion | flops 4160749568 | bytes 35618816 | tf_op jit(solution)/shard_map/dot_general | solution.py:203
  (30 shorter events, 0.2 us)
Async XLA Ops:
  0.6 4.7 %copy-start = (bf16[1984,128]{1,0:T(8,128)(2,1)S(1)}, bf16[1984,128]{1,0:T(8,128)(2,1)}, u32[]{:S(2)}) copy-start(bf16[1984,128]{1,0:T(8,128)(2,1)} %param.3) | copy-start | bytes 1523716
  52.0 70.3 %all-to-all-start.1 = ((bf16[256,34,128]{2,1,0:T(8,128)(2,1)}), bf16[256,34,128]{2,1,0:T(8,128)(2,1)S(1)}, u32[]{:S(2)}, u32[]{:S(2)}) async-start(bf16[256,34,128]{2,1,0:T(8,128)(2,1)} %shard_map.50), calls=%async_computation.1 | async-start | bytes 5242880 | tf_op jit(solution)/shard_map/all_to_all | solution.py:16
  133.2 3.6 %copy-start.4 = (s32[64]{0:T(128)S(1)}, s32[64]{0:T(128)}, u32[]{:S(2)}) copy-start(s32[64]{0:T(128)} %param.5) | copy-start | bytes 772
  133.2 3.7 %copy-start.1 = (bf16[4096,128]{1,0:T(8,128)(2,1)S(1)}, bf16[4096,128]{1,0:T(8,128)(2,1)}, u32[]{:S(2)}) copy-start(bf16[4096,128]{1,0:T(8,128)(2,1)} %shard_map.51) | copy-start | bytes 3145732
  141.1 2.6 %copy-start.3 = (f32[64,128]{1,0:T(8,128)}, f32[64,128]{1,0:T(8,128)S(1)}, u32[]{:S(2)}) copy-start(f32[64,128]{1,0:T(8,128)S(1)} %multiply_add_fusion) | copy-start | bytes 98308
  143.7 6.4 %copy-start.2 = (s32[8192]{0:T(1024)S(1)}, s32[8192]{0:T(1024)}, u32[]{:S(2)}) copy-start(s32[8192]{0:T(1024)} %reshape.318.index_ref) | copy-start | bytes 98308
  143.7 59.8 %all-to-all-start.2 = ((bf16[256,32,128]{2,1,0:T(8,128)(2,1)}), bf16[256,32,128]{2,1,0:T(8,128)(2,1)S(1)}, u32[]{:S(2)}, u32[]{:S(2)}) async-start(bf16[256,32,128]{2,1,0:T(8,128)(2,1)} %bitcast.35), calls=%async_computation.2 | async-start | bytes 4194304 | tf_op jit(solution)/shard_map/all_to_all | solution.py:16

commit v16 on v12

--- a/solution.py
+++ b/solution.py
@@ -27,7 +27,7 @@
     return value
 
 
-GATHER_TILE = 16
+GATHER_TILE = 32
 
 
 def gather_rows_kernel(index_ref, source_ref, out_ref):

time: 214 us -> 214 us (level)
  no operation moved by 1% of the time
where the time goes in v16:
time: 214 us; the launch traced here: 213 us
  blocking collectives  87.9 us (41%)
  waiting for transfers between devices  63.6 us (30%)
  matrix products  24 us (11%)
  Pallas kernels  18.5 us (9%)
  other arithmetic  7.41 us (3%)
  starting transfers between devices  5.56 us (3%)
  local copies, waits for them, and re-layouts  4.93 us (2%)
    all_to_all x2, blocking collectives, exchange(): return lax.all_to_all(values, ('rows', 'grp'), 0, 0, tiled=True)  87.9 us
    all_to_all x1, waiting for transfers between devices, exchange(): return lax.all_to_all(values, ('rows', 'grp'), 0, 0, tiled=True)  63.6 us
    dot_general x1, matrix products, on_device(): jnp.einsum('st,sk->tk', picks, arrived, preferred_element_type=f32)  11 us
    pallas_call x1, Pallas kernels, answer_rows(): pl.pallas_call(answer_kernel, grid_spec=pltpu.PrefetchScalarGridSpec(num_...  10.9 us
    pallas_call x1, Pallas kernels, gather_rows(): pl.pallas_call(gather_rows_kernel, grid_spec=pltpu.PrefetchScalarGridSpec...  7.58 us
    all_to_all x1, starting transfers between devices, exchange(): return lax.all_to_all(values, ('rows', 'grp'), 0, 0, tiled=True)  5.56 us
  transfers between devices with their start and end apart: 1, of which 1 were waited for; matrix products, arithmetic and copies ran while one was open for 0% of the time, Pallas kernels for 0%

profile of v16, /device:TPU:1, one launch (start us, length us, event | category | flops | bytes accessed | tf_op | source)
XLA Modules:
  0.0 212.9 jit_solution(17915499919270138436)
XLA Ops:
  0.6 0.0 copy-start
  0.7 0.8 fusion.74
  1.5 0.1 lt.30
  1.6 0.8 multiply_subtract_fusion.2
  2.4 0.1 reshape.314
  2.4 1.4 fusion.51
  3.8 1.4 fusion.5
  5.3 0.1 broadcast_in_dim.43
  5.4 0.0 copy-done
  5.4 0.3 fusion.95
  5.7 0.1 reshape.317
  5.8 0.1 reshape.316
  5.9 0.1 fusion.27
  6.0 0.1 copy.27
  6.1 1.9 fusion.3
  8.0 0.8 fusion.15
  8.8 0.1 copy.36
  8.9 0.1 reshape.315
  9.0 1.7 fusion.24
  10.7 0.1 copy.28
  10.8 0.1 pad_maximum_fusion
  10.9 28.3 %all_to_all.22 = f32[256,1,96]{2,1,0:T(1,128)S(1)} all-to-all(f32[256,1,96]{2,1,0:T(1,128)S(1)} %bitcast.96), channel_id=1, replica_groups=mesh['rows'=32,'grp'=8] {'rows','grp'}, dimensions={0} | all-to-all | bytes 196608 | tf_op jit(solution)/shard_map/all_to_all | solution.py:16
  39.2 0.1 slice_reduce_fusion
  39.3 0.7 reshape.318.index_ref
  40.0 0.1 fusion.87
  40.1 1.0 maximum_convert_fusion.source_ref
  41.2 10.9 %shard_map.50 = bf16[256,34,128]{2,1,0:T(8,128)(2,1)} custom-call(s32[8192]{0:T(1024)} %reshape.318.index_ref, f32[1986,128]{1,0:T(8,128)} %maximum_convert_fusion.source_ref), custom_call_target="tpu_custom_call" | custom-call | tf_op jit(solution)/shard_map/pallas_call | solution.py:80
  52.0 5.6 %all-to-all-start.1 = ((bf16[256,34,128]{2,1,0:T(8,128)(2,1)}), bf16[256,34,128]{2,1,0:T(8,128)(2,1)S(1)}, u32[]{:S(2)}, u32[]{:S(2)}) async-start(bf16[256,34,128]{2,1,0:T(8,128)(2,1)} %shard_map.50), calls=%async_computation.1 | async-start | bytes 5242880 | tf_op jit(solution)/shard_map/all_to_all | solution.py:16
  57.6 0.1 copy.33
  57.7 0.1 gt.16
  57.9 0.1 copy.32
  58.0 0.1 eq.102
  58.1 0.6 multiply_add_fusion.3.index_ref
  58.7 63.6 %all-to-all-done.1 = bf16[256,34,128]{2,1,0:T(8,128)(2,1)S(1)} async-done(((bf16[256,34,128]{2,1,0:T(8,128)(2,1)}), bf16[256,34,128]{2,1,0:T(8,128)(2,1)S(1)}, u32[]{:S(2)}, u32[]{:S(2)}) %all-to-all-start.1) | async-done | bytes 2228256 | tf_op jit(solution)/shard_map/all_to_all | solution.py:16
  122.3 0.1 slice.48
  122.4 0.1 copy.51
  122.6 0.1 copy.31
  122.6 0.1 add.76
  122.7 2.7 %reshape.326.source_ref = f32[8704,128]{1,0:T(8,128)} reshape(bf16[256,34,128]{2,1,0:T(8,128)(2,1)S(1)} %all-to-all-done.1) | data formatting | bytes 6684672 | tf_op jit(solution)/shard_map/convert_element_type | solution.py:171
  125.4 7.6 %shard_map.51 = bf16[4096,128]{1,0:T(8,128)(2,1)} custom-call(s32[4096]{0:T(1024)} %multiply_add_fusion.3.index_ref, f32[8704,128]{1,0:T(8,128)} %reshape.326.source_ref), custom_call_target="tpu_custom_call" | custom-call | tf_op jit(solution)/shard_map/pallas_call | solution.py:46
  133.0 1.7 fusion.68
  134.7 1.9 fusion.66
  136.6 0.1 fusion.75
  136.7 0.0 copy-done.1
  136.7 0.4 fusion.64
  137.1 0.3 multiply_reduce_fusion.3
  137.4 0.2 multiply_reduce_fusion.2
  137.6 0.1 convert_bitcast_fusion.1
  137.7 0.6 fusion.62
  138.3 0.1 fusion.76
  138.4 0.4 fusion.60
  138.8 0.3 multiply_reduce_fusion.1
  139.1 0.2 multiply_reduce_fusion
  139.3 0.1 convert_bitcast_fusion
  139.4 0.6 fusion.58
  140.1 0.1 fusion.77
  140.1 0.4 fusion.56
  140.5 0.3 fusion.35
  140.8 0.1 multiply_add_fusion
  140.9 0.0 copy-start.3
  141.0 1.3 convolution_convert_fusion
  142.2 0.0 copy-start.2
  142.2 59.6 %all_to_all.23 = bf16[256,32,128]{2,1,0:T(8,128)(2,1)S(1)} all-to-all(bf16[256,32,128]{2,1,0:T(8,128)(2,1)S(1)} %bitcast.80), channel_id=1, replica_groups=mesh['rows'=32,'grp'=8] {'rows','grp'}, dimensions={0} | all-to-all | bytes 4194304 | tf_op jit(solution)/shard_map/all_to_all | solution.py:16
  201.9 11.0 %fusion = f32[1984,128]{1,0:T(8,128)} fusion(bf16[8192,128]{1,0:T(8,128)(2,1)S(1)} %bitcast.81, s32[8192]{0:T(1024)S(1)} %copy-done.2), kind=kOutput, calls=%fused_computation.1 | convolution fusion | flops 4177002496 | bytes 3145728 | tf_op jit(solution)/shard_map/st,sk->tk/dot_general | solution.py:203
  (28 shorter events, 0.2 us)
Async XLA Ops:
  0.6 4.7 %copy-start = (bf16[1984,128]{1,0:T(8,128)(2,1)S(1)}, bf16[1984,128]{1,0:T(8,128)(2,1)}, u32[]{:S(2)}) copy-start(bf16[1984,128]{1,0:T(8,128)(2,1)} %param.3) | copy-start | bytes 1523716
  52.0 70.3 %all-to-all-start.1 = ((bf16[256,34,128]{2,1,0:T(8,128)(2,1)}), bf16[256,34,128]{2,1,0:T(8,128)(2,1)S(1)}, u32[]{:S(2)}, u32[]{:S(2)}) async-start(bf16[256,34,128]{2,1,0:T(8,128)(2,1)} %shard_map.50), calls=%async_computation.1 | async-start | bytes 5242880 | tf_op jit(solution)/shard_map/all_to_all | solution.py:16
  133.0 3.6 %copy-start.4 = (s32[64]{0:T(128)S(1)}, s32[64]{0:T(128)}, u32[]{:S(2)}) copy-start(s32[64]{0:T(128)} %param.5) | copy-start | bytes 772
  133.0 3.7 %copy-start.1 = (bf16[4096,128]{1,0:T(8,128)(2,1)S(1)}, bf16[4096,128]{1,0:T(8,128)(2,1)}, u32[]{:S(2)}) copy-start(bf16[4096,128]{1,0:T(8,128)(2,1)} %shard_map.51) | copy-start | bytes 3145732
  140.9 60.9 %copy-start.3 = (f32[64,128]{1,0:T(8,128)}, f32[64,128]{1,0:T(8,128)S(1)}, u32[]{:S(2)}) copy-start(f32[64,128]{1,0:T(8,128)S(1)} %multiply_add_fusion) | copy-start | bytes 98308
  142.2 59.6 %copy-start.2 = (s32[8192]{0:T(1024)S(1)}, s32[8192]{0:T(1024)}, u32[]{:S(2)}) copy-start(s32[8192]{0:T(1024)} %reshape.318.index_ref) | copy-start | bytes 98308

commit v17 on v13

--- a/solution.py
+++ b/solution.py
@@ -89,13 +89,11 @@
     )(index, wide)
 
 
-def fetch_kernel(owner_ref, rank_ref, source_ref, out_ref, wide_ref):
-    wide_ref[...] = source_ref[...].astype(jnp.float32)
-
+def fetch_kernel(owner_ref, rank_ref, source_ref, out_ref):
     def body(tile, carry):
         first = pl.multiple_of(tile * GATHER_TILE, GATHER_TILE)
         rows = [
-            wide_ref[owner_ref[first + r], pl.ds(rank_ref[first + r], 1), :]
+            source_ref[owner_ref[first + r], pl.ds(rank_ref[first + r], 1), :]
             for r in range(GATHER_TILE)
         ]
         out_ref[pl.ds(first, GATHER_TILE), :] = jnp.concatenate(rows, axis=0).astype(out_ref.dtype)
@@ -104,7 +102,7 @@
     lax.fori_loop(0, out_ref.shape[0] // GATHER_TILE, body, 0, unroll=8)
 
 
-def fetch_rows(source, owner, rank):
+def fetch_rows(source, owner, rank, dtype):
     count = owner.shape[0]
     return pl.pallas_call(
         fetch_kernel,
@@ -113,9 +111,8 @@
             grid=(1,),
             in_specs=[pl.BlockSpec(source.shape, lambda i, owner_ref, rank_ref: (0, 0, 0))],
             out_specs=pl.BlockSpec((count, source.shape[2]), lambda i, owner_ref, rank_ref: (0, 0)),
-            scratch_shapes=[pltpu.VMEM(source.shape, jnp.float32)],
         ),
-        out_shape=jax.ShapeDtypeStruct((count, source.shape[2]), source.dtype),
+        out_shape=jax.ShapeDtypeStruct((count, source.shape[2]), dtype),
     )(owner, rank, source)
 
 
@@ -196,7 +193,7 @@
     parts = replies[:, capacity:].reshape(devices, extra_rows * embed_width)[:, : 3 * gram_width]
     parts = parts.astype(f32).reshape(devices, 3, gram_width)
     gramian = ((parts[:, 0] + parts[:, 1]) + parts[:, 2]).reshape(embed_width, embed_width)
-    fetched = fetch_rows(replies, owners.reshape(lookups), ranks).reshape(
+    fetched = fetch_rows(replies.astype(f32), owners.reshape(lookups), ranks, bf16).reshape(
         user_count, history_length, embed_width
     )
     weights = live.astype(f32)

time: 216 us -> 217 us (level)
  other arithmetic: 6.81 us -> 9.46 us
    convert_element_type x0 -> x1, other arithmetic: none -> 2.65 us  [on_device(): replies.astype(f32)]
where the time goes in v17:
time: 217 us
  blocking collectives  87.9 us (41%)
  waiting for transfers between devices  64.2 us (30%)
  matrix products  24 us (11%)
  Pallas kernels  22.4 us (10%)
  other arithmetic  9.46 us (4%)
  starting transfers between devices  5.56 us (3%)
  local copies, waits for them, and re-layouts  2.24 us (1%)
    all_to_all x2, blocking collectives, exchange(): return lax.all_to_all(values, ('rows', 'grp'), 0, 0, tiled=True)  87.9 us
    all_to_all x1, waiting for transfers between devices, exchange(): return lax.all_to_all(values, ('rows', 'grp'), 0, 0, tiled=True)  64.2 us
    pallas_call x1, Pallas kernels, fetch_rows(): pl.pallas_call(fetch_kernel, grid_spec=pltpu.PrefetchScalarGridSpec(num_s...  11.5 us
    dot_general x1, matrix products, on_device(): jnp.einsum('st,sk->tk', picks, arrived, preferred_element_type=f32)  11 us
    pallas_call x1, Pallas kernels, answer_rows(): pl.pallas_call(answer_kernel, grid_spec=pltpu.PrefetchScalarGridSpec(num_...  10.9 us
    all_to_all x1, starting transfers between devices, exchange(): return lax.all_to_all(values, ('rows', 'grp'), 0, 0, tiled=True)  5.56 us
  transfers between devices with their start and end apart: 1, of which 1 were waited for; matrix products, arithmetic and copies ran while one was open for 0% of the time, Pallas kernels for 0%

profile of v17, /device:TPU:1, one launch (start us, length us, event | category | flops | bytes accessed | tf_op | source)
XLA Modules:
  0.0 216.8 jit_solution(5199387970204569099)
XLA Ops:
  0.6 0.0 copy-start
  0.7 0.8 fusion.74
  1.5 0.1 lt.30
  1.6 0.8 multiply_subtract_fusion.2
  2.4 0.1 reshape.311.owner_ref
  2.4 1.4 fusion.51
  3.9 1.4 fusion.5
  5.3 0.1 broadcast_in_dim.43
  5.4 0.0 copy-done
  5.4 0.3 fusion.95
  5.7 0.1 reshape.314
  5.8 0.1 reshape.313
  5.9 0.1 fusion.27
  6.0 0.1 copy.27
  6.1 1.9 fusion.3
  8.0 0.8 fusion.15
  8.8 0.1 copy.36
  8.9 0.1 reshape.312.rank_ref
  9.0 1.7 fusion.24
  10.7 0.1 copy.28
  10.8 0.1 pad_maximum_fusion
  10.9 28.3 %all_to_all.22 = f32[256,1,96]{2,1,0:T(1,128)S(1)} all-to-all(f32[256,1,96]{2,1,0:T(1,128)S(1)} %bitcast.96), channel_id=1, replica_groups=mesh['rows'=32,'grp'=8] {'rows','grp'}, dimensions={0} | all-to-all | bytes 196608 | tf_op jit(solution)/shard_map/all_to_all | solution.py:16
  39.2 0.1 slice_reduce_fusion
  39.3 0.7 reshape.315.index_ref
  40.1 0.1 fusion.87
  40.1 1.0 maximum_convert_fusion.source_ref
  41.2 10.9 %shard_map.50 = bf16[256,34,128]{2,1,0:T(8,128)(2,1)} custom-call(s32[8192]{0:T(1024)} %reshape.315.index_ref, f32[1986,128]{1,0:T(8,128)} %maximum_convert_fusion.source_ref), custom_call_target="tpu_custom_call" | custom-call | tf_op jit(solution)/shard_map/pallas_call | solution.py:80
  52.1 5.6 %all-to-all-start.1 = ((bf16[256,34,128]{2,1,0:T(8,128)(2,1)}), bf16[256,34,128]{2,1,0:T(8,128)(2,1)S(1)}, u32[]{:S(2)}, u32[]{:S(2)}) async-start(bf16[256,34,128]{2,1,0:T(8,128)(2,1)} %shard_map.50), calls=%async_computation.1 | async-start | bytes 5242880 | tf_op jit(solution)/shard_map/all_to_all | solution.py:16
  57.6 0.1 copy.33
  57.8 0.1 gt.16
  57.9 0.1 copy.32
  58.0 0.1 eq.102
  58.1 64.2 %all-to-all-done.1 = bf16[256,34,128]{2,1,0:T(8,128)(2,1)S(1)} async-done(((bf16[256,34,128]{2,1,0:T(8,128)(2,1)}), bf16[256,34,128]{2,1,0:T(8,128)(2,1)S(1)}, u32[]{:S(2)}, u32[]{:S(2)}) %all-to-all-start.1) | async-done | bytes 2228256 | tf_op jit(solution)/shard_map/all_to_all | solution.py:16
  122.3 0.1 slice.48
  122.4 0.1 copy.51
  122.6 0.1 copy.31
  122.7 0.1 add.72
  122.8 2.7 %convert_element_type.108.source_ref = f32[256,34,128]{2,1,0:T(8,128)} convert(bf16[256,34,128]{2,1,0:T(8,128)(2,1)S(1)} %all-to-all-done.1) | non-fusion elementwise | flops 1114112 | bytes 6684672 | tf_op jit(solution)/shard_map/convert_element_type | solution.py:196
  125.4 11.5 %shard_map.51 = bf16[4096,128]{1,0:T(8,128)(2,1)} custom-call(s32[4096]{0:T(1024)} %copy-done.4, s32[4096]{0:T(1024)} %copy-done.5, f32[256,34,128]{2,1,0:T(8,128)} %convert_element_type.108.source_ref), custom_call_target="tpu_custom_call" | custom-call | tf_op jit(solution)/shard_map/pallas_call | solution.py:107
  136.9 1.7 fusion.68
  138.6 1.9 fusion.66
  140.5 0.1 fusion.75
  140.6 0.0 copy-done.1
  140.6 0.4 fusion.64
  141.0 0.3 multiply_reduce_fusion.3
  141.3 0.2 multiply_reduce_fusion.2
  141.5 0.1 convert_bitcast_fusion.1
  141.6 0.6 fusion.62
  142.2 0.1 fusion.76
  142.3 0.4 fusion.60
  142.7 0.3 multiply_reduce_fusion.1
  143.0 0.2 multiply_reduce_fusion
  143.2 0.1 convert_bitcast_fusion
  143.3 0.6 fusion.58
  144.0 0.1 fusion.77
  144.0 0.4 fusion.56
  144.4 0.3 fusion.35
  144.7 0.1 multiply_add_fusion
  144.8 0.0 copy-start.3
  144.9 1.3 convolution_convert_fusion
  146.1 0.0 copy-start.2
  146.2 59.6 %all_to_all.23 = bf16[256,32,128]{2,1,0:T(8,128)(2,1)S(1)} all-to-all(bf16[256,32,128]{2,1,0:T(8,128)(2,1)S(1)} %bitcast.80), channel_id=1, replica_groups=mesh['rows'=32,'grp'=8] {'rows','grp'}, dimensions={0} | all-to-all | bytes 4194304 | tf_op jit(solution)/shard_map/all_to_all | solution.py:16
  205.8 0.0 copy-done.3
  205.8 11.0 %fusion = f32[1984,128]{1,0:T(8,128)} fusion(bf16[8192,128]{1,0:T(8,128)(2,1)S(1)} %bitcast.81, s32[8192]{0:T(1024)S(1)} %copy-done.2), kind=kOutput, calls=%fused_computation.1 | convolution fusion | flops 4177002496 | bytes 3145728 | tf_op jit(solution)/shard_map/st,sk->tk/dot_general | solution.py:228
  (31 shorter events, 0.2 us)
Async XLA Ops:
  0.6 4.7 %copy-start = (bf16[1984,128]{1,0:T(8,128)(2,1)S(1)}, bf16[1984,128]{1,0:T(8,128)(2,1)}, u32[]{:S(2)}) copy-start(bf16[1984,128]{1,0:T(8,128)(2,1)} %param.3) | copy-start | bytes 1523716
  2.4 6.6 %copy-start.4 = (s32[4096]{0:T(1024)}, s32[4096]{0:T(1024)S(1)}, u32[]{:S(2)}) copy-start(s32[4096]{0:T(1024)S(1)} %reshape.311.owner_ref) | copy-start | bytes 49156
  9.0 1.7 copy-start.5
  52.1 70.3 %all-to-all-start.1 = ((bf16[256,34,128]{2,1,0:T(8,128)(2,1)}), bf16[256,34,128]{2,1,0:T(8,128)(2,1)S(1)}, u32[]{:S(2)}, u32[]{:S(2)}) async-start(bf16[256,34,128]{2,1,0:T(8,128)(2,1)} %shard_map.50), calls=%async_computation.1 | async-start | bytes 5242880 | tf_op jit(solution)/shard_map/all_to_all | solution.py:16
  136.9 3.6 %copy-start.6 = (s32[64]{0:T(128)S(1)}, s32[64]{0:T(128)}, u32[]{:S(2)}) copy-start(s32[64]{0:T(128)} %param.5) | copy-start | bytes 772
  136.9 3.7 %copy-start.1 = (bf16[4096,128]{1,0:T(8,128)(2,1)S(1)}, bf16[4096,128]{1,0:T(8,128)(2,1)}, u32[]{:S(2)}) copy-start(bf16[4096,128]{1,0:T(8,128)(2,1)} %shard_map.51) | copy-start | bytes 3145732
  144.8 60.9 %copy-start.3 = (f32[64,128]{1,0:T(8,128)}, f32[64,128]{1,0:T(8,128)S(1)}, u32[]{:S(2)}) copy-start(f32[64,128]{1,0:T(8,128)S(1)} %multiply_add_fusion) | copy-start | bytes 98308
  146.1 59.6 %copy-start.2 = (s32[8192]{0:T(1024)S(1)}, s32[8192]{0:T(1024)}, u32[]{:S(2)}) copy-start(s32[8192]{0:T(1024)} %reshape.315.index_ref) | copy-start | bytes 98308

commit v18 on v12

--- a/solution.py
+++ b/solution.py
@@ -72,7 +72,7 @@
         out_ref[chunk, pl.ds(capacity, depth - capacity), :] = extra
         return carry
 
-    lax.fori_loop(0, chunks, body, 0, unroll=4)
+    lax.fori_loop(0, chunks, body, 0, unroll=8)
 
 
 def answer_rows(wide, index, chunks, depth, dtype):

time: 214 us -> 213 us (level)
  no operation moved by 1% of the time
where the time goes in v18:
time: 213 us
  blocking collectives  87.9 us (41%)
  waiting for transfers between devices  63.6 us (30%)
  matrix products  24 us (11%)
  Pallas kernels  18.4 us (9%)
  other arithmetic  7.41 us (3%)
  starting transfers between devices  5.56 us (3%)
  local copies, waits for them, and re-layouts  4.93 us (2%)
    all_to_all x2, blocking collectives, exchange(): return lax.all_to_all(values, ('rows', 'grp'), 0, 0, tiled=True)  87.9 us
    all_to_all x1, waiting for transfers between devices, exchange(): return lax.all_to_all(values, ('rows', 'grp'), 0, 0, tiled=True)  63.6 us
    dot_general x1, matrix products, on_device(): jnp.einsum('st,sk->tk', picks, arrived, preferred_element_type=f32)  11 us
    pallas_call x1, Pallas kernels, answer_rows(): pl.pallas_call(answer_kernel, grid_spec=pltpu.PrefetchScalarGridSpec(num_...  10.6 us
    pallas_call x1, Pallas kernels, gather_rows(): pl.pallas_call(gather_rows_kernel, grid_spec=pltpu.PrefetchScalarGridSpec...  7.75 us
    all_to_all x1, starting transfers between devices, exchange(): return lax.all_to_all(values, ('rows', 'grp'), 0, 0, tiled=True)  5.56 us
  transfers between devices with their start and end apart: 1, of which 1 were waited for; matrix products, arithmetic and copies ran while one was open for 0% of the time, Pallas kernels for 0%

profile of v18, /device:TPU:1, one launch (start us, length us, event | category | flops | bytes accessed | tf_op | source)
XLA Modules:
  0.0 212.8 jit_solution(13470039940563750832)
XLA Ops:
  0.6 0.0 copy-start
  0.7 0.8 fusion.74
  1.5 0.1 lt.30
  1.6 0.8 multiply_subtract_fusion.2
  2.4 0.1 reshape.314
  2.4 1.4 fusion.51
  3.8 1.4 fusion.5
  5.3 0.1 broadcast_in_dim.43
  5.4 0.0 copy-done
  5.4 0.3 fusion.95
  5.7 0.1 reshape.317
  5.8 0.1 reshape.316
  5.9 0.1 fusion.27
  6.0 0.1 copy.27
  6.1 1.9 fusion.3
  8.0 0.8 fusion.15
  8.8 0.1 copy.36
  8.9 0.1 reshape.315
  9.0 1.7 fusion.24
  10.7 0.1 copy.28
  10.8 0.1 pad_maximum_fusion
  10.9 28.3 %all_to_all.22 = f32[256,1,96]{2,1,0:T(1,128)S(1)} all-to-all(f32[256,1,96]{2,1,0:T(1,128)S(1)} %bitcast.96), channel_id=1, replica_groups=mesh['rows'=32,'grp'=8] {'rows','grp'}, dimensions={0} | all-to-all | bytes 196608 | tf_op jit(solution)/shard_map/all_to_all | solution.py:16
  39.2 0.1 slice_reduce_fusion
  39.3 0.7 reshape.318.index_ref
  40.0 0.1 fusion.87
  40.1 1.0 maximum_convert_fusion.source_ref
  41.2 10.6 %shard_map.50 = bf16[256,34,128]{2,1,0:T(8,128)(2,1)} custom-call(s32[8192]{0:T(1024)} %reshape.318.index_ref, f32[1986,128]{1,0:T(8,128)} %maximum_convert_fusion.source_ref), custom_call_target="tpu_custom_call" | custom-call | tf_op jit(solution)/shard_map/pallas_call | solution.py:80
  51.8 5.6 %all-to-all-start.1 = ((bf16[256,34,128]{2,1,0:T(8,128)(2,1)}), bf16[256,34,128]{2,1,0:T(8,128)(2,1)S(1)}, u32[]{:S(2)}, u32[]{:S(2)}) async-start(bf16[256,34,128]{2,1,0:T(8,128)(2,1)} %shard_map.50), calls=%async_computation.1 | async-start | bytes 5242880 | tf_op jit(solution)/shard_map/all_to_all | solution.py:16
  57.4 0.1 copy.33
  57.5 0.1 gt.16
  57.6 0.1 copy.32
  57.7 0.1 eq.102
  57.8 0.6 multiply_add_fusion.3.index_ref
  58.4 63.6 %all-to-all-done.1 = bf16[256,34,128]{2,1,0:T(8,128)(2,1)S(1)} async-done(((bf16[256,34,128]{2,1,0:T(8,128)(2,1)}), bf16[256,34,128]{2,1,0:T(8,128)(2,1)S(1)}, u32[]{:S(2)}, u32[]{:S(2)}) %all-to-all-start.1) | async-done | bytes 2228256 | tf_op jit(solution)/shard_map/all_to_all | solution.py:16
  122.1 0.1 slice.48
  122.1 0.1 copy.51
  122.3 0.1 copy.31
  122.4 0.1 add.76
  122.5 2.7 %reshape.326.source_ref = f32[8704,128]{1,0:T(8,128)} reshape(bf16[256,34,128]{2,1,0:T(8,128)(2,1)S(1)} %all-to-all-done.1) | data formatting | bytes 6684672 | tf_op jit(solution)/shard_map/convert_element_type | solution.py:171
  125.2 7.8 %shard_map.51 = bf16[4096,128]{1,0:T(8,128)(2,1)} custom-call(s32[4096]{0:T(1024)} %multiply_add_fusion.3.index_ref, f32[8704,128]{1,0:T(8,128)} %reshape.326.source_ref), custom_call_target="tpu_custom_call" | custom-call | tf_op jit(solution)/shard_map/pallas_call | solution.py:46
  133.0 1.7 fusion.68
  134.7 1.9 fusion.66
  136.5 0.1 fusion.75
  136.6 0.0 copy-done.1
  136.6 0.4 fusion.64
  137.0 0.3 multiply_reduce_fusion.3
  137.3 0.2 multiply_reduce_fusion.2
  137.5 0.1 convert_bitcast_fusion.1
  137.6 0.6 fusion.62
  138.3 0.1 fusion.76
  138.3 0.4 fusion.60
  138.7 0.3 multiply_reduce_fusion.1
  139.0 0.2 multiply_reduce_fusion
  139.2 0.1 convert_bitcast_fusion
  139.3 0.6 fusion.58
  140.0 0.1 fusion.77
  140.1 0.4 fusion.56
  140.5 0.3 fusion.35
  140.8 0.1 multiply_add_fusion
  140.9 0.0 copy-start.3
  140.9 1.3 convolution_convert_fusion
  142.2 0.0 copy-start.2
  142.2 59.6 %all_to_all.23 = bf16[256,32,128]{2,1,0:T(8,128)(2,1)S(1)} all-to-all(bf16[256,32,128]{2,1,0:T(8,128)(2,1)S(1)} %bitcast.80), channel_id=1, replica_groups=mesh['rows'=32,'grp'=8] {'rows','grp'}, dimensions={0} | all-to-all | bytes 4194304 | tf_op jit(solution)/shard_map/all_to_all | solution.py:16
  201.8 11.0 %fusion = f32[1984,128]{1,0:T(8,128)} fusion(bf16[8192,128]{1,0:T(8,128)(2,1)S(1)} %bitcast.81, s32[8192]{0:T(1024)S(1)} %copy-done.2), kind=kOutput, calls=%fused_computation.1 | convolution fusion | flops 4177002496 | bytes 3145728 | tf_op jit(solution)/shard_map/st,sk->tk/dot_general | solution.py:203
  (28 shorter events, 0.2 us)
Async XLA Ops:
  0.6 4.7 %copy-start = (bf16[1984,128]{1,0:T(8,128)(2,1)S(1)}, bf16[1984,128]{1,0:T(8,128)(2,1)}, u32[]{:S(2)}) copy-start(bf16[1984,128]{1,0:T(8,128)(2,1)} %param.3) | copy-start | bytes 1523716
  51.8 70.3 %all-to-all-start.1 = ((bf16[256,34,128]{2,1,0:T(8,128)(2,1)}), bf16[256,34,128]{2,1,0:T(8,128)(2,1)S(1)}, u32[]{:S(2)}, u32[]{:S(2)}) async-start(bf16[256,34,128]{2,1,0:T(8,128)(2,1)} %shard_map.50), calls=%async_computation.1 | async-start | bytes 5242880 | tf_op jit(solution)/shard_map/all_to_all | solution.py:16
  133.0 3.6 %copy-start.4 = (s32[64]{0:T(128)S(1)}, s32[64]{0:T(128)}, u32[]{:S(2)}) copy-start(s32[64]{0:T(128)} %param.5) | copy-start | bytes 772
  133.0 3.7 %copy-start.1 = (bf16[4096,128]{1,0:T(8,128)(2,1)S(1)}, bf16[4096,128]{1,0:T(8,128)(2,1)}, u32[]{:S(2)}) copy-start(bf16[4096,128]{1,0:T(8,128)(2,1)} %shard_map.51) | copy-start | bytes 3145732
  140.9 60.9 %copy-start.3 = (f32[64,128]{1,0:T(8,128)}, f32[64,128]{1,0:T(8,128)S(1)}, u32[]{:S(2)}) copy-start(f32[64,128]{1,0:T(8,128)S(1)} %multiply_add_fusion) | copy-start | bytes 98308
  142.2 59.6 %copy-start.2 = (s32[8192]{0:T(1024)S(1)}, s32[8192]{0:T(1024)}, u32[]{:S(2)}) copy-start(s32[8192]{0:T(1024)} %reshape.318.index_ref) | copy-start | bytes 98308
